TPU v7x, 256 devices: a whole 4x4x8 slice. The times are simulated.
256 devices in a mesh: section: 2 (over core), tok: 32 (over z, y), rep: 4 (over x).
Axes of the slice: x: 4, y: 4, z: 8, core: 2. Of those that a mesh axis runs over, the one named last changes fastest.
Arguments:
- inputs: bfloat16 [2, 4096, 1024], P(None, 'tok')
- segment_ids: int32 [2, 4096], replicated, may hold values from 0 to 7, as said below
- picks: int32 [2, 4096, 2], P(None, 'tok'), may hold values from 0 to 15, all different within a row; in each aligned block of 128 rows (0 to 127, 128 to 255, ..., all dimensions but the last counted through in order) at most 20 rows name the same one
- page_table: int32 [2, 32], replicated, may hold values from 0 to 31, each once within a row
- norm_gains: float32 [2, 2, 1024], P('section'), may hold values from 0.1 to 1.9
- attn_qkv: bfloat16 [2, 1024, 3, 1024], P('section', None, None, 'rep')
- attn_out: bfloat16 [2, 1024, 1024], P('section', 'rep'), may hold values from -0.1875 to 0.1875
- router: bfloat16 [2, 1024, 16], P('section')
- expert_in: bfloat16 [2, 32, 1024, 2, 1408], P('section', 'tok', None, None, 'rep'), may hold values from -0.1875 to 0.1875
- expert_out: bfloat16 [2, 32, 1408, 1024], P('section', 'tok', 'rep')
Outputs:
- layer_out: bfloat16 [2, 2, 4096, 1024], P('section', None, 'tok')
- kv_pages: bfloat16 [2, 2, 32, 128, 2, 1024], P('section', None, 'tok', None, None, 'rep')
Inputs may be any that keep to these rules, and one draw needn't show every extreme that they name: `picks`: within the tokens of one index of tok in one micro-batch, at most 20 tokens pick one expert, and some expert is picked by exactly 20. `segment_ids`: ids never fall along a micro-batch; every prompt has at least one token, a prompt spans at most 2048 tokens and one spans exactly 2048. `page_table`: each row is a permutation.
All inputs are finite; a program needn't handle non-finite values.
Results may differ from a plain program's by a relative error of at most 0.034.
Values may be sent and summed in bfloat16 or wider, within the bound.
No kernel may reach another device: no remote copies, remote signals or barrier semaphores. Data moves between devices by JAX's collectives and lax.ppermute only.
A program may use at most 128 MiB of HBM per device.

v0:
```python
import jax
import jax.numpy as jnp
from jax import lax
from jax.sharding import PartitionSpec as P

HEAD_DIM = 64
TOP = 2
PAGE = 128
CAP = 20


NEG_FILL = -1e30


def shifted(value, axis, steps):
    count = lax.axis_size(axis)
    first, last = (max(0, -steps), min(count, count - steps))
    return lax.ppermute(value, axis, [(source, source + steps) for source in range(first, last)])


def rms_scale(values, gains):
    return values * lax.rsqrt(jnp.mean(values * values, axis=-1, keepdims=True) + 1e-06) * gains


def attend(carry, queries, keys_vals, seg_query, pos_query, seg_key, pos_key):
    run_max, run_sum, run_acc = carry
    heads_here = run_acc.shape[0]
    head_size = run_acc.shape[2]
    rows_key = keys_vals.shape[0]
    key_part = keys_vals[:, 0].reshape(rows_key, heads_here, head_size)
    val_part = keys_vals[:, 1].reshape(rows_key, heads_here, head_size).astype(jnp.float32)
    scores = jnp.einsum(
        "thd,nhd->htn", queries, key_part, preferred_element_type=jnp.float32
    ) * head_size ** (-0.5)
    visible = (seg_query[:, None] == seg_key[None, :]) & (pos_query[:, None] >= pos_key[None, :])
    masked = jnp.where(visible[None], scores, NEG_FILL)
    new_max = jnp.maximum(run_max, jnp.max(masked, axis=-1))
    weights = jnp.where(visible[None], jnp.exp(masked - new_max[..., None]), 0.0)
    decay = jnp.exp(run_max - new_max)
    run_sum = run_sum * decay + jnp.sum(weights, axis=-1)
    run_acc = run_acc * decay[..., None] + jnp.einsum(
        "htn,nhd->htd", weights, val_part, precision=lax.Precision.HIGHEST
    )
    return (new_max, run_sum, run_acc)


def place_pages(pages, keys_vals, table_row, tok_index):
    rows_here = keys_vals.shape[0]
    blocks_dev = pages.shape[0]
    page_rows = pages.shape[1]
    block_ids = jnp.arange(table_row.shape[0], dtype=jnp.int32)
    wanted = tok_index * blocks_dev + 0
    source = jnp.sum(jnp.where(table_row == wanted, block_ids, 0))
    offset = source * page_rows
    inside = (offset >= 0) & (offset + page_rows <= rows_here)
    block = lax.dynamic_slice_in_dim(
        keys_vals, jnp.clip(offset, 0, rows_here - page_rows), page_rows, 0
    )
    updated = [jnp.where(inside, block, pages[0])]
    return jnp.stack(updated)


def per_device(
    inputs,
    segment_ids,
    picks,
    page_table,
    norm_gains,
    attn_qkv,
    attn_out,
    router,
    expert_in,
    expert_out,
):
    section_index = lax.axis_index("section")
    tok_index = lax.axis_index("tok")
    tok_count = lax.axis_size("tok")
    micro_count = inputs.shape[0]
    tok_rows = inputs.shape[1]
    width = inputs.shape[2]
    col_width = attn_qkv.shape[3]
    head_count = col_width // HEAD_DIM
    experts_all = router.shape[2]
    local_pieces = expert_in.shape[1]
    split_count = local_pieces * tok_count // experts_all
    blocks_dev = tok_rows // PAGE
    row_ids = jnp.arange(tok_rows, dtype=jnp.int32)
    pos_query = tok_index * tok_rows + row_ids
    gains = norm_gains[0]
    w_qkv = attn_qkv[0].reshape(width, 3 * col_width)
    w_out = attn_out[0]
    w_router = router[0]
    w_in = expert_in[0]
    w_down = expert_out[0]
    outputs = [jnp.zeros((tok_rows, width), jnp.bfloat16) for slot_micro in range(micro_count)]
    page_out = [
        jnp.zeros((blocks_dev, PAGE, 2, col_width), jnp.bfloat16)
        for slot_micro in range(micro_count)
    ]
    received = jnp.zeros((tok_rows, width), jnp.bfloat16)
    for round_index in range(micro_count + 1):
        own_micro = round_index - section_index
        micro_index = jnp.clip(own_micro, 0, micro_count - 1)
        fresh = inputs[min(round_index, micro_count - 1)]
        layer_in = jnp.where(section_index == 0, fresh, received)
        seg_all = lax.dynamic_index_in_dim(segment_ids, micro_index, 0, keepdims=False)
        seg_query = lax.dynamic_slice_in_dim(seg_all, tok_index * tok_rows, tok_rows)
        table_row = lax.dynamic_index_in_dim(page_table, micro_index, 0, keepdims=False)
        pick_rows = lax.dynamic_index_in_dim(picks, micro_index, 0, keepdims=False)
        resid = layer_in.astype(jnp.float32)
        normed = rms_scale(resid, gains[0]).astype(jnp.bfloat16)
        projected = jnp.dot(normed, w_qkv, preferred_element_type=jnp.float32).astype(jnp.bfloat16)
        projected = projected.reshape(tok_rows, 3, col_width)
        queries = projected[:, 0].reshape(tok_rows, head_count, HEAD_DIM)
        keys_vals = projected[:, 1:]
        soft_init = (
            jnp.full((head_count, tok_rows), NEG_FILL, jnp.float32),
            jnp.zeros((head_count, tok_rows), jnp.float32),
            jnp.zeros((head_count, tok_rows, HEAD_DIM), jnp.float32),
        )
        empty_pages = jnp.zeros((blocks_dev, PAGE, 2, col_width), jnp.bfloat16)
        piece = lax.all_gather(keys_vals, "tok", axis=0, tiled=True)
        rows_key = piece.shape[0]
        step_rows = 1024
        while rows_key % step_rows != 0:
            step_rows = step_rows // 2
        turns = rows_key // step_rows

        def key_block(index, soft_now):
            start = index * step_rows
            block = lax.dynamic_slice_in_dim(piece, start, step_rows, 0)
            seg_key = lax.dynamic_slice_in_dim(seg_all, start, step_rows)
            pos_key = start + jnp.arange(step_rows, dtype=jnp.int32)
            return attend(soft_now, queries, block, seg_query, pos_query, seg_key, pos_key)

        soft_next = lax.fori_loop(0, turns, key_block, soft_init)
        pages = place_pages(empty_pages, piece, table_row, tok_index)
        run_max, run_sum, run_acc = soft_next
        context = (
            (run_acc / run_sum[..., None])
            .transpose(1, 0, 2)
            .reshape(tok_rows, col_width)
            .astype(jnp.bfloat16)
        )
        attn_part = jnp.dot(context, w_out, preferred_element_type=jnp.float32)
        mid = resid + lax.psum(attn_part, "rep")
        normed_mid = rms_scale(mid, gains[1]).astype(jnp.bfloat16)
        logits = jnp.dot(normed_mid, w_router, preferred_element_type=jnp.float32)
        expert_ids = jnp.arange(experts_all, dtype=jnp.int32)
        chosen = (pick_rows[:, :, None] == expert_ids[None, None, :]).astype(jnp.int32)
        picked_logit = jnp.sum(chosen.astype(jnp.float32) * logits[:, None, :], axis=-1)
        top_logit = jnp.max(picked_logit, axis=-1, keepdims=True)
        raised = jnp.exp(picked_logit - top_logit)
        gate_vals = raised / jnp.sum(raised, axis=-1, keepdims=True)
        ordered = chosen.transpose(1, 0, 2).reshape(TOP * tok_rows, experts_all)
        slot_of = jnp.sum((jnp.cumsum(ordered, axis=0) - 1) * ordered, axis=-1)
        flat_slot = pick_rows.T.reshape(TOP * tok_rows) * CAP + slot_of
        slot_ids = jnp.arange(experts_all * CAP, dtype=jnp.int32)
        hits = (flat_slot[:, None] == slot_ids[None, :]).astype(jnp.int32)
        hits = jnp.sum(hits.reshape(TOP, tok_rows, experts_all * CAP), axis=0).astype(jnp.bfloat16)
        dispatch = lax.dot_general(
            hits, normed_mid, (((0,), (0,)), ((), ())), preferred_element_type=jnp.float32
        ).astype(jnp.bfloat16)
        copies = jnp.broadcast_to(
            dispatch.reshape(experts_all, 1, CAP, width), (experts_all, split_count, CAP, width)
        )
        copies = copies.reshape(tok_count, local_pieces, CAP, width)
        act = jnp.einsum(
            "secd,edgf->secgf",
            lax.all_to_all(copies, "tok", split_axis=0, concat_axis=0, tiled=True),
            w_in,
            preferred_element_type=jnp.float32,
        )
        hidden = (jax.nn.gelu(act[..., 0, :]) * act[..., 1, :]).astype(jnp.bfloat16)
        returned = lax.all_to_all(
            jnp.einsum("secf,efd->secd", hidden, w_down, preferred_element_type=jnp.float32).astype(
                jnp.bfloat16
            ),
            "tok",
            split_axis=0,
            concat_axis=0,
            tiled=True,
        )
        summed = jnp.sum(
            returned.reshape(experts_all, split_count, CAP, width).astype(jnp.float32), axis=1
        )
        summed = summed.reshape(experts_all * CAP, width)
        gathered = jnp.take(summed, flat_slot, axis=0).reshape(TOP, tok_rows, width)
        expert_local = jnp.sum(gate_vals.T[:, :, None] * gathered, axis=0)
        expert_total = lax.psum(expert_local, "rep")
        layer_result = (mid + expert_total).astype(jnp.bfloat16)
        for slot_micro in range(micro_count):
            if slot_micro == round_index or slot_micro == round_index - 1:
                taken = own_micro == slot_micro
                outputs[slot_micro] = jnp.where(taken, layer_result, outputs[slot_micro])
                page_out[slot_micro] = jnp.where(taken, pages, page_out[slot_micro])
        if round_index < micro_count:
            received = shifted(layer_result, "section", 1)
    return (jnp.stack(outputs)[None], jnp.stack(page_out)[None])


def solution(mesh):
    return jax.shard_map(
        per_device,
        mesh=mesh,
        in_specs=(
            P(None, "tok", None),
            P(),
            P(None, "tok", None),
            P(),
            P("section", None, None),
            P("section", None, None, "rep"),
            P("section", "rep", None),
            P("section", None, None),
            P("section", "tok", None, None, "rep"),
            P("section", "tok", "rep", None),
        ),
        out_specs=(P("section", None, "tok", None), P("section", None, "tok", None, None, "rep")),
        check_vma=False,
    )
```

profile of v0, /device:TPU:1, one launch (start us, length us, event | category | flops | bytes accessed | tf_op | source)
XLA Modules:
  0.0 1002.5 jit_solution(15672951469307340651)
XLA Ops:
  20.4 77.7 %all-gather.4.cloned.1.call-done = bf16[4096,2,256]{0,2,1:T(8,128)(2,1)} async-done(((bf16[128,2,256]{0,2,1:T(8,128)(2,1)}), bf16[4096,2,256]{0,2,1:T(8,128)(2,1)}) %all-gather.4.cloned.1.call-update) | async-done | bytes 4194320 | tf_op jit(solution)/shard_map/all_gather | solution.py:122
  98.1 34.9 %while.54 = (s32[]{:T(128)}, f32[4,128]{1,0:T(4,128)S(1)}, f32[4,128]{1,0:T(4,128)S(1)}, f32[4,128,64]{1,2,0:T(8,128)}, s32[128]{0:T(128)}, /*index=5*/s32[4096]...) while((s32[]{:T(128)}, f32[4,128]{1,0:T(4,128)S(1)}, ...), condition=%wide.region_4.5_spmd.clone, body=%wide.region_1.4_spmd.clone.sunk | while | flops 476548736 | bytes 14800775 | solution.py:136
  100.4 2.1 constant_dynamic-slice_fusion.18
  109.1 2.1 constant_dynamic-slice_fusion.18
  117.9 2.1 constant_dynamic-slice_fusion.18
  126.6 2.1 constant_dynamic-slice_fusion.18
  134.0 2.1 fusion.102
  138.6 47.0 %all-reduce.7.cloned.1.call-done = f32[128,1024]{1,0:T(8,128)} async-done(((f32[128,1024]{1,0:T(8,128)}), f32[128,1024]{1,0:T(8,128)}) %all-reduce.7.cloned.1.call-update) | async-done | bytes 524304 | tf_op jit(solution)/shard_map/psum | solution.py:146
  189.3 45.4 %all_to_all.30 = bf16[32,1,20,1024]{3,2,1,0:T(8,128)(2,1)S(1)} all-to-all(bf16[32,1,20,1024]{3,2,1,0:T(8,128)(2,1)S(1)} %bitcast.386), channel_id=1, replica_groups=mesh['section'=2,'tok'=32,'rep'=4] {'tok'}, dimensions={0} | all-to-all | bytes 2621440 | tf_op jit(solution)/shard_map/all_to_all | solution.py:170
  234.8 1.8 convolution_bitcast_fusion.2
  237.5 1.9 copy.87
  239.4 6.3 all-to-all-start.1
  248.9 31.6 %all-to-all-done.1 = bf16[32,1,20,1024]{3,2,1,0:T(8,128)(2,1)S(1)} async-done(((bf16[32,1,20,1024]{3,2,1,0:T(8,128)(2,1)}), bf16[32,1,20,1024]{3,2,1,0:T(8,128)(2,1)S(1)}, u32[]{:S(2)}, u32[]{:S(2)}) %all-to-all-start.1) | async-done | bytes 1310752 | tf_op jit(solution)/shard_map/all_to_all | solution.py:175
  283.5 2.2 gather_fusion
  288.0 48.3 %all-reduce.9.cloned.1.call-done = f32[128,1024]{1,0:T(8,128)} async-done(((f32[128,1024]{1,0:T(8,128)}), f32[128,1024]{1,0:T(8,128)}) %all-reduce.9.cloned.1.call-update) | async-done | bytes 524304 | tf_op jit(solution)/shard_map/psum | solution.py:190
  339.2 3.7 collective-permute-done
  349.9 75.5 %all-gather.6.cloned.1.call-done = bf16[4096,2,256]{0,2,1:T(8,128)(2,1)} async-done(((bf16[128,2,256]{0,2,1:T(8,128)(2,1)}), bf16[4096,2,256]{0,2,1:T(8,128)(2,1)}) %all-gather.6.cloned.1.call-update) | async-done | bytes 4194320 | tf_op jit(solution)/shard_map/all_gather | solution.py:122
  425.5 35.0 %while.55 = (s32[]{:T(128)}, f32[4,128]{1,0:T(4,128)S(1)}, f32[4,128]{1,0:T(4,128)S(1)}, f32[4,128,64]{1,2,0:T(8,128)}, s32[128]{0:T(128)}, /*index=5*/s32[4096]...) while((s32[]{:T(128)}, f32[4,128]{1,0:T(4,128)S(1)}, ...), condition=%wide.region_21.23_spmd.clone, body=%wide.region_18.22_spmd.clone.sunk | while | flops 476548736 | bytes 14800775 | solution.py:136
  427.8 2.1 constant_dynamic-slice_fusion.19
  436.6 2.1 constant_dynamic-slice_fusion.19
  445.3 2.1 constant_dynamic-slice_fusion.19
  454.0 2.1 constant_dynamic-slice_fusion.19
  461.4 2.1 fusion.100
  466.5 46.4 %all-reduce.11.cloned.1.call-done = f32[128,1024]{1,0:T(8,128)} async-done(((f32[128,1024]{1,0:T(8,128)}), f32[128,1024]{1,0:T(8,128)}) %all-reduce.11.cloned.1.call-update) | async-done | bytes 524304 | tf_op jit(solution)/shard_map/psum | solution.py:146
  516.0 45.4 %all_to_all.31 = bf16[32,1,20,1024]{3,2,1,0:T(8,128)(2,1)S(1)} all-to-all(bf16[32,1,20,1024]{3,2,1,0:T(8,128)(2,1)S(1)} %bitcast.387), channel_id=1, replica_groups=mesh['section'=2,'tok'=32,'rep'=4] {'tok'}, dimensions={0} | all-to-all | bytes 2621440 | tf_op jit(solution)/shard_map/all_to_all | solution.py:170
  561.4 1.8 convolution_bitcast_fusion.1
  564.2 1.9 copy.93
  566.1 6.3 all-to-all-start.3
  575.3 31.8 %all-to-all-done.3 = bf16[32,1,20,1024]{3,2,1,0:T(8,128)(2,1)S(1)} async-done(((bf16[32,1,20,1024]{3,2,1,0:T(8,128)(2,1)}), bf16[32,1,20,1024]{3,2,1,0:T(8,128)(2,1)S(1)}, u32[]{:S(2)}, u32[]{:S(2)}) %all-to-all-start.3) | async-done | bytes 1310752 | tf_op jit(solution)/shard_map/all_to_all | solution.py:175
  610.1 2.2 gather_fusion.1
  614.8 48.5 %all-reduce.13.cloned.1.call-done = f32[128,1024]{1,0:T(8,128)} async-done(((f32[128,1024]{1,0:T(8,128)}), f32[128,1024]{1,0:T(8,128)}) %all-reduce.13.cloned.1.call-update) | async-done | bytes 524304 | tf_op jit(solution)/shard_map/psum | solution.py:190
  663.2 2.1 select_bitcast_fusion
  666.6 3.9 collective-permute-done.1
  673.9 79.2 %all-gather.8.cloned.1.call-done = bf16[4096,2,256]{0,2,1:T(8,128)(2,1)} async-done(((bf16[128,2,256]{0,2,1:T(8,128)(2,1)}), bf16[4096,2,256]{0,2,1:T(8,128)(2,1)}) %all-gather.8.cloned.1.call-update) | async-done | bytes 4194320 | tf_op jit(solution)/shard_map/all_gather | solution.py:122
  753.1 34.7 %while.56 = (s32[]{:T(128)}, f32[4,128]{1,0:T(4,128)S(1)}, f32[4,128]{1,0:T(4,128)S(1)}, f32[4,128,64]{1,2,0:T(8,128)}, s32[128]{0:T(128)}, /*index=5*/s32[4096]...) while((s32[]{:T(128)}, f32[4,128]{1,0:T(4,128)S(1)}, ...), condition=%wide.region_38.40_spmd.clone, body=%wide.region_35.39_spmd.clone.sunk | while | flops 476548736 | bytes 14800775 | solution.py:136
  755.4 2.1 constant_dynamic-slice_fusion.20
  764.0 2.1 constant_dynamic-slice_fusion.20
  772.7 2.1 constant_dynamic-slice_fusion.20
  781.4 2.1 constant_dynamic-slice_fusion.20
  788.8 2.1 fusion.98
  791.6 48.8 %all-reduce.15.cloned.1.call-done = f32[128,1024]{1,0:T(8,128)} async-done(((f32[128,1024]{1,0:T(8,128)}), f32[128,1024]{1,0:T(8,128)}) %all-reduce.15.cloned.1.call-update) | async-done | bytes 524304 | tf_op jit(solution)/shard_map/psum | solution.py:146
  845.3 45.4 %all_to_all.32 = bf16[32,1,20,1024]{3,2,1,0:T(8,128)(2,1)S(1)} all-to-all(bf16[32,1,20,1024]{3,2,1,0:T(8,128)(2,1)S(1)} %bitcast.388), channel_id=1, replica_groups=mesh['section'=2,'tok'=32,'rep'=4] {'tok'}, dimensions={0} | all-to-all | bytes 2621440 | tf_op jit(solution)/shard_map/all_to_all | solution.py:170
  893.5 1.9 copy.99
  895.4 6.5 all-to-all-start.5
  902.2 34.3 %all-to-all-done.5 = bf16[32,1,20,1024]{3,2,1,0:T(8,128)(2,1)} async-done(((bf16[32,1,20,1024]{3,2,1,0:T(8,128)(2,1)}), bf16[32,1,20,1024]{3,2,1,0:T(8,128)(2,1)}, u32[]{:S(2)}, u32[]{:S(2)}) %all-to-all-start.5) | async-done | bytes 1310752 | tf_op jit(solution)/shard_map/all_to_all | solution.py:175
  936.5 3.1 convert_reduce_fusion
  941.0 2.1 gather_fusion.2
  950.3 43.7 %all-reduce.17.cloned.1.call-done = f32[128,1024]{1,0:T(8,128)} async-done(((f32[128,1024]{1,0:T(8,128)}), f32[128,1024]{1,0:T(8,128)}) %all-reduce.17.cloned.1.call-update) | async-done | bytes 524304 | tf_op jit(solution)/shard_map/psum | solution.py:190
  (473 shorter events, 157.1 us)
Async XLA Ops:
  7.2 227.6 %copy-start = (bf16[1,1,1024,2,352]{2,4,3,1,0:T(8,128)(2,1)S(1)}, bf16[1,1,1024,2,352]{2,4,3,1,0:T(8,128)(2,1)}, u32[]{:S(2)}) copy-start(bf16[1,1,1024,2,352]{2,4,3,1,0:T(8,128)(2,1)} %param.26) | copy-start | bytes 4325380
  7.2 3.9 copy-start.17
  7.2 90.9 %all-gather.4.cloned.1.call-start = ((), (), s32[]{:S(2)}) async-start(), calls=%async_computation.6 | async-start | bytes 4325376 | tf_op jit(solution)/shard_map/all_gather | solution.py:122
  9.3 3.1 copy-start.38
  11.0 87.0 %copy-start.7 = (bf16[1,1024,3,256]{1,3,2,0:T(8,128)(2,1)}, bf16[1,1024,3,256]{1,3,2,0:T(8,128)(2,1)S(1)}, u32[]{:S(2)}) copy-start(bf16[1,1024,3,256]{1,3,2,0:T(8,128)(2,1)S(1)} %copy.83) | copy-start | bytes 4718596
  14.2 171.4 %all-reduce.7.cloned.1.call-start = ((), (), s32[]{:S(2)}) async-start(), calls=%async_computation.7 | async-start | bytes 1048576 | tf_op jit(solution)/shard_map/psum | solution.py:146
  16.2 81.8 %copy-start.45 = (s32[2,128]{1,0:T(2,128)}, s32[2,128]{1,0:T(2,128)S(1)}, u32[]{:S(2)}) copy-start(s32[2,128]{1,0:T(2,128)S(1)} %get-tuple-element.708) | copy-start | bytes 3076
  100.4 2.1 copy-start.21
  109.1 2.1 copy-start.21
  126.6 2.1 copy-start.21
  133.0 52.6 %copy-start.18 = (bf16[2,128,1024]{2,1,0:T(8,128)(2,1)S(1)}, bf16[2,128,1024]{2,1,0:T(8,128)(2,1)}, u32[]{:S(2)}) copy-start(bf16[2,128,1024]{2,1,0:T(8,128)(2,1)} %param.18) | copy-start | bytes 1572868
  239.4 6.4 copy-start.44
  239.4 41.1 %all-to-all-start.1 = ((bf16[32,1,20,1024]{3,2,1,0:T(8,128)(2,1)}), bf16[32,1,20,1024]{3,2,1,0:T(8,128)(2,1)S(1)}, u32[]{:S(2)}, u32[]{:S(2)}) async-start(bf16[32,1,20,1024]{3,2,1,0:T(8,128)(2,1)} %copy.87), calls=%async_computation.1 | async-start | bytes 3145728 | tf_op jit(solution)/shard_map/all_to_all | solution.py:175
  245.7 90.7 %all-reduce.9.cloned.1.call-start = ((), (), s32[]{:S(2)}) async-start(), calls=%async_computation.8 | async-start | bytes 1048576 | tf_op jit(solution)/shard_map/psum | solution.py:190
  283.5 2.2 copy-start.48
  287.0 56.8 %copy-start.8 = (bf16[1,1024,3,256]{1,3,2,0:T(8,128)(2,1)S(1)}, bf16[1,1024,3,256]{1,3,2,0:T(8,128)(2,1)}, u32[]{:S(2)}) copy-start(bf16[1,1024,3,256]{1,3,2,0:T(8,128)(2,1)} %copy-done.7) | copy-start | bytes 4718596
  287.0 56.7 %copy-start.39 = (f32[1,1,1024]{2,1,0:T(1,128)S(1)}, f32[1,1,1024]{2,1,0:T(1,128)}, u32[]{:S(2)}) copy-start(f32[1,1,1024]{2,1,0:T(1,128)} %copy-done.38) | copy-start | bytes 12292
  288.0 137.5 %all-gather.6.cloned.1.call-start = ((), (), s32[]{:S(2)}) async-start(), calls=%async_computation.9 | async-start | bytes 4325376 | tf_op jit(solution)/shard_map/all_gather | solution.py:122
  337.7 5.4 copy-start.28
  337.7 5.2 collective-permute-start
  345.3 167.7 %all-reduce.11.cloned.1.call-start = ((), (), s32[]{:S(2)}) async-start(), calls=%async_computation.10 | async-start | bytes 1048576 | tf_op jit(solution)/shard_map/psum | solution.py:146
  346.7 78.8 %copy-start.31 = (s32[16,2,128]{2,0,1:T(8,128)}, s32[16,2,128]{2,0,1:T(8,128)S(1)}, u32[]{:S(2)}) copy-start(s32[16,2,128]{2,0,1:T(8,128)S(1)} %reduce-window.24) | copy-start | bytes 49156
  445.3 2.1 copy-start.23
  454.0 2.1 copy-start.23
  460.4 52.6 %copy-start.16 = (bf16[128,1024]{1,0:T(8,128)(2,1)S(1)}, bf16[128,1024]{1,0:T(8,128)(2,1)}, u32[]{:S(2)}) copy-start(bf16[128,1024]{1,0:T(8,128)(2,1)} %copy-done.15) | copy-start | bytes 786436
  566.0 6.4 copy-start.42
  566.1 41.1 %all-to-all-start.3 = ((bf16[32,1,20,1024]{3,2,1,0:T(8,128)(2,1)}), bf16[32,1,20,1024]{3,2,1,0:T(8,128)(2,1)S(1)}, u32[]{:S(2)}, u32[]{:S(2)}) async-start(bf16[32,1,20,1024]{3,2,1,0:T(8,128)(2,1)} %copy.93), calls=%async_computation.3 | async-start | bytes 3145728 | tf_op jit(solution)/shard_map/all_to_all | solution.py:175
  572.4 90.8 %all-reduce.13.cloned.1.call-start = ((), (), s32[]{:S(2)}) async-start(), calls=%async_computation.11 | async-start | bytes 1048576 | tf_op jit(solution)/shard_map/psum | solution.py:190
  610.1 2.2 copy-start.49
  612.3 50.9 %copy-start.29 = (bf16[128,1024]{1,0:T(8,128)(2,1)S(1)}, bf16[128,1024]{1,0:T(8,128)(2,1)}, u32[]{:S(2)}) copy-start(bf16[128,1024]{1,0:T(8,128)(2,1)} %copy-done.28) | copy-start | bytes 786436
  614.7 56.7 %copy-start.9 = (bf16[1,1024,3,256]{1,3,2,0:T(8,128)(2,1)S(1)}, bf16[1,1024,3,256]{1,3,2,0:T(8,128)(2,1)}, u32[]{:S(2)}) copy-start(bf16[1,1024,3,256]{1,3,2,0:T(8,128)(2,1)} %copy-done.7) | copy-start | bytes 4718596
  614.7 56.7 %copy-start.40 = (f32[1,1,1024]{2,1,0:T(1,128)S(1)}, f32[1,1,1024]{2,1,0:T(1,128)}, u32[]{:S(2)}) copy-start(f32[1,1,1024]{2,1,0:T(1,128)} %copy-done.38) | copy-start | bytes 12292
  614.7 138.4 %all-gather.8.cloned.1.call-start = ((), (), s32[]{:S(2)}) async-start(), calls=%async_computation.12 | async-start | bytes 4325376 | tf_op jit(solution)/shard_map/all_gather | solution.py:122
  663.2 7.3 copy-start.19
  665.4 5.4 copy-start.25
  665.4 5.2 collective-permute-start.1
  672.9 167.4 %all-reduce.15.cloned.1.call-start = ((), (), s32[]{:S(2)}) async-start(), calls=%async_computation.13 | async-start | bytes 1048576 | tf_op jit(solution)/shard_map/psum | solution.py:146
  787.8 52.6 %copy-start.14 = (bf16[128,1024]{1,0:T(8,128)(2,1)S(1)}, bf16[128,1024]{1,0:T(8,128)(2,1)}, u32[]{:S(2)}) copy-start(bf16[128,1024]{1,0:T(8,128)(2,1)} %copy-done.13) | copy-start | bytes 786436
  895.4 6.5 copy-start.41
  895.4 6.5 copy-start.43
  895.4 6.6 copy-start.30
  895.4 6.8 copy-start.46
  895.4 41.1 %all-to-all-start.5 = ((bf16[32,1,20,1024]{3,2,1,0:T(8,128)(2,1)}), bf16[32,1,20,1024]{3,2,1,0:T(8,128)(2,1)}, u32[]{:S(2)}, u32[]{:S(2)}) async-start(bf16[32,1,20,1024]{3,2,1,0:T(8,128)(2,1)} %copy.99), calls=%async_computation.5 | async-start | bytes 3145728 | tf_op jit(solution)/shard_map/all_to_all | solution.py:175
  901.9 92.1 %all-reduce.17.cloned.1.call-start = ((), (), s32[]{:S(2)}) async-start(), calls=%async_computation.14 | async-start | bytes 1048576 | tf_op jit(solution)/shard_map/psum | solution.py:190
  943.1 2.3 copy-start.47
  944.5 49.5 %copy-start.20 = (f32[128,1024]{1,0:T(8,128)S(1)}, f32[128,1024]{1,0:T(8,128)}, u32[]{:S(2)}) copy-start(f32[128,1024]{1,0:T(8,128)} %all-reduce.15.cloned.1.call-done) | copy-start | bytes 1572868
  944.5 49.5 %copy-start.26 = (bf16[128,1024]{1,0:T(8,128)(2,1)S(1)}, bf16[128,1024]{1,0:T(8,128)(2,1)}, u32[]{:S(2)}) copy-start(bf16[128,1024]{1,0:T(8,128)(2,1)} %copy-done.25) | copy-start | bytes 786436
  945.4 49.7 %copy-start.27 = (bf16[1,128,1024]{2,1,0:T(8,128)(2,1)S(1)}, bf16[1,128,1024]{2,1,0:T(8,128)(2,1)}, u32[]{:S(2)}) copy-start(bf16[1,128,1024]{2,1,0:T(8,128)(2,1)} %get-tuple-element.669) | copy-start | bytes 786436
  (73 other events, 111.8 us)
Sparse Core Ops, SparseCore 0:
  14.3 83.7 all-gather.3
  136.2 49.3 all-reduce.6
  288.1 48.2 all-reduce.8
  345.5 79.9 all-gather.5
  463.6 49.3 all-reduce.10
  614.8 48.3 all-reduce.12
  673.1 79.9 all-gather.7
  791.0 49.3 all-reduce.14
  945.6 48.3 all-reduce.16
where the time goes:
time: 1010 us; the launch traced here: 1000 us
  waiting for transfers between devices  620 us (61%)
  blocking collectives  136 us (13%)
  other arithmetic  82.9 us (8%)
  local copies, waits for them, and re-layouts  77.7 us (8%)
  matrix products  45.3 us (4%)
  starting transfers between devices  22.5 us (2%)
  between operations  16.4 us (2%)
    all_gather x3, waiting for transfers between devices, per_device(): piece = lax.all_gather(keys_vals, 'tok', axis=0, tiled=True)  232 us
    psum x3, waiting for transfers between devices, per_device(): mid = resid + lax.psum(attn_part, 'rep')  142 us
    psum x3, waiting for transfers between devices, per_device(): expert_total = lax.psum(expert_local, 'rep')  141 us
    all_to_all x3, blocking collectives, per_device(): lax.all_to_all(copies, 'tok', split_axis=0, concat_axis=0, tiled=True)  136 us
    all_to_all x3, waiting for transfers between devices, per_device(): lax.all_to_all(jnp.einsum('secf,efd->secd', hidden, w_down, preferred_ele...  97.7 us
    slice x12, local copies, waits for them, and re-layouts, attend(): keys_vals[:, 1].reshape(rows_key, heads_here, head_size).astype(jnp.float32)  25.2 us
  transfers between devices with their start and end apart: 14, of which 14 were waited for; matrix products, arithmetic and copies ran while one was open for 3% of the time, Pallas kernels for 0%

commit v1 on v0

v1 whole, which is shorter than its diff:
```python
import jax
import jax.numpy as jnp
from jax import lax
from jax.sharding import PartitionSpec as P

HEAD_DIM = 64
TOP = 2
PAGE = 128
CAP = 20


NEG_FILL = -1e30


def shifted(value, axis, steps):
    count = lax.axis_size(axis)
    first, last = (max(0, -steps), min(count, count - steps))
    return lax.ppermute(value, axis, [(source, source + steps) for source in range(first, last)])


def rms_scale(values, gains):
    return values * lax.rsqrt(jnp.mean(values * values, axis=-1, keepdims=True) + 1e-06) * gains


def attend(carry, queries, keys_vals, seg_query, pos_query, seg_key, pos_key):
    run_max, run_sum, run_acc = carry
    heads_here = run_acc.shape[0]
    head_size = run_acc.shape[2]
    rows_key = keys_vals.shape[0]
    key_part = keys_vals[:, 0].reshape(rows_key, heads_here, head_size)
    val_part = keys_vals[:, 1].reshape(rows_key, heads_here, head_size).astype(jnp.float32)
    scores = jnp.einsum(
        "thd,nhd->htn", queries, key_part, preferred_element_type=jnp.float32
    ) * head_size ** (-0.5)
    visible = (seg_query[:, None] == seg_key[None, :]) & (pos_query[:, None] >= pos_key[None, :])
    masked = jnp.where(visible[None], scores, NEG_FILL)
    new_max = jnp.maximum(run_max, jnp.max(masked, axis=-1))
    weights = jnp.where(visible[None], jnp.exp(masked - new_max[..., None]), 0.0)
    decay = jnp.exp(run_max - new_max)
    run_sum = run_sum * decay + jnp.sum(weights, axis=-1)
    run_acc = run_acc * decay[..., None] + jnp.einsum(
        "htn,nhd->htd", weights, val_part, precision=lax.Precision.HIGHEST
    )
    return (new_max, run_sum, run_acc)


def place_pages(pages, keys_vals, table_row, tok_index):
    rows_here = keys_vals.shape[0]
    blocks_dev = pages.shape[0]
    page_rows = pages.shape[1]
    block_ids = jnp.arange(table_row.shape[0], dtype=jnp.int32)
    wanted = tok_index * blocks_dev + 0
    source = jnp.sum(jnp.where(table_row == wanted, block_ids, 0))
    offset = source * page_rows
    inside = (offset >= 0) & (offset + page_rows <= rows_here)
    block = lax.dynamic_slice_in_dim(
        keys_vals, jnp.clip(offset, 0, rows_here - page_rows), page_rows, 0
    )
    updated = [jnp.where(inside, block, pages[0])]
    return jnp.stack(updated)


def one_layer(
    layer_in, seg_all, table_row, pick_rows, gains, w_qkv, w_out, w_router, w_in, w_down
):
    tok_index = lax.axis_index("tok")
    tok_count = lax.axis_size("tok")
    tok_rows = layer_in.shape[0]
    width = layer_in.shape[1]
    col_width = w_qkv.shape[1] // 3
    head_count = col_width // HEAD_DIM
    experts_all = w_router.shape[1]
    local_pieces = w_in.shape[0]
    split_count = local_pieces * tok_count // experts_all
    blocks_dev = tok_rows // PAGE
    row_ids = jnp.arange(tok_rows, dtype=jnp.int32)
    pos_query = tok_index * tok_rows + row_ids
    seg_query = lax.dynamic_slice_in_dim(seg_all, tok_index * tok_rows, tok_rows)
    resid = layer_in.astype(jnp.float32)
    normed = rms_scale(resid, gains[0]).astype(jnp.bfloat16)
    projected = jnp.dot(normed, w_qkv, preferred_element_type=jnp.float32).astype(jnp.bfloat16)
    projected = projected.reshape(tok_rows, 3, col_width)
    queries = projected[:, 0].reshape(tok_rows, head_count, HEAD_DIM)
    keys_vals = projected[:, 1:]
    soft_init = (
        jnp.full((head_count, tok_rows), NEG_FILL, jnp.float32),
        jnp.zeros((head_count, tok_rows), jnp.float32),
        jnp.zeros((head_count, tok_rows, HEAD_DIM), jnp.float32),
    )
    empty_pages = jnp.zeros((blocks_dev, PAGE, 2, col_width), jnp.bfloat16)
    piece = lax.all_gather(keys_vals, "tok", axis=0, tiled=True)
    rows_key = piece.shape[0]
    step_rows = 1024
    while rows_key % step_rows != 0:
        step_rows = step_rows // 2
    turns = rows_key // step_rows

    def key_block(index, soft_now):
        start = index * step_rows
        block = lax.dynamic_slice_in_dim(piece, start, step_rows, 0)
        seg_key = lax.dynamic_slice_in_dim(seg_all, start, step_rows)
        pos_key = start + jnp.arange(step_rows, dtype=jnp.int32)
        return attend(soft_now, queries, block, seg_query, pos_query, seg_key, pos_key)

    soft_next = lax.fori_loop(0, turns, key_block, soft_init)
    pages = place_pages(empty_pages, piece, table_row, tok_index)
    run_max, run_sum, run_acc = soft_next
    context = (
        (run_acc / run_sum[..., None])
        .transpose(1, 0, 2)
        .reshape(tok_rows, col_width)
        .astype(jnp.bfloat16)
    )
    attn_part = jnp.dot(context, w_out, preferred_element_type=jnp.float32)
    mid = resid + lax.psum(attn_part, "rep")
    normed_mid = rms_scale(mid, gains[1]).astype(jnp.bfloat16)
    logits = jnp.dot(normed_mid, w_router, preferred_element_type=jnp.float32)
    expert_ids = jnp.arange(experts_all, dtype=jnp.int32)
    chosen = (pick_rows[:, :, None] == expert_ids[None, None, :]).astype(jnp.int32)
    picked_logit = jnp.sum(chosen.astype(jnp.float32) * logits[:, None, :], axis=-1)
    top_logit = jnp.max(picked_logit, axis=-1, keepdims=True)
    raised = jnp.exp(picked_logit - top_logit)
    gate_vals = raised / jnp.sum(raised, axis=-1, keepdims=True)
    ordered = chosen.transpose(1, 0, 2).reshape(TOP * tok_rows, experts_all)
    slot_of = jnp.sum((jnp.cumsum(ordered, axis=0) - 1) * ordered, axis=-1)
    flat_slot = pick_rows.T.reshape(TOP * tok_rows) * CAP + slot_of
    slot_ids = jnp.arange(experts_all * CAP, dtype=jnp.int32)
    hits = (flat_slot[:, None] == slot_ids[None, :]).astype(jnp.int32)
    hits = jnp.sum(hits.reshape(TOP, tok_rows, experts_all * CAP), axis=0).astype(jnp.bfloat16)
    dispatch = lax.dot_general(
        hits, normed_mid, (((0,), (0,)), ((), ())), preferred_element_type=jnp.float32
    ).astype(jnp.bfloat16)
    copies = jnp.broadcast_to(
        dispatch.reshape(experts_all, 1, CAP, width), (experts_all, split_count, CAP, width)
    )
    copies = copies.reshape(tok_count, local_pieces, CAP, width)
    act = jnp.einsum(
        "secd,edgf->secgf",
        lax.all_to_all(copies, "tok", split_axis=0, concat_axis=0, tiled=True),
        w_in,
        preferred_element_type=jnp.float32,
    )
    hidden = (jax.nn.gelu(act[..., 0, :]) * act[..., 1, :]).astype(jnp.bfloat16)
    returned = lax.all_to_all(
        jnp.einsum("secf,efd->secd", hidden, w_down, preferred_element_type=jnp.float32).astype(
            jnp.bfloat16
        ),
        "tok",
        split_axis=0,
        concat_axis=0,
        tiled=True,
    )
    summed = jnp.sum(
        returned.reshape(experts_all, split_count, CAP, width).astype(jnp.float32), axis=1
    )
    summed = summed.reshape(experts_all * CAP, width)
    gathered = jnp.take(summed, flat_slot, axis=0).reshape(TOP, tok_rows, width)
    expert_local = jnp.sum(gate_vals.T[:, :, None] * gathered, axis=0)
    expert_total = lax.psum(expert_local, "rep")
    layer_result = (mid + expert_total).astype(jnp.bfloat16)
    return layer_result, pages


def per_device(
    inputs,
    segment_ids,
    picks,
    page_table,
    norm_gains,
    attn_qkv,
    attn_out,
    router,
    expert_in,
    expert_out,
):
    section_index = lax.axis_index("section")
    is_first = section_index == 0
    width = inputs.shape[2]
    own = (
        norm_gains[0],
        attn_qkv[0].reshape(width, -1),
        attn_out[0],
        router[0],
        expert_in[0],
        expert_out[0],
    )
    swap = [(0, 1), (1, 0)]
    other = tuple(lax.ppermute(w, "section", swap) for w in own)
    weights_of = [
        tuple(jnp.where(is_first, a, b) for a, b in zip(own, other)),
        tuple(jnp.where(is_first, b, a) for a, b in zip(own, other)),
    ]
    micro = section_index
    hidden = lax.dynamic_index_in_dim(inputs, micro, 0, keepdims=False)
    seg_all = lax.dynamic_index_in_dim(segment_ids, micro, 0, keepdims=False)
    table_row = lax.dynamic_index_in_dim(page_table, micro, 0, keepdims=False)
    pick_rows = lax.dynamic_index_in_dim(picks, micro, 0, keepdims=False)
    results = []
    for layer in range(2):
        hidden, pages = one_layer(hidden, seg_all, table_row, pick_rows, *weights_of[layer])
        results.append((hidden, pages))
    (res0, pages0), (res1, pages1) = results
    got0 = lax.ppermute(res0, "section", [(1, 0)])
    gotp0 = lax.ppermute(pages0, "section", [(1, 0)])
    got1 = lax.ppermute(res1, "section", [(0, 1)])
    gotp1 = lax.ppermute(pages1, "section", [(0, 1)])
    outputs = jnp.where(is_first, jnp.stack([res0, got0]), jnp.stack([got1, res1]))
    page_out = jnp.where(is_first, jnp.stack([pages0, gotp0]), jnp.stack([gotp1, pages1]))
    return (outputs[None], page_out[None])


def solution(mesh):
    return jax.shard_map(
        per_device,
        mesh=mesh,
        in_specs=(
            P(None, "tok", None),
            P(),
            P(None, "tok", None),
            P(),
            P("section", None, None),
            P("section", None, None, "rep"),
            P("section", "rep", None),
            P("section", None, None),
            P("section", "tok", None, None, "rep"),
            P("section", "tok", "rep", None),
        ),
        out_specs=(P("section", None, "tok", None), P("section", None, "tok", None, None, "rep")),
        check_vma=False,
    )
```

time: 1010 us -> 636 us (0.63)
  waiting for transfers between devices: 620 us -> 450 us
  blocking collectives: 136 us -> 45.7 us
  other arithmetic: 82.9 us -> 22 us
  local copies, waits for them, and re-layouts: 77.7 us -> 23.3 us
  starting transfers between devices: 22.5 us -> 47.2 us
  matrix products: 45.3 us -> 30.8 us
    psum x6 -> x4, waiting for transfers between devices: 283 us -> 183 us  [the longest x2 98.6 us: one_layer(): mid = resid + lax.psum(attn_part, 'rep')]
    all_to_all x3 -> x1, blocking collectives: 136 us -> 45.7 us  [one_layer(): lax.all_to_all(copies, 'tok', split_axis=0, concat_axis=0, tiled=True)]
    all_gather x3 -> x2, waiting for transfers between devices: 232 us -> 164 us  [one_layer(): piece = lax.all_gather(keys_vals, 'tok', axis=0, tiled=True)]
    ppermute x2 -> x10, starting transfers between devices: 2.75 us -> 23.6 us  [the longest x6 9.87 us: per_device(): other = tuple((lax.ppermute(w, 'section', swap) for w in own))]
    and x12 -> x8, other arithmetic: 19.7 us -> 2.7 us  [attend(): (seg_query[:, None] == seg_key[None, :]) & (pos_query[:, None] >= pos_key...]
    slice x12 -> x8, local copies, waits for them, and re-layouts: 25.2 us -> 10.2 us  [attend(): keys_vals[:, 1].reshape(rows_key, heads_here, head_size).astype(jnp.float32)]
    reduce_sum x12 -> x8, other arithmetic: 18 us -> 4.24 us  [attend(): run_sum = run_sum * decay + jnp.sum(weights, axis=-1)]
    dot_general x18 -> x12, matrix products: 21.1 us -> 14.6 us  [the longest x2 5.36 us: one_layer(): jnp.einsum('secd,edgf->secgf', lax.all_to_all(copies, 'tok', split_axis=0...]
  transfers between devices with their start and end apart: 14 -> 19, of which waited for: 14 -> 13; matrix products, arithmetic and copies ran while one was open for 3% -> 4% of each run, Pallas kernels for 0% -> 0%
where the time goes in v1:
time: 636 us; the launch traced here: 634 us
  waiting for transfers between devices  450 us (71%)
  starting transfers between devices  47.2 us (7%)
  blocking collectives  45.7 us (7%)
  matrix products  30.8 us (5%)
  local copies, waits for them, and re-layouts  23.3 us (4%)
  other arithmetic  22 us (3%)
  between operations  15.4 us (2%)
    all_gather x2, waiting for transfers between devices, one_layer(): piece = lax.all_gather(keys_vals, 'tok', axis=0, tiled=True)  164 us
    psum x2, waiting for transfers between devices, one_layer(): mid = resid + lax.psum(attn_part, 'rep')  98.6 us
    psum x2, waiting for transfers between devices, one_layer(): expert_total = lax.psum(expert_local, 'rep')  84.6 us
    all_to_all x2, waiting for transfers between devices, one_layer(): lax.all_to_all(jnp.einsum('secf,efd->secd', hidden, w_down, preferred_ele...  63.3 us
    all_to_all x1, blocking collectives, one_layer(): lax.all_to_all(copies, 'tok', split_axis=0, concat_axis=0, tiled=True)  45.7 us
    all_to_all x1, waiting for transfers between devices, one_layer(): lax.all_to_all(copies, 'tok', split_axis=0, concat_axis=0, tiled=True)  28.6 us
    all_to_all x2, starting transfers between devices, one_layer(): lax.all_to_all(jnp.einsum('secf,efd->secd', hidden, w_down, preferred_ele...  13.6 us
  transfers between devices with their start and end apart: 19, of which 13 were waited for; matrix products, arithmetic and copies ran while one was open for 4% of the time, Pallas kernels for 0%

profile of v1, /device:TPU:1, one launch (start us, length us, event | category | flops | bytes accessed | tf_op | source)
XLA Modules:
  0.0 634.5 jit_solution(9774270104577038417)
XLA Ops:
  7.2 1.8 copy.55
  9.0 3.3 collective-permute-start.1
  12.6 2.9 collective-permute-done
  15.5 2.1 fusion.48
  19.5 79.9 %all-gather.3.cloned.1.call-done = bf16[4096,2,256]{0,2,1:T(8,128)(2,1)} async-done(((bf16[128,2,256]{0,2,1:T(8,128)(2,1)}), bf16[4096,2,256]{0,2,1:T(8,128)(2,1)}) %all-gather.3.cloned.1.call-update) | async-done | bytes 4194320 | tf_op jit(solution)/shard_map/all_gather | solution.py:91
  99.4 17.1 %while.36 = (s32[]{:T(128)}, f32[4,128]{1,0:T(4,128)S(1)}, f32[4,128]{1,0:T(4,128)S(1)}, f32[4,128,64]{1,2,0:T(8,128)S(1)}, s32[128]{0:T(128)S(1)}, /*index=5*/s...) while((s32[]{:T(128)}, f32[4,128]{1,0:T(4,128)S(1)}, ...), condition=%wide.region_4.5_spmd.clone, body=%wide.region_1.4_spmd.clone.sunk | while | flops 476548736 | bytes 10344167 | solution.py:105
  99.7 1.3 constant_dynamic-slice_fusion.9
  102.2 1.4 fusion.180
  104.0 1.3 constant_dynamic-slice_fusion.9
  106.5 1.4 fusion.180
  108.3 1.3 constant_dynamic-slice_fusion.9
  110.8 1.4 fusion.180
  112.6 1.3 constant_dynamic-slice_fusion.9
  115.1 1.4 fusion.180
  118.0 49.1 %all-reduce.5.cloned.1.call-done = f32[128,1024]{1,0:T(8,128)} async-done(((f32[128,1024]{1,0:T(8,128)}), f32[128,1024]{1,0:T(8,128)}) %all-reduce.5.cloned.1.call-update) | async-done | bytes 524304 | tf_op jit(solution)/shard_map/psum | solution.py:115
  170.0 1.4 broadcast_in_dim.165
  171.5 9.7 %all-to-all-start = ((bf16[32,1,20,1024]{3,2,1,0:T(8,128)(2,1)}), bf16[32,1,20,1024]{3,2,1,0:T(8,128)(2,1)S(1)}, u32[]{:S(2)}, u32[]{:S(2)}) async-start(bf16[32,1,20,1024]{3,2,1,0:T(8,128)(2,1)} %bitcast.29), calls=%async_computation | async-start | bytes 3145728 | tf_op jit(solution)/shard_map/all_to_all | solution.py:139
  181.2 3.2 collective-permute-start.5
  184.7 2.9 collective-permute-done.5
  187.6 28.6 %all-to-all-done = bf16[32,1,20,1024]{3,2,1,0:T(8,128)(2,1)S(1)} async-done(((bf16[32,1,20,1024]{3,2,1,0:T(8,128)(2,1)}), bf16[32,1,20,1024]{3,2,1,0:T(8,128)(2,1)S(1)}, u32[]{:S(2)}, u32[]{:S(2)}) %all-to-all-start) | async-done | bytes 1310752 | tf_op jit(solution)/shard_map/all_to_all | solution.py:139
  216.2 3.6 convolution_bitcast_fusion.1
  219.8 2.3 fusion.42
  222.1 2.0 copy.59
  224.1 7.5 %all-to-all-start.1 = ((bf16[32,1,20,1024]{3,2,1,0:T(8,128)(2,1)}), bf16[32,1,20,1024]{3,2,1,0:T(8,128)(2,1)S(1)}, u32[]{:S(2)}, u32[]{:S(2)}) async-start(bf16[32,1,20,1024]{3,2,1,0:T(8,128)(2,1)} %copy.59), calls=%async_computation.1 | async-start | bytes 3145728 | tf_op jit(solution)/shard_map/all_to_all | solution.py:144
  231.7 2.9 collective-permute-start.3
  235.6 31.5 %all-to-all-done.1 = bf16[32,1,20,1024]{3,2,1,0:T(8,128)(2,1)S(1)} async-done(((bf16[32,1,20,1024]{3,2,1,0:T(8,128)(2,1)}), bf16[32,1,20,1024]{3,2,1,0:T(8,128)(2,1)S(1)}, u32[]{:S(2)}, u32[]{:S(2)}) %all-to-all-start.1) | async-done | bytes 1310752 | tf_op jit(solution)/shard_map/all_to_all | solution.py:144
  269.9 47.1 %all-reduce.7.cloned.1.call-done = f32[128,1024]{1,0:T(8,128)} async-done(((f32[128,1024]{1,0:T(8,128)}), f32[128,1024]{1,0:T(8,128)}) %all-reduce.7.cloned.1.call-update) | async-done | bytes 524304 | tf_op jit(solution)/shard_map/psum | solution.py:159
  319.9 84.1 %all-gather.5.cloned.1.call-done = bf16[4096,2,256]{0,2,1:T(8,128)(2,1)} async-done(((bf16[128,2,256]{0,2,1:T(8,128)(2,1)}), bf16[4096,2,256]{0,2,1:T(8,128)(2,1)}) %all-gather.5.cloned.1.call-update) | async-done | bytes 4194320 | tf_op jit(solution)/shard_map/all_gather | solution.py:91
  404.0 17.1 %while.37 = (s32[]{:T(128)}, f32[4,128]{1,0:T(4,128)S(1)}, f32[4,128]{1,0:T(4,128)S(1)}, f32[4,128,64]{1,2,0:T(8,128)S(1)}, s32[128]{0:T(128)S(1)}, /*index=5*/s...) while((s32[]{:T(128)}, f32[4,128]{1,0:T(4,128)S(1)}, ...), condition=%wide.region_21.23_spmd.clone, body=%wide.region_18.22_spmd.clone.sunk | while | flops 476548736 | bytes 10344167 | solution.py:105
  404.4 1.3 constant_dynamic-slice_fusion.10
  406.9 1.4 fusion.187
  408.7 1.3 constant_dynamic-slice_fusion.10
  411.2 1.4 fusion.187
  413.0 1.3 constant_dynamic-slice_fusion.10
  415.4 1.4 fusion.187
  419.7 1.4 fusion.187
  422.3 49.5 %all-reduce.9.cloned.1.call-done = f32[128,1024]{1,0:T(8,128)} async-done(((f32[128,1024]{1,0:T(8,128)}), f32[128,1024]{1,0:T(8,128)}) %all-reduce.9.cloned.1.call-update) | async-done | bytes 524304 | tf_op jit(solution)/shard_map/psum | solution.py:115
  474.8 45.7 %all_to_all.20 = bf16[32,1,20,1024]{3,2,1,0:T(8,128)(2,1)S(1)} all-to-all(bf16[32,1,20,1024]{3,2,1,0:T(8,128)(2,1)S(1)} %bitcast.258), channel_id=1, replica_groups=mesh['section'=2,'tok'=32,'rep'=4] {'tok'}, dimensions={0} | all-to-all | bytes 2621440 | tf_op jit(solution)/shard_map/all_to_all | solution.py:139
  520.5 1.8 convolution_bitcast_fusion
  523.4 2.0 copy.64
  525.3 6.1 all-to-all-start.3
  531.7 31.8 %all-to-all-done.3 = bf16[32,1,20,1024]{3,2,1,0:T(8,128)(2,1)S(1)} async-done(((bf16[32,1,20,1024]{3,2,1,0:T(8,128)(2,1)}), bf16[32,1,20,1024]{3,2,1,0:T(8,128)(2,1)S(1)}, u32[]{:S(2)}, u32[]{:S(2)}) %all-to-all-start.3) | async-done | bytes 1310752 | tf_op jit(solution)/shard_map/all_to_all | solution.py:144
  568.6 9.9 %collective-permute-start.8 = (bf16[1,128,2,256]{1,3,2,0:T(8,128)(2,1)S(1)}, bf16[1,128,2,256]{1,3,2,0:T(8,128)(2,1)S(1)}, u32[]{:S(2)}, u32[]{:S(2)}) collective-permute-start(bf16[1,128,2,256]{1,3,2,0:T(8,128)(2,1)S(1)} %get-tuple-element.462), channel_id=1, source_target_pairs={{128,0},{129,1},{130,2},{131,3},{132,4},{133,5},{134,6},{135,7},{1... | collective-permute-start | bytes 393224 | tf_op jit(solution)/shard_map/ppermute | solution.py:204
  578.5 1.3 collective-permute-start.6
  579.8 37.5 %all-reduce.11.cloned.1.call-done = f32[128,1024]{1,0:T(8,128)} async-done(((f32[128,1024]{1,0:T(8,128)}), f32[128,1024]{1,0:T(8,128)}) %all-reduce.11.cloned.1.call-update) | async-done | bytes 524304 | tf_op jit(solution)/shard_map/psum | solution.py:159
  618.4 1.3 collective-permute-start.7
  620.8 1.3 collective-permute-start.9
  622.1 3.7 collective-permute-done.9
  (208 shorter events, 40.5 us)
Async XLA Ops:
  7.2 12.2 %copy-start = (s32[2,4096]{1,0:T(2,128)S(1)}, s32[2,4096]{1,0:T(2,128)}, u32[]{:S(2)}) copy-start(s32[2,4096]{1,0:T(2,128)} %param.17) | copy-start | bytes 98308
  7.2 5.1 copy-start.13
  7.2 5.2 copy-start.4
  7.2 92.2 %all-gather.3.cloned.1.call-start = ((), (), s32[]{:S(2)}) async-start(), calls=%async_computation.4 | async-start | bytes 4325376 | tf_op jit(solution)/shard_map/all_gather | solution.py:91
  9.0 8.7 %copy-start.10 = (bf16[1,1024,3,256]{1,3,2,0:T(8,128)(2,1)}, bf16[1,1024,3,256]{1,3,2,0:T(8,128)(2,1)S(1)}, u32[]{:S(2)}) copy-start(bf16[1,1024,3,256]{1,3,2,0:T(8,128)(2,1)S(1)} %copy.55) | copy-start | bytes 4718596
  9.0 6.5 %collective-permute-start.1 = (bf16[1024,768]{0,1:T(8,128)(2,1)S(1)}, bf16[1024,768]{0,1:T(8,128)(2,1)}, u32[]{:S(2)}, u32[]{:S(2)}) collective-permute-start(bf16[1024,768]{0,1:T(8,128)(2,1)S(1)} %bitcast.264), channel_id=1, source_target_pairs={{0,128},{128,0},{1,129},{129,1},{2,130},{130,2},{3,131},{131,3},{4... | collective-permute-start | bytes 4718600 | tf_op jit(solution)/shard_map/ppermute | solution.py:188
  12.3 3.2 collective-permute-start
  15.5 3.1 copy-start.6
  15.5 3.2 copy-start.14
  18.6 148.6 %all-reduce.5.cloned.1.call-start = ((), (), s32[]{:S(2)}) async-start(), calls=%async_computation.5 | async-start | bytes 1048576 | tf_op jit(solution)/shard_map/psum | solution.py:115
  18.6 97.9 %collective-permute-start.2 = (bf16[256,1024]{1,0:T(8,128)(2,1)S(1)}, bf16[256,1024]{1,0:T(8,128)(2,1)S(1)}, u32[]{:S(2)}, u32[]{:S(2)}) collective-permute-start(bf16[256,1024]{1,0:T(8,128)(2,1)S(1)} %bitcast.263), channel_id=1, source_target_pairs={{0,128},{128,0},{1,129},{129,1},{2,130},{130,2},{3,131},{131,3},{4... | collective-permute-start | bytes 1572872 | tf_op jit(solution)/shard_map/ppermute | solution.py:188
  116.6 51.8 %copy-start.8 = (bf16[256,1024]{1,0:T(8,128)(2,1)}, bf16[256,1024]{1,0:T(8,128)(2,1)S(1)}, u32[]{:S(2)}) copy-start(bf16[256,1024]{1,0:T(8,128)(2,1)S(1)} %collective-permute-done.2) | copy-start | bytes 1572868
  171.5 13.0 %copy-start.17 = (bf16[1,1,352,1024]{3,2,1,0:T(8,128)(2,1)S(1)}, bf16[1,1,352,1024]{3,2,1,0:T(8,128)(2,1)}, u32[]{:S(2)}) copy-start(bf16[1,1,352,1024]{3,2,1,0:T(8,128)(2,1)} %param.25) | copy-start | bytes 2162692
  171.5 44.8 %all-to-all-start = ((bf16[32,1,20,1024]{3,2,1,0:T(8,128)(2,1)}), bf16[32,1,20,1024]{3,2,1,0:T(8,128)(2,1)S(1)}, u32[]{:S(2)}, u32[]{:S(2)}) async-start(bf16[32,1,20,1024]{3,2,1,0:T(8,128)(2,1)} %bitcast.29), calls=%async_computation | async-start | bytes 3145728 | tf_op jit(solution)/shard_map/all_to_all | solution.py:139
  181.2 6.4 %collective-permute-start.5 = (bf16[1,1024,2,352]{1,3,2,0:T(8,128)(2,1)}, bf16[1,1024,2,352]{1,3,2,0:T(8,128)(2,1)}, u32[]{:S(2)}, u32[]{:S(2)}) collective-permute-start(bf16[1,1024,2,352]{1,3,2,0:T(8,128)(2,1)} %bitcast.285), channel_id=1, source_target_pairs={{0,128},{128,0},{1,129},{129,1},{2,130},{130,2},{3,131},{131,3},{4... | collective-permute-start | bytes 4325384 | tf_op jit(solution)/shard_map/ppermute | solution.py:188
  184.4 35.4 %collective-permute-start.4 = (bf16[1,352,1024]{2,1,0:T(8,128)(2,1)S(1)}, bf16[1,352,1024]{2,1,0:T(8,128)(2,1)}, u32[]{:S(2)}, u32[]{:S(2)}) collective-permute-start(bf16[1,352,1024]{2,1,0:T(8,128)(2,1)S(1)} %bitcast.286), channel_id=1, source_target_pairs={{0,128},{128,0},{1,129},{129,1},{2,130},{130,2},{3,131},{131,3},{4... | collective-permute-start | bytes 2162696 | tf_op jit(solution)/shard_map/ppermute | solution.py:188
  224.1 7.6 %copy-start.12 = (bf16[1,1024,16]{1,2,0:T(8,128)(2,1)S(1)}, bf16[1,1024,16]{1,2,0:T(8,128)(2,1)}, u32[]{:S(2)}) copy-start(bf16[1,1024,16]{1,2,0:T(8,128)(2,1)} %param.23) | copy-start | bytes 98308
  224.1 43.1 %all-to-all-start.1 = ((bf16[32,1,20,1024]{3,2,1,0:T(8,128)(2,1)}), bf16[32,1,20,1024]{3,2,1,0:T(8,128)(2,1)S(1)}, u32[]{:S(2)}, u32[]{:S(2)}) async-start(bf16[32,1,20,1024]{3,2,1,0:T(8,128)(2,1)} %copy.59), calls=%async_computation.1 | async-start | bytes 3145728 | tf_op jit(solution)/shard_map/all_to_all | solution.py:144
  231.6 85.4 %all-reduce.7.cloned.1.call-start = ((), (), s32[]{:S(2)}) async-start(), calls=%async_computation.6 | async-start | bytes 1048576 | tf_op jit(solution)/shard_map/psum | solution.py:159
  231.7 3.7 collective-permute-start.3
  268.7 48.3 %copy-start.3 = (f32[128,1024]{1,0:T(8,128)S(1)}, f32[128,1024]{1,0:T(8,128)}, u32[]{:S(2)}) copy-start(f32[128,1024]{1,0:T(8,128)} %all-reduce.5.cloned.1.call-done) | copy-start | bytes 1572868
  268.8 48.3 %copy-start.5 = (bf16[2,128,1024]{2,1,0:T(8,128)(2,1)S(1)}, bf16[2,128,1024]{2,1,0:T(8,128)(2,1)}, u32[]{:S(2)}) copy-start(bf16[2,128,1024]{2,1,0:T(8,128)(2,1)} %param.16) | copy-start | bytes 1572868
  268.9 49.3 %copy-start.11 = (bf16[1,1024,3,256]{1,3,2,0:T(8,128)(2,1)S(1)}, bf16[1,1024,3,256]{1,3,2,0:T(8,128)(2,1)}, u32[]{:S(2)}) copy-start(bf16[1,1024,3,256]{1,3,2,0:T(8,128)(2,1)} %copy-done.10) | copy-start | bytes 4718596
  269.9 134.2 %all-gather.5.cloned.1.call-start = ((), (), s32[]{:S(2)}) async-start(), calls=%async_computation.7 | async-start | bytes 4325376 | tf_op jit(solution)/shard_map/all_gather | solution.py:91
  319.8 152.0 %all-reduce.9.cloned.1.call-start = ((), (), s32[]{:S(2)}) async-start(), calls=%async_computation.8 | async-start | bytes 1048576 | tf_op jit(solution)/shard_map/psum | solution.py:115
  404.0 17.2 %copy-start.7 = (bf16[1,256,1024]{2,1,0:T(8,128)(2,1)S(1)}, bf16[1,256,1024]{2,1,0:T(8,128)(2,1)}, u32[]{:S(2)}) copy-start(bf16[1,256,1024]{2,1,0:T(8,128)(2,1)} %param.22) | copy-start | bytes 1572868
  404.0 17.2 %copy-start.9 = (bf16[256,1024]{1,0:T(8,128)(2,1)S(1)}, bf16[256,1024]{1,0:T(8,128)(2,1)}, u32[]{:S(2)}) copy-start(bf16[256,1024]{1,0:T(8,128)(2,1)} %copy-done.8) | copy-start | bytes 1572868
  474.8 45.7 %copy-start.16 = (bf16[1,1,1024,2,352]{2,4,3,1,0:T(8,128)(2,1)S(1)}, bf16[1,1,1024,2,352]{2,4,3,1,0:T(8,128)(2,1)}, u32[]{:S(2)}) copy-start(bf16[1,1,1024,2,352]{2,4,3,1,0:T(8,128)(2,1)} %param.24) | copy-start | bytes 4325380
  520.5 1.8 copy-start.18
  525.3 38.2 %all-to-all-start.3 = ((bf16[32,1,20,1024]{3,2,1,0:T(8,128)(2,1)}), bf16[32,1,20,1024]{3,2,1,0:T(8,128)(2,1)S(1)}, u32[]{:S(2)}, u32[]{:S(2)}) async-start(bf16[32,1,20,1024]{3,2,1,0:T(8,128)(2,1)} %copy.64), calls=%async_computation.3 | async-start | bytes 3145728 | tf_op jit(solution)/shard_map/all_to_all | solution.py:144
  531.4 85.8 %all-reduce.11.cloned.1.call-start = ((), (), s32[]{:S(2)}) async-start(), calls=%async_computation.9 | async-start | bytes 1048576 | tf_op jit(solution)/shard_map/psum | solution.py:159
  565.1 1.1 copy-start.15
  565.1 52.2 %copy-start.2 = (f32[128,1024]{1,0:T(8,128)S(1)}, f32[128,1024]{1,0:T(8,128)}, u32[]{:S(2)}) copy-start(f32[128,1024]{1,0:T(8,128)} %all-reduce.9.cloned.1.call-done) | copy-start | bytes 1572868
  568.6 53.5 %collective-permute-start.8 = (bf16[1,128,2,256]{1,3,2,0:T(8,128)(2,1)S(1)}, bf16[1,128,2,256]{1,3,2,0:T(8,128)(2,1)S(1)}, u32[]{:S(2)}, u32[]{:S(2)}) collective-permute-start(bf16[1,128,2,256]{1,3,2,0:T(8,128)(2,1)S(1)} %get-tuple-element.462), channel_id=1, source_target_pairs={{128,0},{129,1},{130,2},{131,3},{132,4},{133,5},{134,6},{135,7},{1... | collective-permute-start | bytes 393224 | tf_op jit(solution)/shard_map/ppermute | solution.py:204
  578.5 48.3 %collective-permute-start.6 = (bf16[128,1024]{1,0:T(8,128)(2,1)S(1)}, bf16[128,1024]{1,0:T(8,128)(2,1)S(1)}, u32[]{:S(2)}, u32[]{:S(2)}) collective-permute-start(bf16[128,1024]{1,0:T(8,128)(2,1)S(1)} %get-tuple-element.448), channel_id=1, source_target_pairs={{128,0},{129,1},{130,2},{131,3},{132,4},{133,5},{134,6},{135,7},{1... | collective-permute-start | bytes 786440 | tf_op jit(solution)/shard_map/ppermute | solution.py:203
  617.3 10.4 %copy-start.1 = (s32[2,4096]{1,0:T(2,128)S(1)}, s32[2,4096]{1,0:T(2,128)}, u32[]{:S(2)}) copy-start(s32[2,4096]{1,0:T(2,128)} %param.17) | copy-start | bytes 98308
  618.4 8.3 %collective-permute-start.7 = (bf16[128,1024]{1,0:T(8,128)(2,1)S(1)}, bf16[128,1024]{1,0:T(8,128)(2,1)S(1)}, u32[]{:S(2)}, u32[]{:S(2)}) collective-permute-start(bf16[128,1024]{1,0:T(8,128)(2,1)S(1)} %add_convert_fusion), channel_id=1, source_target_pairs={{0,128},{1,129},{2,130},{3,131},{4,132},{5,133},{6,134},{7,135},{8... | collective-permute-start | bytes 786440 | tf_op jit(solution)/shard_map/ppermute | solution.py:205
  620.8 5.0 collective-permute-start.9
Sparse Core Ops, SparseCore 0:
  18.7 80.6 all-gather.2
  117.8 49.3 all-reduce.4
  270.0 46.9 all-reduce.6
  319.9 84.0 all-gather.4
  422.4 49.3 all-reduce.8
  566.3 50.8 all-reduce.10

commit v2 on v1

--- a/solution.py
+++ b/solution.py
@@ -20,6 +20,19 @@
 
 def rms_scale(values, gains):
     return values * lax.rsqrt(jnp.mean(values * values, axis=-1, keepdims=True) + 1e-06) * gains
+
+
+def rep_sum(values):
+    count = lax.axis_size("rep")
+    total = values.astype(jnp.bfloat16)
+    stride = 1
+    while stride < count:
+        pairs = [(index, index ^ stride) for index in range(count)]
+        partner = lax.ppermute(total, "rep", pairs)
+        summed = total.astype(jnp.float32) + partner.astype(jnp.float32)
+        stride = stride * 2
+        total = summed.astype(jnp.bfloat16) if stride < count else summed
+    return total
 
 
 def attend(carry, queries, keys_vals, seg_query, pos_query, seg_key, pos_key):
@@ -112,7 +125,7 @@
         .astype(jnp.bfloat16)
     )
     attn_part = jnp.dot(context, w_out, preferred_element_type=jnp.float32)
-    mid = resid + lax.psum(attn_part, "rep")
+    mid = resid + rep_sum(attn_part)
     normed_mid = rms_scale(mid, gains[1]).astype(jnp.bfloat16)
     logits = jnp.dot(normed_mid, w_router, preferred_element_type=jnp.float32)
     expert_ids = jnp.arange(experts_all, dtype=jnp.int32)
@@ -156,7 +169,7 @@
     summed = summed.reshape(experts_all * CAP, width)
     gathered = jnp.take(summed, flat_slot, axis=0).reshape(TOP, tok_rows, width)
     expert_local = jnp.sum(gate_vals.T[:, :, None] * gathered, axis=0)
-    expert_total = lax.psum(expert_local, "rep")
+    expert_total = rep_sum(expert_local)
     layer_result = (mid + expert_total).astype(jnp.bfloat16)
     return layer_result, pages
 

time: 636 us -> 479 us (0.75)
  waiting for transfers between devices: 450 us -> 282 us
  starting transfers between devices: 47.2 us -> 71 us
  other arithmetic: 22 us -> 14.8 us
    psum x4 -> x0, waiting for transfers between devices: 183 us -> none  [the longest x2 98.6 us: one_layer(): mid = resid + lax.psum(attn_part, 'rep')]
    ppermute x0 -> x8, waiting for transfers between devices: none -> 35.5 us  [rep_sum(): partner = lax.ppermute(total, 'rep', pairs)]
    ppermute x0 -> x8, starting transfers between devices: none -> 12.3 us  [rep_sum(): partner = lax.ppermute(total, 'rep', pairs)]
    all_to_all x2, waiting for transfers between devices: 63.3 us -> 52.8 us  [one_layer(): lax.all_to_all(jnp.einsum('secf,efd->secd', hidden, w_down, preferred_ele...]
    all_to_all x1, waiting for transfers between devices: 28.6 us -> 18.2 us  [one_layer(): lax.all_to_all(copies, 'tok', split_axis=0, concat_axis=0, tiled=True)]
    ppermute x6, starting transfers between devices: 9.87 us -> 18.1 us  [per_device(): other = tuple((lax.ppermute(w, 'section', swap) for w in own))]
  transfers between devices with their start and end apart: 19 -> 23, of which waited for: 13 -> 16; matrix products, arithmetic and copies ran while one was open for 4% -> 6% of each run, Pallas kernels for 0% -> 0%
where the time goes in v2:
time: 479 us; the launch traced here: 478 us
  waiting for transfers between devices  282 us (59%)
  starting transfers between devices  71 us (15%)
  blocking collectives  39.8 us (8%)
  matrix products  29 us (6%)
  local copies, waits for them, and re-layouts  24.9 us (5%)
  between operations  15.4 us (3%)
  other arithmetic  14.8 us (3%)
    all_gather x2, waiting for transfers between devices, one_layer(): piece = lax.all_gather(keys_vals, 'tok', axis=0, tiled=True)  167 us
    all_to_all x2, waiting for transfers between devices, one_layer(): lax.all_to_all(jnp.einsum('secf,efd->secd', hidden, w_down, preferred_ele...  52.8 us
    all_to_all x1, blocking collectives, one_layer(): lax.all_to_all(copies, 'tok', split_axis=0, concat_axis=0, tiled=True)  39.8 us
    ppermute x8, waiting for transfers between devices, rep_sum(): partner = lax.ppermute(total, 'rep', pairs)  35.5 us
    all_to_all x1, waiting for transfers between devices, one_layer(): lax.all_to_all(copies, 'tok', split_axis=0, concat_axis=0, tiled=True)  18.2 us
    ppermute x6, starting transfers between devices, per_device(): other = tuple((lax.ppermute(w, 'section', swap) for w in own))  18.1 us
    ppermute x1, starting transfers between devices, per_device(): gotp0 = lax.ppermute(pages0, 'section', [(1, 0)])  14.8 us
    all_to_all x2, starting transfers between devices, one_layer(): lax.all_to_all(jnp.einsum('secf,efd->secd', hidden, w_down, preferred_ele...  14.5 us
  transfers between devices with their start and end apart: 23, of which 16 were waited for; matrix products, arithmetic and copies ran while one was open for 6% of the time, Pallas kernels for 0%

profile of v2, /device:TPU:1, one launch (start us, length us, event | category | flops | bytes accessed | tf_op | source)
XLA Modules:
  0.0 477.8 jit_solution(18435462429088255148)
XLA Ops:
  7.2 1.8 copy.55
  9.0 3.3 collective-permute-start.1
  12.6 2.9 collective-permute-done
  15.5 2.1 fusion.48
  19.7 79.7 %all-gather.3.cloned.1.call-done = bf16[4096,2,256]{0,2,1:T(8,128)(2,1)} async-done(((bf16[128,2,256]{0,2,1:T(8,128)(2,1)}), bf16[4096,2,256]{0,2,1:T(8,128)(2,1)}) %all-gather.3.cloned.1.call-update) | async-done | bytes 4194320 | tf_op jit(solution)/shard_map/all_gather | solution.py:104
  99.4 17.1 %while.36 = (s32[]{:T(128)}, f32[4,128]{1,0:T(4,128)S(1)}, f32[4,128]{1,0:T(4,128)S(1)}, f32[4,128,64]{1,2,0:T(8,128)S(1)}, s32[128]{0:T(128)S(1)}, /*index=5*/s...) while((s32[]{:T(128)}, f32[4,128]{1,0:T(4,128)S(1)}, ...), condition=%wide.region_4.5_spmd.clone, body=%wide.region_1.4_spmd.clone.sunk | while | flops 476548736 | bytes 10344167 | solution.py:118
  102.2 1.4 fusion.178
  106.5 1.4 fusion.178
  110.8 1.4 fusion.178
  115.1 1.4 fusion.178
  119.1 3.1 collective-permute-done.3
  122.3 2.8 collective-permute-start.4
  125.1 5.9 %collective-permute-done.4 = bf16[128,1024]{1,0:T(8,128)(2,1)S(1)} collective-permute-done((bf16[128,1024]{1,0:T(8,128)(2,1)S(1)}, bf16[128,1024]{1,0:T(8,128)(2,1)S(1)}, u32[]{:S(2)}, u32[]{:S(2)}) %collective-permute-start.4) | collective-permute-done | bytes 262176 | tf_op jit(solution)/shard_map/ppermute | solution.py:31
  132.2 1.4 broadcast_in_dim.165
  133.7 7.3 %all-to-all-start = ((bf16[32,1,20,1024]{3,2,1,0:T(8,128)(2,1)}), bf16[32,1,20,1024]{3,2,1,0:T(8,128)(2,1)S(1)}, u32[]{:S(2)}, u32[]{:S(2)}) async-start(bf16[32,1,20,1024]{3,2,1,0:T(8,128)(2,1)} %bitcast.29), calls=%async_computation | async-start | bytes 3145728 | tf_op jit(solution)/shard_map/all_to_all | solution.py:152
  141.0 8.2 %collective-permute-start.7 = (bf16[1,1024,2,352]{1,3,2,0:T(8,128)(2,1)}, bf16[1,1024,2,352]{1,3,2,0:T(8,128)(2,1)}, u32[]{:S(2)}, u32[]{:S(2)}) collective-permute-start(bf16[1,1024,2,352]{1,3,2,0:T(8,128)(2,1)} %bitcast.285), channel_id=1, source_target_pairs={{0,128},{128,0},{1,129},{129,1},{2,130},{130,2},{3,131},{131,3},{4... | collective-permute-start | bytes 4325384 | tf_op jit(solution)/shard_map/ppermute | solution.py:201
  149.4 2.9 collective-permute-done.7
  152.3 18.2 %all-to-all-done = bf16[32,1,20,1024]{3,2,1,0:T(8,128)(2,1)S(1)} async-done(((bf16[32,1,20,1024]{3,2,1,0:T(8,128)(2,1)}), bf16[32,1,20,1024]{3,2,1,0:T(8,128)(2,1)S(1)}, u32[]{:S(2)}, u32[]{:S(2)}) %all-to-all-start) | async-done | bytes 1310752 | tf_op jit(solution)/shard_map/all_to_all | solution.py:152
  170.5 3.6 convolution_bitcast_fusion.1
  174.1 2.1 fusion.42
  176.2 2.0 copy.59
  178.2 8.8 %all-to-all-start.1 = ((bf16[32,1,20,1024]{3,2,1,0:T(8,128)(2,1)}), bf16[32,1,20,1024]{3,2,1,0:T(8,128)(2,1)S(1)}, u32[]{:S(2)}, u32[]{:S(2)}) async-start(bf16[32,1,20,1024]{3,2,1,0:T(8,128)(2,1)} %copy.59), calls=%async_computation.1 | async-start | bytes 3145728 | tf_op jit(solution)/shard_map/all_to_all | solution.py:157
  187.0 6.2 %collective-permute-start.5 = (bf16[1024,16]{0,1:T(8,128)(2,1)S(1)}, bf16[1024,16]{0,1:T(8,128)(2,1)S(1)}, u32[]{:S(2)}, u32[]{:S(2)}) collective-permute-start(bf16[1024,16]{0,1:T(8,128)(2,1)S(1)} %bitcast.279), channel_id=1, source_target_pairs={{0,128},{128,0},{1,129},{129,1},{2,130},{130,2},{3,131},{131,3},{4... | collective-permute-start | bytes 98312 | tf_op jit(solution)/shard_map/ppermute | solution.py:201
  194.3 24.7 %all-to-all-done.1 = bf16[32,1,20,1024]{3,2,1,0:T(8,128)(2,1)S(1)} async-done(((bf16[32,1,20,1024]{3,2,1,0:T(8,128)(2,1)}), bf16[32,1,20,1024]{3,2,1,0:T(8,128)(2,1)S(1)}, u32[]{:S(2)}, u32[]{:S(2)}) %all-to-all-start.1) | async-done | bytes 1310752 | tf_op jit(solution)/shard_map/all_to_all | solution.py:157
  221.1 5.5 %collective-permute-done.8 = bf16[128,1024]{1,0:T(8,128)(2,1)S(1)} collective-permute-done((bf16[128,1024]{1,0:T(8,128)(2,1)S(1)}, bf16[128,1024]{1,0:T(8,128)(2,1)S(1)}, u32[]{:S(2)}, u32[]{:S(2)}) %collective-permute-start.8) | collective-permute-done | bytes 262176 | tf_op jit(solution)/shard_map/ppermute | solution.py:31
  226.7 3.1 collective-permute-start.9
  229.8 5.8 %collective-permute-done.9 = bf16[128,1024]{1,0:T(8,128)(2,1)S(1)} collective-permute-done((bf16[128,1024]{1,0:T(8,128)(2,1)S(1)}, bf16[128,1024]{1,0:T(8,128)(2,1)S(1)}, u32[]{:S(2)}, u32[]{:S(2)}) %collective-permute-start.9) | collective-permute-done | bytes 262176 | tf_op jit(solution)/shard_map/ppermute | solution.py:31
  237.5 87.2 %all-gather.5.cloned.1.call-done = bf16[4096,2,256]{0,2,1:T(8,128)(2,1)} async-done(((bf16[128,2,256]{0,2,1:T(8,128)(2,1)}), bf16[4096,2,256]{0,2,1:T(8,128)(2,1)}) %all-gather.5.cloned.1.call-update) | async-done | bytes 4194320 | tf_op jit(solution)/shard_map/all_gather | solution.py:104
  324.6 17.1 %while.37 = (s32[]{:T(128)}, f32[4,128]{1,0:T(4,128)S(1)}, f32[4,128]{1,0:T(4,128)S(1)}, f32[4,128,64]{1,2,0:T(8,128)S(1)}, s32[128]{0:T(128)S(1)}, /*index=5*/s...) while((s32[]{:T(128)}, f32[4,128]{1,0:T(4,128)S(1)}, ...), condition=%wide.region_19.21_spmd.clone, body=%wide.region_16.20_spmd.clone.sunk | while | flops 476548736 | bytes 10344167 | solution.py:118
  325.0 1.3 constant_dynamic-slice_fusion.10
  327.5 1.4 fusion.185
  331.8 1.4 fusion.185
  336.1 1.4 fusion.185
  340.4 1.4 fusion.185
  343.4 4.0 collective-permute-done.11
  347.5 3.0 collective-permute-start.12
  350.5 5.7 %collective-permute-done.12 = bf16[128,1024]{1,0:T(8,128)(2,1)S(1)} collective-permute-done((bf16[128,1024]{1,0:T(8,128)(2,1)S(1)}, bf16[128,1024]{1,0:T(8,128)(2,1)S(1)}, u32[]{:S(2)}, u32[]{:S(2)}) %collective-permute-start.12) | collective-permute-done | bytes 262176 | tf_op jit(solution)/shard_map/ppermute | solution.py:31
  357.6 39.8 %all_to_all.20 = bf16[32,1,20,1024]{3,2,1,0:T(8,128)(2,1)S(1)} all-to-all(bf16[32,1,20,1024]{3,2,1,0:T(8,128)(2,1)S(1)} %bitcast.258), channel_id=1, replica_groups=mesh['section'=2,'tok'=32,'rep'=4] {'tok'}, dimensions={0} | all-to-all | bytes 2621440 | tf_op jit(solution)/shard_map/all_to_all | solution.py:152
  397.4 1.8 convolution_bitcast_fusion
  400.2 2.0 copy.64
  402.2 5.8 %all-to-all-start.3 = ((bf16[32,1,20,1024]{3,2,1,0:T(8,128)(2,1)}), bf16[32,1,20,1024]{3,2,1,0:T(8,128)(2,1)S(1)}, u32[]{:S(2)}, u32[]{:S(2)}) async-start(bf16[32,1,20,1024]{3,2,1,0:T(8,128)(2,1)} %copy.64), calls=%async_computation.3 | async-start | bytes 3145728 | tf_op jit(solution)/shard_map/all_to_all | solution.py:157
  408.3 28.1 %all-to-all-done.3 = bf16[32,1,20,1024]{3,2,1,0:T(8,128)(2,1)S(1)} async-done(((bf16[32,1,20,1024]{3,2,1,0:T(8,128)(2,1)}), bf16[32,1,20,1024]{3,2,1,0:T(8,128)(2,1)S(1)}, u32[]{:S(2)}, u32[]{:S(2)}) %all-to-all-start.3) | async-done | bytes 1310752 | tf_op jit(solution)/shard_map/all_to_all | solution.py:157
  438.4 5.4 %collective-permute-done.13 = bf16[128,1024]{1,0:T(8,128)(2,1)S(1)} collective-permute-done((bf16[128,1024]{1,0:T(8,128)(2,1)S(1)}, bf16[128,1024]{1,0:T(8,128)(2,1)S(1)}, u32[]{:S(2)}, u32[]{:S(2)}) %collective-permute-start.13) | collective-permute-done | bytes 262176 | tf_op jit(solution)/shard_map/ppermute | solution.py:31
  446.8 14.8 %collective-permute-start.16 = (bf16[1,128,2,256]{1,3,2,0:T(8,128)(2,1)S(1)}, bf16[1,128,2,256]{1,3,2,0:T(8,128)(2,1)S(1)}, u32[]{:S(2)}, u32[]{:S(2)}) collective-permute-start(bf16[1,128,2,256]{1,3,2,0:T(8,128)(2,1)S(1)} %get-tuple-element.462), channel_id=1, source_target_pairs={{128,0},{129,1},{130,2},{131,3},{132,4},{133,5},{134,6},{135,7},{1... | collective-permute-start | bytes 393224 | tf_op jit(solution)/shard_map/ppermute | solution.py:217
  461.6 1.3 collective-permute-start.10
  463.2 1.3 collective-permute-start.15
  465.6 1.3 collective-permute-start.17
  466.9 2.3 collective-permute-done.17
  (234 shorter events, 44.2 us)
Async XLA Ops:
  7.2 11.6 %copy-start = (s32[2,4096]{1,0:T(2,128)S(1)}, s32[2,4096]{1,0:T(2,128)}, u32[]{:S(2)}) copy-start(s32[2,4096]{1,0:T(2,128)} %param.17) | copy-start | bytes 98308
  7.2 5.1 %copy-start.22 = (f32[1,2,1024]{2,1,0:T(2,128)S(1)}, f32[1,2,1024]{2,1,0:T(2,128)}, u32[]{:S(2)}) copy-start(f32[1,2,1024]{2,1,0:T(2,128)} %param.20) | copy-start | bytes 24580
  7.2 5.2 %copy-start.14 = (bf16[2,128,1024]{2,1,0:T(8,128)(2,1)S(1)}, bf16[2,128,1024]{2,1,0:T(8,128)(2,1)}, u32[]{:S(2)}) copy-start(bf16[2,128,1024]{2,1,0:T(8,128)(2,1)} %param.16) | copy-start | bytes 1572868
  7.2 92.2 %all-gather.3.cloned.1.call-start = ((), (), s32[]{:S(2)}) async-start(), calls=%async_computation.4 | async-start | bytes 4325376 | tf_op jit(solution)/shard_map/all_gather | solution.py:104
  9.0 8.7 %copy-start.16 = (bf16[1,1024,3,256]{1,3,2,0:T(8,128)(2,1)}, bf16[1,1024,3,256]{1,3,2,0:T(8,128)(2,1)S(1)}, u32[]{:S(2)}) copy-start(bf16[1,1024,3,256]{1,3,2,0:T(8,128)(2,1)S(1)} %copy.55) | copy-start | bytes 4718596
  9.0 6.5 %collective-permute-start.1 = (bf16[1024,768]{0,1:T(8,128)(2,1)S(1)}, bf16[1024,768]{0,1:T(8,128)(2,1)}, u32[]{:S(2)}, u32[]{:S(2)}) collective-permute-start(bf16[1024,768]{0,1:T(8,128)(2,1)S(1)} %bitcast.264), channel_id=1, source_target_pairs={{0,128},{128,0},{1,129},{129,1},{2,130},{130,2},{3,131},{131,3},{4... | collective-permute-start | bytes 4718600 | tf_op jit(solution)/shard_map/ppermute | solution.py:201
  12.3 3.2 collective-permute-start
  15.5 3.1 copy-start.10
  15.5 3.3 copy-start.23
  18.6 98.0 %collective-permute-start.2 = (bf16[256,1024]{1,0:T(8,128)(2,1)S(1)}, bf16[256,1024]{1,0:T(8,128)(2,1)S(1)}, u32[]{:S(2)}, u32[]{:S(2)}) collective-permute-start(bf16[256,1024]{1,0:T(8,128)(2,1)S(1)} %bitcast.263), channel_id=1, source_target_pairs={{0,128},{128,0},{1,129},{129,1},{2,130},{130,2},{3,131},{131,3},{4... | collective-permute-start | bytes 1572872 | tf_op jit(solution)/shard_map/ppermute | solution.py:201
  116.6 14.6 %copy-start.12 = (bf16[256,1024]{1,0:T(8,128)(2,1)}, bf16[256,1024]{1,0:T(8,128)(2,1)S(1)}, u32[]{:S(2)}) copy-start(bf16[256,1024]{1,0:T(8,128)(2,1)S(1)} %collective-permute-done.2) | copy-start | bytes 1572868
  116.9 5.3 %collective-permute-start.3 = (bf16[128,1024]{1,0:T(8,128)(2,1)S(1)}, bf16[128,1024]{1,0:T(8,128)(2,1)S(1)}, u32[]{:S(2)}, u32[]{:S(2)}) collective-permute-start(bf16[128,1024]{1,0:T(8,128)(2,1)S(1)} %convolution_convert_fusion.5), channel_id=1, source_target_pairs={{0,1},{1,0},{2,3},{3,2},{4,5},{5,4},{6,7},{7,6},{8,9},{9,8},{10,11... | collective-permute-start | bytes 786440 | tf_op jit(solution)/shard_map/ppermute | solution.py:31
  122.3 9.9 %copy-start.2 = (bf16[128,1024]{1,0:T(8,128)(2,1)}, bf16[128,1024]{1,0:T(8,128)(2,1)S(1)}, u32[]{:S(2)}) copy-start(bf16[128,1024]{1,0:T(8,128)(2,1)S(1)} %add_convert_fusion.5) | copy-start | bytes 786436
  122.3 8.7 %collective-permute-start.4 = (bf16[128,1024]{1,0:T(8,128)(2,1)S(1)}, bf16[128,1024]{1,0:T(8,128)(2,1)S(1)}, u32[]{:S(2)}, u32[]{:S(2)}) collective-permute-start(bf16[128,1024]{1,0:T(8,128)(2,1)S(1)} %add_convert_fusion.5), channel_id=1, source_target_pairs={{0,2},{1,3},{2,0},{3,1},{4,6},{5,7},{6,4},{7,5},{8,10},{9,11},{10,... | collective-permute-start | bytes 786440 | tf_op jit(solution)/shard_map/ppermute | solution.py:31
  125.1 6.3 %copy-start.18 = (s32[128,320]{0,1:T(8,128)}, s32[128,320]{0,1:T(8,128)S(1)}, u32[]{:S(2)}) copy-start(s32[128,320]{0,1:T(8,128)S(1)} %convert_reduce_fusion.2) | copy-start | bytes 491524
  133.7 15.5 %copy-start.26 = (bf16[1,1,352,1024]{3,2,1,0:T(8,128)(2,1)S(1)}, bf16[1,1,352,1024]{3,2,1,0:T(8,128)(2,1)}, u32[]{:S(2)}) copy-start(bf16[1,1,352,1024]{3,2,1,0:T(8,128)(2,1)} %param.25) | copy-start | bytes 2162692
  133.7 36.9 %all-to-all-start = ((bf16[32,1,20,1024]{3,2,1,0:T(8,128)(2,1)}), bf16[32,1,20,1024]{3,2,1,0:T(8,128)(2,1)S(1)}, u32[]{:S(2)}, u32[]{:S(2)}) async-start(bf16[32,1,20,1024]{3,2,1,0:T(8,128)(2,1)} %bitcast.29), calls=%async_computation | async-start | bytes 3145728 | tf_op jit(solution)/shard_map/all_to_all | solution.py:152
  141.0 11.4 %collective-permute-start.7 = (bf16[1,1024,2,352]{1,3,2,0:T(8,128)(2,1)}, bf16[1,1024,2,352]{1,3,2,0:T(8,128)(2,1)}, u32[]{:S(2)}, u32[]{:S(2)}) collective-permute-start(bf16[1,1024,2,352]{1,3,2,0:T(8,128)(2,1)} %bitcast.285), channel_id=1, source_target_pairs={{0,128},{128,0},{1,129},{129,1},{2,130},{130,2},{3,131},{131,3},{4... | collective-permute-start | bytes 4325384 | tf_op jit(solution)/shard_map/ppermute | solution.py:201
  149.1 25.0 %collective-permute-start.6 = (bf16[1,352,1024]{2,1,0:T(8,128)(2,1)S(1)}, bf16[1,352,1024]{2,1,0:T(8,128)(2,1)}, u32[]{:S(2)}, u32[]{:S(2)}) collective-permute-start(bf16[1,352,1024]{2,1,0:T(8,128)(2,1)S(1)} %bitcast.286), channel_id=1, source_target_pairs={{0,128},{128,0},{1,129},{129,1},{2,130},{130,2},{3,131},{131,3},{4... | collective-permute-start | bytes 2162696 | tf_op jit(solution)/shard_map/ppermute | solution.py:201
  178.2 8.8 %copy-start.21 = (bf16[1,1024,16]{1,2,0:T(8,128)(2,1)S(1)}, bf16[1,1024,16]{1,2,0:T(8,128)(2,1)}, u32[]{:S(2)}) copy-start(bf16[1,1024,16]{1,2,0:T(8,128)(2,1)} %param.23) | copy-start | bytes 98308
  178.2 40.9 %all-to-all-start.1 = ((bf16[32,1,20,1024]{3,2,1,0:T(8,128)(2,1)}), bf16[32,1,20,1024]{3,2,1,0:T(8,128)(2,1)S(1)}, u32[]{:S(2)}, u32[]{:S(2)}) async-start(bf16[32,1,20,1024]{3,2,1,0:T(8,128)(2,1)} %copy.59), calls=%async_computation.1 | async-start | bytes 3145728 | tf_op jit(solution)/shard_map/all_to_all | solution.py:157
  187.0 137.7 %all-gather.5.cloned.1.call-start = ((), (), s32[]{:S(2)}) async-start(), calls=%async_computation.5 | async-start | bytes 4325376 | tf_op jit(solution)/shard_map/all_gather | solution.py:104
  187.0 7.0 %collective-permute-start.5 = (bf16[1024,16]{0,1:T(8,128)(2,1)S(1)}, bf16[1024,16]{0,1:T(8,128)(2,1)S(1)}, u32[]{:S(2)}, u32[]{:S(2)}) collective-permute-start(bf16[1024,16]{0,1:T(8,128)(2,1)S(1)} %bitcast.279), channel_id=1, source_target_pairs={{0,128},{128,0},{1,129},{129,1},{2,130},{130,2},{3,131},{131,3},{4... | collective-permute-start | bytes 98312 | tf_op jit(solution)/shard_map/ppermute | solution.py:201
  220.7 14.9 %copy-start.3 = (bf16[128,1024]{1,0:T(8,128)(2,1)S(1)}, bf16[128,1024]{1,0:T(8,128)(2,1)}, u32[]{:S(2)}) copy-start(bf16[128,1024]{1,0:T(8,128)(2,1)} %copy-done.2) | copy-start | bytes 786436
  220.7 14.9 %copy-start.7 = (bf16[128,1024]{1,0:T(8,128)(2,1)S(1)}, bf16[128,1024]{1,0:T(8,128)(2,1)}, u32[]{:S(2)}) copy-start(bf16[128,1024]{1,0:T(8,128)(2,1)} %copy-done.6) | copy-start | bytes 786436
  220.7 14.8 %copy-start.15 = (bf16[2,128,1024]{2,1,0:T(8,128)(2,1)S(1)}, bf16[2,128,1024]{2,1,0:T(8,128)(2,1)}, u32[]{:S(2)}) copy-start(bf16[2,128,1024]{2,1,0:T(8,128)(2,1)} %param.16) | copy-start | bytes 1572868
  220.8 15.0 %copy-start.17 = (bf16[1,1024,3,256]{1,3,2,0:T(8,128)(2,1)S(1)}, bf16[1,1024,3,256]{1,3,2,0:T(8,128)(2,1)}, u32[]{:S(2)}) copy-start(bf16[1,1024,3,256]{1,3,2,0:T(8,128)(2,1)} %copy-done.16) | copy-start | bytes 4718596
  221.0 5.6 %collective-permute-start.8 = (bf16[128,1024]{1,0:T(8,128)(2,1)S(1)}, bf16[128,1024]{1,0:T(8,128)(2,1)S(1)}, u32[]{:S(2)}, u32[]{:S(2)}) collective-permute-start(bf16[128,1024]{1,0:T(8,128)(2,1)S(1)} %multiply_reduce_fusion.1), channel_id=1, source_target_pairs={{0,1},{1,0},{2,3},{3,2},{4,5},{5,4},{6,7},{7,6},{8,9},{9,8},{10,11... | collective-permute-start | bytes 786440 | tf_op jit(solution)/shard_map/ppermute | solution.py:31
  226.7 8.9 %collective-permute-start.9 = (bf16[128,1024]{1,0:T(8,128)(2,1)S(1)}, bf16[128,1024]{1,0:T(8,128)(2,1)S(1)}, u32[]{:S(2)}, u32[]{:S(2)}) collective-permute-start(bf16[128,1024]{1,0:T(8,128)(2,1)S(1)} %add_convert_fusion.4), channel_id=1, source_target_pairs={{0,2},{1,3},{2,0},{3,1},{4,6},{5,7},{6,4},{7,5},{8,10},{9,11},{10,... | collective-permute-start | bytes 786440 | tf_op jit(solution)/shard_map/ppermute | solution.py:31
  324.6 17.2 %copy-start.11 = (bf16[1,256,1024]{2,1,0:T(8,128)(2,1)S(1)}, bf16[1,256,1024]{2,1,0:T(8,128)(2,1)}, u32[]{:S(2)}) copy-start(bf16[1,256,1024]{2,1,0:T(8,128)(2,1)} %param.22) | copy-start | bytes 1572868
  324.6 17.2 %copy-start.13 = (bf16[256,1024]{1,0:T(8,128)(2,1)S(1)}, bf16[256,1024]{1,0:T(8,128)(2,1)}, u32[]{:S(2)}) copy-start(bf16[256,1024]{1,0:T(8,128)(2,1)} %copy-done.12) | copy-start | bytes 1572868
  341.8 15.1 %copy-start.19 = (s32[128,320]{0,1:T(8,128)S(1)}, s32[128,320]{0,1:T(8,128)}, u32[]{:S(2)}) copy-start(s32[128,320]{0,1:T(8,128)} %copy-done.18) | copy-start | bytes 491524
  342.1 5.3 %collective-permute-start.11 = (bf16[128,1024]{1,0:T(8,128)(2,1)S(1)}, bf16[128,1024]{1,0:T(8,128)(2,1)S(1)}, u32[]{:S(2)}, u32[]{:S(2)}) collective-permute-start(bf16[128,1024]{1,0:T(8,128)(2,1)S(1)} %convolution_convert_fusion.4), channel_id=1, source_target_pairs={{0,1},{1,0},{2,3},{3,2},{4,5},{5,4},{6,7},{7,6},{8,9},{9,8},{10,11... | collective-permute-start | bytes 786440 | tf_op jit(solution)/shard_map/ppermute | solution.py:31
  347.5 9.0 %copy-start.4 = (bf16[128,1024]{1,0:T(8,128)(2,1)}, bf16[128,1024]{1,0:T(8,128)(2,1)S(1)}, u32[]{:S(2)}) copy-start(bf16[128,1024]{1,0:T(8,128)(2,1)S(1)} %add_convert_fusion.2) | copy-start | bytes 786436
  347.5 8.7 %collective-permute-start.12 = (bf16[128,1024]{1,0:T(8,128)(2,1)S(1)}, bf16[128,1024]{1,0:T(8,128)(2,1)S(1)}, u32[]{:S(2)}, u32[]{:S(2)}) collective-permute-start(bf16[128,1024]{1,0:T(8,128)(2,1)S(1)} %add_convert_fusion.2), channel_id=1, source_target_pairs={{0,2},{1,3},{2,0},{3,1},{4,6},{5,7},{6,4},{7,5},{8,10},{9,11},{10,... | collective-permute-start | bytes 786440 | tf_op jit(solution)/shard_map/ppermute | solution.py:31
  357.6 39.8 %copy-start.25 = (bf16[1,1,1024,2,352]{2,4,3,1,0:T(8,128)(2,1)S(1)}, bf16[1,1,1024,2,352]{2,4,3,1,0:T(8,128)(2,1)}, u32[]{:S(2)}) copy-start(bf16[1,1,1024,2,352]{2,4,3,1,0:T(8,128)(2,1)} %param.24) | copy-start | bytes 4325380
  397.4 1.8 copy-start.27
  402.2 34.1 %all-to-all-start.3 = ((bf16[32,1,20,1024]{3,2,1,0:T(8,128)(2,1)}), bf16[32,1,20,1024]{3,2,1,0:T(8,128)(2,1)S(1)}, u32[]{:S(2)}, u32[]{:S(2)}) async-start(bf16[32,1,20,1024]{3,2,1,0:T(8,128)(2,1)} %copy.64), calls=%async_computation.3 | async-start | bytes 3145728 | tf_op jit(solution)/shard_map/all_to_all | solution.py:157
  437.9 6.6 %copy-start.24 = (s32[2,32]{1,0:T(2,128)S(1)}, s32[2,32]{1,0:T(2,128)}, u32[]{:S(2)}) copy-start(s32[2,32]{1,0:T(2,128)} %param.19) | copy-start | bytes 772
  437.9 25.0 %copy-start.5 = (bf16[128,1024]{1,0:T(8,128)(2,1)S(1)}, bf16[128,1024]{1,0:T(8,128)(2,1)}, u32[]{:S(2)}) copy-start(bf16[128,1024]{1,0:T(8,128)(2,1)} %copy-done.4) | copy-start | bytes 786436
  438.0 25.0 %copy-start.9 = (bf16[128,1024]{1,0:T(8,128)(2,1)S(1)}, bf16[128,1024]{1,0:T(8,128)(2,1)}, u32[]{:S(2)}) copy-start(bf16[128,1024]{1,0:T(8,128)(2,1)} %copy-done.8) | copy-start | bytes 786436
  438.2 5.6 %collective-permute-start.13 = (bf16[128,1024]{1,0:T(8,128)(2,1)S(1)}, bf16[128,1024]{1,0:T(8,128)(2,1)S(1)}, u32[]{:S(2)}, u32[]{:S(2)}) collective-permute-start(bf16[128,1024]{1,0:T(8,128)(2,1)S(1)} %multiply_reduce_fusion), channel_id=1, source_target_pairs={{0,1},{1,0},{2,3},{3,2},{4,5},{5,4},{6,7},{7,6},{8,9},{9,8},{10,11... | collective-permute-start | bytes 786440 | tf_op jit(solution)/shard_map/ppermute | solution.py:31
  443.9 19.0 %collective-permute-start.14 = (bf16[128,1024]{1,0:T(8,128)(2,1)S(1)}, bf16[128,1024]{1,0:T(8,128)(2,1)S(1)}, u32[]{:S(2)}, u32[]{:S(2)}) collective-permute-start(bf16[128,1024]{1,0:T(8,128)(2,1)S(1)} %add_convert_fusion.1), channel_id=1, source_target_pairs={{0,2},{1,3},{2,0},{3,1},{4,6},{5,7},{6,4},{7,5},{8,10},{9,11},{10,... | collective-permute-start | bytes 786440 | tf_op jit(solution)/shard_map/ppermute | solution.py:31
  446.8 20.1 %collective-permute-start.16 = (bf16[1,128,2,256]{1,3,2,0:T(8,128)(2,1)S(1)}, bf16[1,128,2,256]{1,3,2,0:T(8,128)(2,1)S(1)}, u32[]{:S(2)}, u32[]{:S(2)}) collective-permute-start(bf16[1,128,2,256]{1,3,2,0:T(8,128)(2,1)S(1)} %get-tuple-element.462), channel_id=1, source_target_pairs={{128,0},{129,1},{130,2},{131,3},{132,4},{133,5},{134,6},{135,7},{1... | collective-permute-start | bytes 393224 | tf_op jit(solution)/shard_map/ppermute | solution.py:217
  461.6 8.5 %collective-permute-start.10 = (bf16[128,1024]{1,0:T(8,128)(2,1)S(1)}, bf16[128,1024]{1,0:T(8,128)(2,1)S(1)}, u32[]{:S(2)}, u32[]{:S(2)}) collective-permute-start(bf16[128,1024]{1,0:T(8,128)(2,1)S(1)} %get-tuple-element.448), channel_id=1, source_target_pairs={{128,0},{129,1},{130,2},{131,3},{132,4},{133,5},{134,6},{135,7},{1... | collective-permute-start | bytes 786440 | tf_op jit(solution)/shard_map/ppermute | solution.py:216
  463.0 8.0 %copy-start.1 = (s32[2,4096]{1,0:T(2,128)S(1)}, s32[2,4096]{1,0:T(2,128)}, u32[]{:S(2)}) copy-start(s32[2,4096]{1,0:T(2,128)} %param.17) | copy-start | bytes 98308
  463.2 6.9 %collective-permute-start.15 = (bf16[128,1024]{1,0:T(8,128)(2,1)S(1)}, bf16[128,1024]{1,0:T(8,128)(2,1)S(1)}, u32[]{:S(2)}, u32[]{:S(2)}) collective-permute-start(bf16[128,1024]{1,0:T(8,128)(2,1)S(1)} %add_convert_fusion), channel_id=1, source_target_pairs={{0,128},{1,129},{2,130},{3,131},{4,132},{5,133},{6,134},{7,135},{8... | collective-permute-start | bytes 786440 | tf_op jit(solution)/shard_map/ppermute | solution.py:218
  465.6 3.6 collective-permute-start.17
  (3 other events, 2.4 us)
Sparse Core Ops, SparseCore 0:
  18.7 80.6 all-gather.2
  237.6 87.0 all-gather.4

commit v3 on v2

--- a/solution.py
+++ b/solution.py
@@ -33,6 +33,46 @@
         stride = stride * 2
         total = summed.astype(jnp.bfloat16) if stride < count else summed
     return total
+
+
+def ring_gather(block):
+    tok_count = lax.axis_size("tok")
+    inner = 4 if tok_count % 4 == 0 else 1
+    outer = tok_count // inner
+    tok_index = lax.axis_index("tok")
+    outer_at = tok_index // inner
+    inner_at = tok_index % inner
+
+    def moved(value, size, stride, steps):
+        pairs = []
+        for source in range(tok_count):
+            high, low = source // inner, source % inner
+            if stride == 1:
+                low = (low + steps) % size
+            else:
+                high = (high + steps) % size
+            pairs.append((source, high * inner + low))
+        return lax.ppermute(value, "tok", pairs)
+
+    def ring(value, size, stride):
+        ahead = [value]
+        behind = []
+        fwd = value
+        back = value
+        for step in range(size // 2):
+            fwd = moved(fwd, size, stride, -1)
+            ahead.append(fwd)
+            if len(ahead) + len(behind) == size:
+                break
+            back = moved(back, size, stride, 1)
+            behind.append(back)
+        return jnp.stack(ahead + behind[::-1])
+
+    group = ring(block, inner, 1) if inner > 1 else block[None]
+    every = ring(group, outer, inner).reshape((tok_count,) + block.shape)
+    ids = jnp.arange(tok_count, dtype=jnp.int32)
+    rel = ((ids // inner - outer_at) % outer) * inner + (ids % inner - inner_at) % inner
+    return jnp.take(every, rel, axis=0).reshape((tok_count * block.shape[0],) + block.shape[1:])
 
 
 def attend(carry, queries, keys_vals, seg_query, pos_query, seg_key, pos_key):
@@ -101,7 +141,7 @@
         jnp.zeros((head_count, tok_rows, HEAD_DIM), jnp.float32),
     )
     empty_pages = jnp.zeros((blocks_dev, PAGE, 2, col_width), jnp.bfloat16)
-    piece = lax.all_gather(keys_vals, "tok", axis=0, tiled=True)
+    piece = ring_gather(keys_vals)
     rows_key = piece.shape[0]
     step_rows = 1024
     while rows_key % step_rows != 0:

time: 479 us -> 565 us (1.18); the launches traced: 478 us -> 555 us
  local copies, waits for them, and re-layouts: 24.9 us -> 122 us
  waiting for transfers between devices: 282 us -> 213 us
  starting transfers between devices: 71 us -> 108 us
  matrix products: 29 us -> 48 us
  other arithmetic: 14.8 us -> 28.4 us
  between operations: 15.4 us -> 2.58 us
  blocking collectives: 39.8 us -> 32.8 us
    all_gather x2 -> x0, waiting for transfers between devices: 167 us -> none  [one_layer(): piece = lax.all_gather(keys_vals, 'tok', axis=0, tiled=True)]
    ppermute x0 -> x20, waiting for transfers between devices: none -> 90.6 us  [moved(): return lax.ppermute(value, 'tok', pairs)]
    while x8 -> x24, local copies, waits for them, and re-layouts: 0.02 us -> 36.6 us
    ppermute x0 -> x20, starting transfers between devices: none -> 33.4 us  [moved(): return lax.ppermute(value, 'tok', pairs)]
    select_n x0 -> x2, local copies, waits for them, and re-layouts: none -> 22.4 us  [ring_gather(): jnp.take(every, rel, axis=0)]
    slice x8, local copies, waits for them, and re-layouts: 10.2 us -> 26.2 us  [attend(): keys_vals[:, 1].reshape(rows_key, heads_here, head_size).astype(jnp.float32)]
    gather x0 -> x2, local copies, waits for them, and re-layouts: none -> 10.7 us  [ring_gather(): jnp.take(every, rel, axis=0)]
    unnamed x58 -> x93, local copies, waits for them, and re-layouts: 3.43 us -> 13.1 us
  transfers between devices with their start and end apart: 23 -> 41, of which waited for: 16 -> 30; matrix products, arithmetic and copies ran while one was open for 6% -> 17% of each run, Pallas kernels for 0% -> 0%
where the time goes in v3:
time: 565 us; the launch traced here: 555 us
  waiting for transfers between devices  213 us (38%)
  local copies, waits for them, and re-layouts  122 us (22%)
  starting transfers between devices  108 us (19%)
  matrix products  48 us (8%)
  blocking collectives  32.8 us (6%)
  other arithmetic  28.4 us (5%)
    ppermute x20, waiting for transfers between devices, moved(): return lax.ppermute(value, 'tok', pairs)  90.6 us
    all_to_all x2, waiting for transfers between devices, one_layer(): lax.all_to_all(jnp.einsum('secf,efd->secd', hidden, w_down, preferred_ele...  53.2 us
    while x24, local copies, waits for them, and re-layouts  36.6 us
    ppermute x20, starting transfers between devices, moved(): return lax.ppermute(value, 'tok', pairs)  33.4 us
    ppermute x8, waiting for transfers between devices, rep_sum(): partner = lax.ppermute(total, 'rep', pairs)  33.2 us
    all_to_all x1, blocking collectives, one_layer(): lax.all_to_all(copies, 'tok', split_axis=0, concat_axis=0, tiled=True)  32.8 us
    all_to_all x1, waiting for transfers between devices, one_layer(): lax.all_to_all(copies, 'tok', split_axis=0, concat_axis=0, tiled=True)  27.3 us
    slice x8, local copies, waits for them, and re-layouts, attend(): keys_vals[:, 1].reshape(rows_key, heads_here, head_size).astype(jnp.float32)  26.2 us
  transfers between devices with their start and end apart: 41, of which 30 were waited for; matrix products, arithmetic and copies ran while one was open for 17% of the time, Pallas kernels for 0%

profile of v3, /device:TPU:1, one launch (start us, length us, event | category | flops | bytes accessed | tf_op | source)
XLA Modules:
  0.0 555.1 jit_solution(2989679009534251062)
XLA Ops:
  2.5 3.3 collective-permute-start.1
  13.4 3.5 collective-permute-done.2
  22.2 5.1 collective-permute-start.5
  27.3 10.3 %collective-permute-done.5 = bf16[4,128,2,256]{1,3,2,0:T(8,128)(2,1)S(1)} collective-permute-done((bf16[4,128,2,256]{1,3,2,0:T(8,128)(2,1)S(1)}, bf16[4,128,2,256]{1,3,2,0:T(8,128)(2,1)S(1)}, u32[]{:S(2)}, u32[]{:S(2)}) %collective-permute-start.5) | collective-permute-done | bytes 524320 | tf_op jit(solution)/shard_map/ppermute | solution.py:55
  37.6 3.4 collective-permute-start.6
  43.1 7.3 %collective-permute-done.6 = bf16[4,128,2,256]{1,3,2,0:T(8,128)(2,1)S(1)} collective-permute-done((bf16[4,128,2,256]{1,3,2,0:T(8,128)(2,1)S(1)}, bf16[4,128,2,256]{1,3,2,0:T(8,128)(2,1)S(1)}, u32[]{:S(2)}, u32[]{:S(2)}) %collective-permute-start.6) | collective-permute-done | bytes 524320 | tf_op jit(solution)/shard_map/ppermute | solution.py:55
  50.5 3.4 collective-permute-start.7
  54.5 3.3 collective-permute-done.9
  58.8 3.7 collective-permute-done.7
  62.5 3.4 collective-permute-start.8
  66.7 4.9 collective-permute-done.10
  74.6 10.4 %collective-permute-done.11 = bf16[4,128,2,256]{1,3,2,0:T(8,128)(2,1)S(1)} collective-permute-done((bf16[4,128,2,256]{1,3,2,0:T(8,128)(2,1)S(1)}, bf16[4,128,2,256]{1,3,2,0:T(8,128)(2,1)S(1)}, u32[]{:S(2)}, u32[]{:S(2)}) %collective-permute-start.11) | collective-permute-done | bytes 524320 | tf_op jit(solution)/shard_map/ppermute | solution.py:55
  87.6 5.3 gather_fusion
  92.9 4.7 broadcast_select_fusion.1
  97.5 11.2 %copy.63 = bf16[32,128,2,256]{3,2,1,0:T(2,128)(2,1)} copy(bf16[32,128,2,256]{1,3,2,0:T(8,128)(2,1)} %broadcast_select_fusion.1) | data formatting | bytes 8388608 | tf_op jit(solution)/shard_map/jit(_take)/select_n | solution.py:75
  108.7 51.6 %while.36 = (s32[]{:T(128)}, f32[4,128]{1,0:T(4,128)S(1)}, f32[4,128]{1,0:T(4,128)S(1)}, f32[4,128,64]{1,2,0:T(8,128)S(1)}, s32[128]{0:T(128)S(1)}, /*index=5*/s...) while((s32[]{:T(128)}, f32[4,128]{1,0:T(4,128)S(1)}, ...), condition=%wide.region_4.6_spmd.clone, body=%wide.region_1.5_spmd.clone.sunk | while | flops 476548736 | bytes 12441311 | solution.py:158
  109.1 3.3 constant_dynamic-slice_fusion.9
  170.2 4.9 collective-permute-done.14
  177.7 6.3 %all-to-all-start = ((bf16[32,1,20,1024]{3,2,1,0:T(8,128)(2,1)}), bf16[32,1,20,1024]{3,2,1,0:T(8,128)(2,1)S(1)}, u32[]{:S(2)}, u32[]{:S(2)}) async-start(bf16[32,1,20,1024]{3,2,1,0:T(8,128)(2,1)} %bitcast.43), calls=%async_computation | async-start | bytes 3145728 | tf_op jit(solution)/shard_map/all_to_all | solution.py:192
  183.9 4.1 collective-permute-start.17
  191.2 27.3 %all-to-all-done = bf16[32,1,20,1024]{3,2,1,0:T(8,128)(2,1)S(1)} async-done(((bf16[32,1,20,1024]{3,2,1,0:T(8,128)(2,1)}), bf16[32,1,20,1024]{3,2,1,0:T(8,128)(2,1)S(1)}, u32[]{:S(2)}, u32[]{:S(2)}) %all-to-all-start) | async-done | bytes 1310752 | tf_op jit(solution)/shard_map/all_to_all | solution.py:192
  218.6 3.6 convolution_bitcast_fusion.1
  226.4 7.6 %all-to-all-start.1 = ((bf16[32,1,20,1024]{3,2,1,0:T(8,128)(2,1)}), bf16[32,1,20,1024]{3,2,1,0:T(8,128)(2,1)S(1)}, u32[]{:S(2)}, u32[]{:S(2)}) async-start(bf16[32,1,20,1024]{3,2,1,0:T(8,128)(2,1)} %copy.67), calls=%async_computation.1 | async-start | bytes 3145728 | tf_op jit(solution)/shard_map/all_to_all | solution.py:197
  238.3 30.9 %all-to-all-done.1 = bf16[32,1,20,1024]{3,2,1,0:T(8,128)(2,1)S(1)} async-done(((bf16[32,1,20,1024]{3,2,1,0:T(8,128)(2,1)}), bf16[32,1,20,1024]{3,2,1,0:T(8,128)(2,1)S(1)}, u32[]{:S(2)}, u32[]{:S(2)}) %all-to-all-start.1) | async-done | bytes 1310752 | tf_op jit(solution)/shard_map/all_to_all | solution.py:197
  271.2 5.2 collective-permute-done.18
  277.3 6.7 %collective-permute-done.19 = bf16[128,1024]{1,0:T(8,128)(2,1)S(1)} collective-permute-done((bf16[128,1024]{1,0:T(8,128)(2,1)S(1)}, bf16[128,1024]{1,0:T(8,128)(2,1)S(1)}, u32[]{:S(2)}, u32[]{:S(2)}) %collective-permute-start.19) | collective-permute-done | bytes 262176 | tf_op jit(solution)/shard_map/ppermute | solution.py:31
  295.9 9.1 %collective-permute-done.24 = bf16[4,128,2,256]{1,3,2,0:T(8,128)(2,1)S(1)} collective-permute-done((bf16[4,128,2,256]{1,3,2,0:T(8,128)(2,1)S(1)}, bf16[4,128,2,256]{1,3,2,0:T(8,128)(2,1)S(1)}, u32[]{:S(2)}, u32[]{:S(2)}) %collective-permute-start.24) | collective-permute-done | bytes 524320 | tf_op jit(solution)/shard_map/ppermute | solution.py:55
  306.9 10.7 %collective-permute-done.25 = bf16[4,128,2,256]{1,3,2,0:T(8,128)(2,1)S(1)} collective-permute-done((bf16[4,128,2,256]{1,3,2,0:T(8,128)(2,1)S(1)}, bf16[4,128,2,256]{1,3,2,0:T(8,128)(2,1)S(1)}, u32[]{:S(2)}, u32[]{:S(2)}) %collective-permute-start.25) | collective-permute-done | bytes 524320 | tf_op jit(solution)/shard_map/ppermute | solution.py:55
  317.6 3.4 collective-permute-start.26
  321.9 9.1 %collective-permute-done.26 = bf16[4,128,2,256]{1,3,2,0:T(8,128)(2,1)S(1)} collective-permute-done((bf16[4,128,2,256]{1,3,2,0:T(8,128)(2,1)S(1)}, bf16[4,128,2,256]{1,3,2,0:T(8,128)(2,1)S(1)}, u32[]{:S(2)}, u32[]{:S(2)}) %collective-permute-start.26) | collective-permute-done | bytes 524320 | tf_op jit(solution)/shard_map/ppermute | solution.py:55
  331.0 3.4 collective-permute-start.27
  336.9 6.6 %collective-permute-done.27 = bf16[4,128,2,256]{1,3,2,0:T(8,128)(2,1)S(1)} collective-permute-done((bf16[4,128,2,256]{1,3,2,0:T(8,128)(2,1)S(1)}, bf16[4,128,2,256]{1,3,2,0:T(8,128)(2,1)S(1)}, u32[]{:S(2)}, u32[]{:S(2)}) %collective-permute-start.27) | collective-permute-done | bytes 524320 | tf_op jit(solution)/shard_map/ppermute | solution.py:55
  344.4 4.0 collective-permute-done.30
  350.9 5.4 gather_fusion.2
  356.3 4.7 broadcast_select_fusion
  361.0 11.2 %copy.71 = bf16[32,128,2,256]{3,2,1,0:T(2,128)(2,1)} copy(bf16[32,128,2,256]{1,3,2,0:T(8,128)(2,1)} %broadcast_select_fusion) | data formatting | bytes 8388608 | tf_op jit(solution)/shard_map/jit(_take)/select_n | solution.py:75
  372.2 51.8 %while.37 = (s32[]{:T(128)}, f32[4,128]{1,0:T(4,128)S(1)}, f32[4,128]{1,0:T(4,128)S(1)}, f32[4,128,64]{1,2,0:T(8,128)S(1)}, s32[128]{0:T(128)S(1)}, /*index=5*/s...) while((s32[]{:T(128)}, f32[4,128]{1,0:T(4,128)S(1)}, ...), condition=%wide.region_19.22_spmd.clone, body=%wide.region_16.21_spmd.clone.sunk | while | flops 476548736 | bytes 12441311 | solution.py:158
  398.4 3.3 constant_dynamic-slice_fusion.10
  411.4 3.4 constant_dynamic-slice_fusion.10
  425.4 4.2 collective-permute-start.31
  429.6 3.8 collective-permute-done.31
  435.1 5.5 collective-permute-done.32
  441.6 32.8 %all_to_all.20 = bf16[32,1,20,1024]{3,2,1,0:T(8,128)(2,1)S(1)} all-to-all(bf16[32,1,20,1024]{3,2,1,0:T(8,128)(2,1)S(1)} %bitcast.306), channel_id=1, replica_groups=mesh['section'=2,'tok'=32,'rep'=4] {'tok'}, dimensions={0} | all-to-all | bytes 2621440 | tf_op jit(solution)/shard_map/all_to_all | solution.py:192
  479.1 5.3 all-to-all-start.3
  484.7 22.3 %all-to-all-done.3 = bf16[32,1,20,1024]{3,2,1,0:T(8,128)(2,1)S(1)} async-done(((bf16[32,1,20,1024]{3,2,1,0:T(8,128)(2,1)}), bf16[32,1,20,1024]{3,2,1,0:T(8,128)(2,1)S(1)}, u32[]{:S(2)}, u32[]{:S(2)}) %all-to-all-start.3) | async-done | bytes 1310752 | tf_op jit(solution)/shard_map/all_to_all | solution.py:197
  513.3 4.1 collective-permute-done.33
  517.4 5.7 %collective-permute-start.34 = (bf16[128,1024]{1,0:T(8,128)(2,1)S(1)}, bf16[128,1024]{1,0:T(8,128)(2,1)S(1)}, u32[]{:S(2)}, u32[]{:S(2)}) collective-permute-start(bf16[128,1024]{1,0:T(8,128)(2,1)S(1)} %add_convert_fusion.1), channel_id=1, source_target_pairs={{0,2},{1,3},{2,0},{3,1},{4,6},{5,7},{6,4},{7,5},{8,10},{9,11},{10,... | collective-permute-start | bytes 786440 | tf_op jit(solution)/shard_map/ppermute | solution.py:31
  525.4 19.8 %collective-permute-start.36 = (bf16[1,128,2,256]{3,2,1,0:T(2,128)(2,1)S(1)}, bf16[1,128,2,256]{3,2,1,0:T(2,128)(2,1)S(1)}, u32[]{:S(2)}, u32[]{:S(2)}) collective-permute-start(bf16[1,128,2,256]{3,2,1,0:T(2,128)(2,1)S(1)} %get-tuple-element.513), channel_id=1, source_target_pairs={{128,0},{129,1},{130,2},{131,3},{132,4},{133,5},{134,6},{135,7},{1... | collective-permute-start | bytes 393224 | tf_op jit(solution)/shard_map/ppermute | solution.py:257
  (333 shorter events, 191.2 us)
Async XLA Ops:
  0.6 42.5 %copy-start = (s32[2,4096]{1,0:T(2,128)S(1)}, s32[2,4096]{1,0:T(2,128)}, u32[]{:S(2)}) copy-start(s32[2,4096]{1,0:T(2,128)} %param.19) | copy-start | bytes 98308
  2.5 7.1 %collective-permute-start.1 = (bf16[1024,768]{0,1:T(8,128)(2,1)S(1)}, bf16[1024,768]{0,1:T(8,128)(2,1)}, u32[]{:S(2)}, u32[]{:S(2)}) collective-permute-start(bf16[1024,768]{0,1:T(8,128)(2,1)S(1)} %bitcast.311), channel_id=1, source_target_pairs={{0,128},{128,0},{1,129},{129,1},{2,130},{130,2},{3,131},{131,3},{4... | collective-permute-start | bytes 4718600 | tf_op jit(solution)/shard_map/ppermute | solution.py:241
  5.8 3.2 collective-permute-start
  9.5 44.4 %copy-start.35 = (s32[2,128,2]{1,2,0:T(2,128)S(1)}, s32[2,128,2]{1,2,0:T(2,128)}, u32[]{:S(2)}) copy-start(s32[2,128,2]{1,2,0:T(2,128)} %param.20) | copy-start | bytes 6148
  11.8 5.0 collective-permute-start.2
  12.9 6.1 %collective-permute-start.4 = (bf16[128,2,256]{0,2,1:T(8,128)(2,1)S(1)}, bf16[128,2,256]{0,2,1:T(8,128)(2,1)S(1)}, u32[]{:S(2)}, u32[]{:S(2)}) collective-permute-start(bf16[128,2,256]{0,2,1:T(8,128)(2,1)S(1)} %get-tuple-element.517), channel_id=1, source_target_pairs={{0,4},{4,8},{8,12},{12,0},{16,20},{20,24},{24,28},{28,16},{32,36},... | collective-permute-start | bytes 393224 | tf_op jit(solution)/shard_map/ppermute | solution.py:55
  16.9 5.2 collective-permute-start.3
  22.2 15.4 %collective-permute-start.5 = (bf16[4,128,2,256]{1,3,2,0:T(8,128)(2,1)S(1)}, bf16[4,128,2,256]{1,3,2,0:T(8,128)(2,1)S(1)}, u32[]{:S(2)}, u32[]{:S(2)}) collective-permute-start(bf16[4,128,2,256]{1,3,2,0:T(8,128)(2,1)S(1)} %pad_maximum_fusion), channel_id=1, source_target_pairs={{0,112},{4,116},{8,120},{12,124},{16,0},{20,4},{24,8},{28,12},{32,... | collective-permute-start | bytes 1572872 | tf_op jit(solution)/shard_map/ppermute | solution.py:55
  37.6 12.9 %collective-permute-start.6 = (bf16[4,128,2,256]{1,3,2,0:T(8,128)(2,1)S(1)}, bf16[4,128,2,256]{1,3,2,0:T(8,128)(2,1)S(1)}, u32[]{:S(2)}, u32[]{:S(2)}) collective-permute-start(bf16[4,128,2,256]{1,3,2,0:T(8,128)(2,1)S(1)} %collective-permute-done.5), channel_id=1, source_target_pairs={{0,112},{4,116},{8,120},{12,124},{16,0},{20,4},{24,8},{28,12},{32,... | collective-permute-start | bytes 1572872 | tf_op jit(solution)/shard_map/ppermute | solution.py:55
  41.0 119.4 %collective-permute-start.12 = (bf16[256,1024]{1,0:T(8,128)(2,1)}, bf16[256,1024]{1,0:T(8,128)(2,1)}, u32[]{:S(2)}, u32[]{:S(2)}) collective-permute-start(bf16[256,1024]{1,0:T(8,128)(2,1)} %bitcast.25), channel_id=1, source_target_pairs={{0,128},{128,0},{1,129},{129,1},{2,130},{130,2},{3,131},{131,3},{4... | collective-permute-start | bytes 1572872 | tf_op jit(solution)/shard_map/ppermute | solution.py:241
  43.1 14.7 %collective-permute-start.9 = (bf16[4,128,2,256]{1,3,2,0:T(8,128)(2,1)S(1)}, bf16[4,128,2,256]{1,3,2,0:T(8,128)(2,1)S(1)}, u32[]{:S(2)}, u32[]{:S(2)}) collective-permute-start(bf16[4,128,2,256]{1,3,2,0:T(8,128)(2,1)S(1)} %pad_maximum_fusion), channel_id=1, source_target_pairs={{0,16},{4,20},{8,24},{12,28},{16,32},{20,36},{24,40},{28,44},{32,4... | collective-permute-start | bytes 1572872 | tf_op jit(solution)/shard_map/ppermute | solution.py:55
  50.5 12.0 %collective-permute-start.7 = (bf16[4,128,2,256]{1,3,2,0:T(8,128)(2,1)S(1)}, bf16[4,128,2,256]{1,3,2,0:T(8,128)(2,1)S(1)}, u32[]{:S(2)}, u32[]{:S(2)}) collective-permute-start(bf16[4,128,2,256]{1,3,2,0:T(8,128)(2,1)S(1)} %collective-permute-done.6), channel_id=1, source_target_pairs={{0,112},{4,116},{8,120},{12,124},{16,0},{20,4},{24,8},{28,12},{32,... | collective-permute-start | bytes 1572872 | tf_op jit(solution)/shard_map/ppermute | solution.py:55
  53.9 39.0 %copy-start.32 = (pred[32]{0:T(512)(128)(4,1)}, pred[32]{0:T(512)(128)(4,1)S(1)}, u32[]{:S(2)}) copy-start(pred[32]{0:T(512)(128)(4,1)S(1)} %get-tuple-element.500) | copy-start | bytes 100
  54.5 109.5 %copy-start.26 = (s32[256]{0:T(256)}, s32[256]{0:T(256)S(1)}, u32[]{:S(2)}) copy-start(s32[256]{0:T(256)S(1)} %get-tuple-element.526) | copy-start | bytes 3076
  57.8 13.8 %collective-permute-start.10 = (bf16[4,128,2,256]{1,3,2,0:T(8,128)(2,1)S(1)}, bf16[4,128,2,256]{1,3,2,0:T(8,128)(2,1)S(1)}, u32[]{:S(2)}, u32[]{:S(2)}) collective-permute-start(bf16[4,128,2,256]{1,3,2,0:T(8,128)(2,1)S(1)} %collective-permute-done.9), channel_id=1, source_target_pairs={{0,16},{4,20},{8,24},{12,28},{16,32},{20,36},{24,40},{28,44},{32,4... | collective-permute-start | bytes 1572872 | tf_op jit(solution)/shard_map/ppermute | solution.py:55
  62.5 11.3 %collective-permute-start.8 = (bf16[4,128,2,256]{1,3,2,0:T(8,128)(2,1)S(1)}, bf16[4,128,2,256]{1,3,2,0:T(8,128)(2,1)S(1)}, u32[]{:S(2)}, u32[]{:S(2)}) collective-permute-start(bf16[4,128,2,256]{1,3,2,0:T(8,128)(2,1)S(1)} %collective-permute-done.7), channel_id=1, source_target_pairs={{0,112},{4,116},{8,120},{12,124},{16,0},{20,4},{24,8},{28,12},{32,... | collective-permute-start | bytes 1572872 | tf_op jit(solution)/shard_map/ppermute | solution.py:55
  71.6 13.4 %collective-permute-start.11 = (bf16[4,128,2,256]{1,3,2,0:T(8,128)(2,1)S(1)}, bf16[4,128,2,256]{1,3,2,0:T(8,128)(2,1)S(1)}, u32[]{:S(2)}, u32[]{:S(2)}) collective-permute-start(bf16[4,128,2,256]{1,3,2,0:T(8,128)(2,1)S(1)} %collective-permute-done.10), channel_id=1, source_target_pairs={{0,16},{4,20},{8,24},{12,28},{16,32},{20,36},{24,40},{28,44},{32,4... | collective-permute-start | bytes 1572872 | tf_op jit(solution)/shard_map/ppermute | solution.py:55
  161.9 5.3 collective-permute-start.13
  167.3 7.8 %collective-permute-start.14 = (bf16[128,1024]{1,0:T(8,128)(2,1)S(1)}, bf16[128,1024]{1,0:T(8,128)(2,1)S(1)}, u32[]{:S(2)}, u32[]{:S(2)}) collective-permute-start(bf16[128,1024]{1,0:T(8,128)(2,1)S(1)} %add_convert_fusion.5), channel_id=1, source_target_pairs={{0,2},{1,3},{2,0},{3,1},{4,6},{5,7},{6,4},{7,5},{8,10},{9,11},{10,... | collective-permute-start | bytes 786440 | tf_op jit(solution)/shard_map/ppermute | solution.py:31
  177.7 40.9 %all-to-all-start = ((bf16[32,1,20,1024]{3,2,1,0:T(8,128)(2,1)}), bf16[32,1,20,1024]{3,2,1,0:T(8,128)(2,1)S(1)}, u32[]{:S(2)}, u32[]{:S(2)}) async-start(bf16[32,1,20,1024]{3,2,1,0:T(8,128)(2,1)} %bitcast.43), calls=%async_computation | async-start | bytes 3145728 | tf_op jit(solution)/shard_map/all_to_all | solution.py:192
  183.9 7.3 %collective-permute-start.17 = (bf16[1,1024,2,352]{1,3,2,0:T(8,128)(2,1)}, bf16[1,1024,2,352]{1,3,2,0:T(8,128)(2,1)}, u32[]{:S(2)}, u32[]{:S(2)}) collective-permute-start(bf16[1,1024,2,352]{1,3,2,0:T(8,128)(2,1)} %bitcast.344), channel_id=1, source_target_pairs={{0,128},{128,0},{1,129},{129,1},{2,130},{130,2},{3,131},{131,3},{4... | collective-permute-start | bytes 4325384 | tf_op jit(solution)/shard_map/ppermute | solution.py:241
  188.0 34.1 %collective-permute-start.16 = (bf16[1,352,1024]{2,1,0:T(8,128)(2,1)S(1)}, bf16[1,352,1024]{2,1,0:T(8,128)(2,1)}, u32[]{:S(2)}, u32[]{:S(2)}) collective-permute-start(bf16[1,352,1024]{2,1,0:T(8,128)(2,1)S(1)} %bitcast.345), channel_id=1, source_target_pairs={{0,128},{128,0},{1,129},{129,1},{2,130},{130,2},{3,131},{131,3},{4... | collective-permute-start | bytes 2162696 | tf_op jit(solution)/shard_map/ppermute | solution.py:241
  226.4 42.8 %all-to-all-start.1 = ((bf16[32,1,20,1024]{3,2,1,0:T(8,128)(2,1)}), bf16[32,1,20,1024]{3,2,1,0:T(8,128)(2,1)S(1)}, u32[]{:S(2)}, u32[]{:S(2)}) async-start(bf16[32,1,20,1024]{3,2,1,0:T(8,128)(2,1)} %copy.67), calls=%async_computation.1 | async-start | bytes 3145728 | tf_op jit(solution)/shard_map/all_to_all | solution.py:197
  234.0 4.0 collective-permute-start.15
  237.2 33.6 %copy-start.30 = (pred[256]{0:T(512)(128)(4,1)}, pred[256]{0:T(512)(128)(4,1)S(1)}, u32[]{:S(2)}) copy-start(pred[256]{0:T(512)(128)(4,1)S(1)} %get-tuple-element.498) | copy-start | bytes 772
  271.1 5.3 collective-permute-start.18
  276.5 7.5 %collective-permute-start.19 = (bf16[128,1024]{1,0:T(8,128)(2,1)S(1)}, bf16[128,1024]{1,0:T(8,128)(2,1)S(1)}, u32[]{:S(2)}, u32[]{:S(2)}) collective-permute-start(bf16[128,1024]{1,0:T(8,128)(2,1)S(1)} %add_convert_fusion.4), channel_id=1, source_target_pairs={{0,2},{1,3},{2,0},{3,1},{4,6},{5,7},{6,4},{7,5},{8,10},{9,11},{10,... | collective-permute-start | bytes 786440 | tf_op jit(solution)/shard_map/ppermute | solution.py:31
  286.0 5.6 %collective-permute-start.21 = (bf16[128,2,256]{0,2,1:T(8,128)(2,1)S(1)}, bf16[128,2,256]{0,2,1:T(8,128)(2,1)S(1)}, u32[]{:S(2)}, u32[]{:S(2)}) collective-permute-start(bf16[128,2,256]{0,2,1:T(8,128)(2,1)S(1)} %get-tuple-element.515), channel_id=1, source_target_pairs={{0,12},{4,0},{8,4},{12,8},{16,28},{20,16},{24,20},{28,24},{32,44},... | collective-permute-start | bytes 393224 | tf_op jit(solution)/shard_map/ppermute | solution.py:55
  288.5 5.3 collective-permute-start.23
  291.6 4.1 collective-permute-start.22
  295.8 9.2 %collective-permute-start.24 = (bf16[4,128,2,256]{1,3,2,0:T(8,128)(2,1)S(1)}, bf16[4,128,2,256]{1,3,2,0:T(8,128)(2,1)S(1)}, u32[]{:S(2)}, u32[]{:S(2)}) collective-permute-start(bf16[4,128,2,256]{1,3,2,0:T(8,128)(2,1)S(1)} %pad_maximum_fusion.1), channel_id=1, source_target_pairs={{0,112},{4,116},{8,120},{12,124},{16,0},{20,4},{24,8},{28,12},{32,... | collective-permute-start | bytes 1572872 | tf_op jit(solution)/shard_map/ppermute | solution.py:55
  305.0 12.6 %collective-permute-start.25 = (bf16[4,128,2,256]{1,3,2,0:T(8,128)(2,1)S(1)}, bf16[4,128,2,256]{1,3,2,0:T(8,128)(2,1)S(1)}, u32[]{:S(2)}, u32[]{:S(2)}) collective-permute-start(bf16[4,128,2,256]{1,3,2,0:T(8,128)(2,1)S(1)} %collective-permute-done.24), channel_id=1, source_target_pairs={{0,112},{4,116},{8,120},{12,124},{16,0},{20,4},{24,8},{28,12},{32,... | collective-permute-start | bytes 1572872 | tf_op jit(solution)/shard_map/ppermute | solution.py:55
  306.7 14.3 %collective-permute-start.28 = (bf16[4,128,2,256]{1,3,2,0:T(8,128)(2,1)S(1)}, bf16[4,128,2,256]{1,3,2,0:T(8,128)(2,1)S(1)}, u32[]{:S(2)}, u32[]{:S(2)}) collective-permute-start(bf16[4,128,2,256]{1,3,2,0:T(8,128)(2,1)S(1)} %pad_maximum_fusion.1), channel_id=1, source_target_pairs={{0,16},{4,20},{8,24},{12,28},{16,32},{20,36},{24,40},{28,44},{32,4... | collective-permute-start | bytes 1572872 | tf_op jit(solution)/shard_map/ppermute | solution.py:55
  317.6 13.4 %collective-permute-start.26 = (bf16[4,128,2,256]{1,3,2,0:T(8,128)(2,1)S(1)}, bf16[4,128,2,256]{1,3,2,0:T(8,128)(2,1)S(1)}, u32[]{:S(2)}, u32[]{:S(2)}) collective-permute-start(bf16[4,128,2,256]{1,3,2,0:T(8,128)(2,1)S(1)} %collective-permute-done.25), channel_id=1, source_target_pairs={{0,112},{4,116},{8,120},{12,124},{16,0},{20,4},{24,8},{28,12},{32,... | collective-permute-start | bytes 1572872 | tf_op jit(solution)/shard_map/ppermute | solution.py:55
  321.0 14.3 %collective-permute-start.29 = (bf16[4,128,2,256]{1,3,2,0:T(8,128)(2,1)S(1)}, bf16[4,128,2,256]{1,3,2,0:T(8,128)(2,1)S(1)}, u32[]{:S(2)}, u32[]{:S(2)}) collective-permute-start(bf16[4,128,2,256]{1,3,2,0:T(8,128)(2,1)S(1)} %collective-permute-done.28), channel_id=1, source_target_pairs={{0,16},{4,20},{8,24},{12,28},{16,32},{20,36},{24,40},{28,44},{32,4... | collective-permute-start | bytes 1572872 | tf_op jit(solution)/shard_map/ppermute | solution.py:55
  331.0 12.6 %collective-permute-start.27 = (bf16[4,128,2,256]{1,3,2,0:T(8,128)(2,1)S(1)}, bf16[4,128,2,256]{1,3,2,0:T(8,128)(2,1)S(1)}, u32[]{:S(2)}, u32[]{:S(2)}) collective-permute-start(bf16[4,128,2,256]{1,3,2,0:T(8,128)(2,1)S(1)} %collective-permute-done.26), channel_id=1, source_target_pairs={{0,112},{4,116},{8,120},{12,124},{16,0},{20,4},{24,8},{28,12},{32,... | collective-permute-start | bytes 1572872 | tf_op jit(solution)/shard_map/ppermute | solution.py:55
  335.2 13.1 %collective-permute-start.30 = (bf16[4,128,2,256]{1,3,2,0:T(8,128)(2,1)S(1)}, bf16[4,128,2,256]{1,3,2,0:T(8,128)(2,1)S(1)}, u32[]{:S(2)}, u32[]{:S(2)}) collective-permute-start(bf16[4,128,2,256]{1,3,2,0:T(8,128)(2,1)S(1)} %collective-permute-done.29), channel_id=1, source_target_pairs={{0,16},{4,20},{8,24},{12,28},{16,32},{20,36},{24,40},{28,44},{32,4... | collective-permute-start | bytes 1572872 | tf_op jit(solution)/shard_map/ppermute | solution.py:55
  425.4 7.9 %collective-permute-start.31 = (bf16[128,1024]{1,0:T(8,128)(2,1)S(1)}, bf16[128,1024]{1,0:T(8,128)(2,1)S(1)}, u32[]{:S(2)}, u32[]{:S(2)}) collective-permute-start(bf16[128,1024]{1,0:T(8,128)(2,1)S(1)} %convolution_convert_fusion.4), channel_id=1, source_target_pairs={{0,1},{1,0},{2,3},{3,2},{4,5},{5,4},{6,7},{7,6},{8,9},{9,8},{10,11... | collective-permute-start | bytes 786440 | tf_op jit(solution)/shard_map/ppermute | solution.py:31
  433.5 7.1 %collective-permute-start.32 = (bf16[128,1024]{1,0:T(8,128)(2,1)S(1)}, bf16[128,1024]{1,0:T(8,128)(2,1)S(1)}, u32[]{:S(2)}, u32[]{:S(2)}) collective-permute-start(bf16[128,1024]{1,0:T(8,128)(2,1)S(1)} %add_convert_fusion.2), channel_id=1, source_target_pairs={{0,2},{1,3},{2,0},{3,1},{4,6},{5,7},{6,4},{7,5},{8,10},{9,11},{10,... | collective-permute-start | bytes 786440 | tf_op jit(solution)/shard_map/ppermute | solution.py:31
  441.6 32.8 %copy-start.37 = (bf16[1,1,1024,2,352]{2,4,3,1,0:T(8,128)(2,1)S(1)}, bf16[1,1,1024,2,352]{2,4,3,1,0:T(8,128)(2,1)}, u32[]{:S(2)}) copy-start(bf16[1,1,1024,2,352]{2,4,3,1,0:T(8,128)(2,1)} %param.26) | copy-start | bytes 4325380
  479.1 27.9 %all-to-all-start.3 = ((bf16[32,1,20,1024]{3,2,1,0:T(8,128)(2,1)}), bf16[32,1,20,1024]{3,2,1,0:T(8,128)(2,1)S(1)}, u32[]{:S(2)}, u32[]{:S(2)}) async-start(bf16[32,1,20,1024]{3,2,1,0:T(8,128)(2,1)} %copy.74), calls=%async_computation.3 | async-start | bytes 3145728 | tf_op jit(solution)/shard_map/all_to_all | solution.py:197
  511.3 35.3 %copy-start.7 = (bf16[128,1024]{1,0:T(8,128)(2,1)S(1)}, bf16[128,1024]{1,0:T(8,128)(2,1)}, u32[]{:S(2)}) copy-start(bf16[128,1024]{1,0:T(8,128)(2,1)} %copy-done.6) | copy-start | bytes 786436
  511.6 5.7 %collective-permute-start.33 = (bf16[128,1024]{1,0:T(8,128)(2,1)S(1)}, bf16[128,1024]{1,0:T(8,128)(2,1)S(1)}, u32[]{:S(2)}, u32[]{:S(2)}) collective-permute-start(bf16[128,1024]{1,0:T(8,128)(2,1)S(1)} %multiply_reduce_fusion), channel_id=1, source_target_pairs={{0,1},{1,0},{2,3},{3,2},{4,5},{5,4},{6,7},{7,6},{8,9},{9,8},{10,11... | collective-permute-start | bytes 786440 | tf_op jit(solution)/shard_map/ppermute | solution.py:31
  517.4 29.2 %collective-permute-start.34 = (bf16[128,1024]{1,0:T(8,128)(2,1)S(1)}, bf16[128,1024]{1,0:T(8,128)(2,1)S(1)}, u32[]{:S(2)}, u32[]{:S(2)}) collective-permute-start(bf16[128,1024]{1,0:T(8,128)(2,1)S(1)} %add_convert_fusion.1), channel_id=1, source_target_pairs={{0,2},{1,3},{2,0},{3,1},{4,6},{5,7},{6,4},{7,5},{8,10},{9,11},{10,... | collective-permute-start | bytes 786440 | tf_op jit(solution)/shard_map/ppermute | solution.py:31
  525.4 25.0 %collective-permute-start.36 = (bf16[1,128,2,256]{3,2,1,0:T(2,128)(2,1)S(1)}, bf16[1,128,2,256]{3,2,1,0:T(2,128)(2,1)S(1)}, u32[]{:S(2)}, u32[]{:S(2)}) collective-permute-start(bf16[1,128,2,256]{3,2,1,0:T(2,128)(2,1)S(1)} %get-tuple-element.513), channel_id=1, source_target_pairs={{128,0},{129,1},{130,2},{131,3},{132,4},{133,5},{134,6},{135,7},{1... | collective-permute-start | bytes 393224 | tf_op jit(solution)/shard_map/ppermute | solution.py:257
  545.2 8.5 %collective-permute-start.20 = (bf16[128,1024]{1,0:T(8,128)(2,1)S(1)}, bf16[128,1024]{1,0:T(8,128)(2,1)S(1)}, u32[]{:S(2)}, u32[]{:S(2)}) collective-permute-start(bf16[128,1024]{1,0:T(8,128)(2,1)S(1)} %copy-done.3), channel_id=1, source_target_pairs={{128,0},{129,1},{130,2},{131,3},{132,4},{133,5},{134,6},{135,7},{1... | collective-permute-start | bytes 786440 | tf_op jit(solution)/shard_map/ppermute | solution.py:256
  546.8 7.0 %collective-permute-start.35 = (bf16[128,1024]{1,0:T(8,128)(2,1)S(1)}, bf16[128,1024]{1,0:T(8,128)(2,1)S(1)}, u32[]{:S(2)}, u32[]{:S(2)}) collective-permute-start(bf16[128,1024]{1,0:T(8,128)(2,1)S(1)} %add_convert_fusion), channel_id=1, source_target_pairs={{0,128},{1,129},{2,130},{3,131},{4,132},{5,133},{6,134},{7,135},{8... | collective-permute-start | bytes 786440 | tf_op jit(solution)/shard_map/ppermute | solution.py:258
  549.2 3.3 collective-permute-start.37
  (33 other events, 390.9 us)

commit v4 on v2

--- a/solution.py
+++ b/solution.py
@@ -103,10 +103,12 @@
     empty_pages = jnp.zeros((blocks_dev, PAGE, 2, col_width), jnp.bfloat16)
     piece = lax.all_gather(keys_vals, "tok", axis=0, tiled=True)
     rows_key = piece.shape[0]
-    step_rows = 1024
+    step_rows = 512
     while rows_key % step_rows != 0:
         step_rows = step_rows // 2
-    turns = rows_key // step_rows
+    seg_start = jnp.sum((seg_all < seg_query[0]).astype(jnp.int32))
+    first_turn = seg_start // step_rows
+    last_turn = (tok_index * tok_rows + tok_rows - 1) // step_rows
 
     def key_block(index, soft_now):
         start = index * step_rows
@@ -115,7 +117,7 @@
         pos_key = start + jnp.arange(step_rows, dtype=jnp.int32)
         return attend(soft_now, queries, block, seg_query, pos_query, seg_key, pos_key)
 
-    soft_next = lax.fori_loop(0, turns, key_block, soft_init)
+    soft_next = lax.fori_loop(first_turn, last_turn + 1, key_block, soft_init)
     pages = place_pages(empty_pages, piece, table_row, tok_index)
     run_max, run_sum, run_acc = soft_next
     context = (

time: 479 us -> 479 us (level); the launches traced: 478 us -> 488 us
  blocking collectives: 39.8 us -> 56.2 us
  waiting for transfers between devices: 282 us -> 296 us
  matrix products: 29 us -> 16.7 us
  local copies, waits for them, and re-layouts: 24.9 us -> 18.1 us
  other arithmetic: 14.8 us -> 9.1 us
    all_to_all x1, blocking collectives: 39.8 us -> 56.2 us  [one_layer(): lax.all_to_all(copies, 'tok', split_axis=0, concat_axis=0, tiled=True)]
    all_to_all x2, waiting for transfers between devices: 52.8 us -> 65.7 us  [one_layer(): lax.all_to_all(jnp.einsum('secf,efd->secd', hidden, w_down, preferred_ele...]
    all_to_all x1, starting transfers between devices: 7.29 us -> 19.3 us  [one_layer(): lax.all_to_all(copies, 'tok', split_axis=0, concat_axis=0, tiled=True)]
    all_to_all x1, waiting for transfers between devices: 18.2 us -> 30.1 us  [one_layer(): lax.all_to_all(copies, 'tok', split_axis=0, concat_axis=0, tiled=True)]
    dot_general x8 -> x2, matrix products: 11.3 us -> 1.47 us  [attend(): jnp.einsum('htn,nhd->htd', weights, val_part, precision=lax.Precision.HIG...]
    ppermute x6, starting transfers between devices: 18.1 us -> 8.64 us  [per_device(): other = tuple((lax.ppermute(w, 'section', swap) for w in own))]
    all_gather x2, waiting for transfers between devices: 167 us -> 158 us  [one_layer(): piece = lax.all_gather(keys_vals, 'tok', axis=0, tiled=True)]
    slice x8 -> x2, local copies, waits for them, and re-layouts: 10.2 us -> 2.15 us  [attend(): keys_vals[:, 1].reshape(rows_key, heads_here, head_size).astype(jnp.float32)]
  transfers between devices with their start and end apart: 23 -> 23, of which waited for: 16 -> 16; matrix products, arithmetic and copies ran while one was open for 6% -> 3% of each run, Pallas kernels for 0% -> 0%
where the time goes in v4:
time: 479 us; the launch traced here: 488 us
  waiting for transfers between devices  296 us (62%)
  starting transfers between devices  73.4 us (15%)
  blocking collectives  56.2 us (12%)
  local copies, waits for them, and re-layouts  18.1 us (4%)
  between operations  17.9 us (4%)
  matrix products  16.7 us (3%)
  other arithmetic  9.1 us (2%)
    all_gather x2, waiting for transfers between devices, one_layer(): piece = lax.all_gather(keys_vals, 'tok', axis=0, tiled=True)  158 us
    all_to_all x2, waiting for transfers between devices, one_layer(): lax.all_to_all(jnp.einsum('secf,efd->secd', hidden, w_down, preferred_ele...  65.7 us
    all_to_all x1, blocking collectives, one_layer(): lax.all_to_all(copies, 'tok', split_axis=0, concat_axis=0, tiled=True)  56.2 us
    ppermute x8, waiting for transfers between devices, rep_sum(): partner = lax.ppermute(total, 'rep', pairs)  33.9 us
    all_to_all x1, waiting for transfers between devices, one_layer(): lax.all_to_all(copies, 'tok', split_axis=0, concat_axis=0, tiled=True)  30.1 us
    all_to_all x1, starting transfers between devices, one_layer(): lax.all_to_all(copies, 'tok', split_axis=0, concat_axis=0, tiled=True)  19.3 us
    ppermute x8, starting transfers between devices, rep_sum(): partner = lax.ppermute(total, 'rep', pairs)  16.2 us
    all_to_all x2, starting transfers between devices, one_layer(): lax.all_to_all(jnp.einsum('secf,efd->secd', hidden, w_down, preferred_ele...  13.7 us
  transfers between devices with their start and end apart: 23, of which 16 were waited for; matrix products, arithmetic and copies ran while one was open for 3% of the time, Pallas kernels for 0%

profile of v4, /device:TPU:1, one launch (start us, length us, event | category | flops | bytes accessed | tf_op | source)
XLA Modules:
  0.0 488.0 jit_solution(2580073702640197109)
XLA Ops:
  7.2 2.7 copy.55
  9.9 3.2 collective-permute-start.1
  13.3 3.1 collective-permute-done
  16.4 1.2 copy-done.19
  17.6 2.1 fusion.36
  24.5 77.1 %all-gather.3.cloned.1.call-done = bf16[4096,2,256]{0,2,1:T(8,128)(2,1)} async-done(((bf16[128,2,256]{0,2,1:T(8,128)(2,1)}), bf16[4096,2,256]{0,2,1:T(8,128)(2,1)}) %all-gather.3.cloned.1.call-update) | async-done | bytes 4194320 | tf_op jit(solution)/shard_map/all_gather | solution.py:104
  101.7 2.8 while.30
  102.0 1.1 constant_dynamic-slice_fusion.9
  104.8 1.3 collective-permute-start.3
  107.0 3.1 collective-permute-done.3
  110.2 2.8 collective-permute-start.4
  113.0 5.9 %collective-permute-done.4 = bf16[128,1024]{1,0:T(8,128)(2,1)S(1)} collective-permute-done((bf16[128,1024]{1,0:T(8,128)(2,1)S(1)}, bf16[128,1024]{1,0:T(8,128)(2,1)S(1)}, u32[]{:S(2)}, u32[]{:S(2)}) %collective-permute-start.4) | collective-permute-done | bytes 262176 | tf_op jit(solution)/shard_map/ppermute | solution.py:31
  120.1 1.4 broadcast_in_dim.71
  121.5 19.3 %all-to-all-start = ((bf16[32,1,20,1024]{3,2,1,0:T(8,128)(2,1)}), bf16[32,1,20,1024]{3,2,1,0:T(8,128)(2,1)S(1)}, u32[]{:S(2)}, u32[]{:S(2)}) async-start(bf16[32,1,20,1024]{3,2,1,0:T(8,128)(2,1)} %bitcast.30), calls=%async_computation | async-start | bytes 3145728 | tf_op jit(solution)/shard_map/all_to_all | solution.py:154
  140.8 2.5 collective-permute-start.7
  143.4 3.1 collective-permute-done.7
  146.5 30.1 %all-to-all-done = bf16[32,1,20,1024]{3,2,1,0:T(8,128)(2,1)S(1)} async-done(((bf16[32,1,20,1024]{3,2,1,0:T(8,128)(2,1)}), bf16[32,1,20,1024]{3,2,1,0:T(8,128)(2,1)S(1)}, u32[]{:S(2)}, u32[]{:S(2)}) %all-to-all-start) | async-done | bytes 1310752 | tf_op jit(solution)/shard_map/all_to_all | solution.py:154
  176.6 3.6 convolution_bitcast_fusion.1
  180.2 2.3 fusion.30
  182.5 2.0 copy.59
  184.5 7.4 %all-to-all-start.1 = ((bf16[32,1,20,1024]{3,2,1,0:T(8,128)(2,1)}), bf16[32,1,20,1024]{3,2,1,0:T(8,128)(2,1)S(1)}, u32[]{:S(2)}, u32[]{:S(2)}) async-start(bf16[32,1,20,1024]{3,2,1,0:T(8,128)(2,1)} %copy.59), calls=%async_computation.1 | async-start | bytes 3145728 | tf_op jit(solution)/shard_map/all_to_all | solution.py:159
  192.0 2.4 collective-permute-start.5
  195.5 32.3 %all-to-all-done.1 = bf16[32,1,20,1024]{3,2,1,0:T(8,128)(2,1)S(1)} async-done(((bf16[32,1,20,1024]{3,2,1,0:T(8,128)(2,1)}), bf16[32,1,20,1024]{3,2,1,0:T(8,128)(2,1)S(1)}, u32[]{:S(2)}, u32[]{:S(2)}) %all-to-all-start.1) | async-done | bytes 1310752 | tf_op jit(solution)/shard_map/all_to_all | solution.py:159
  229.7 1.2 collective-permute-start.8
  230.9 4.1 collective-permute-done.8
  235.1 2.7 collective-permute-start.9
  237.8 6.8 %collective-permute-done.9 = bf16[128,1024]{1,0:T(8,128)(2,1)S(1)} collective-permute-done((bf16[128,1024]{1,0:T(8,128)(2,1)S(1)}, bf16[128,1024]{1,0:T(8,128)(2,1)S(1)}, u32[]{:S(2)}, u32[]{:S(2)}) %collective-permute-start.9) | collective-permute-done | bytes 262176 | tf_op jit(solution)/shard_map/ppermute | solution.py:31
  244.9 2.1 fusion.39
  247.9 80.5 %all-gather.5.cloned.1.call-done = bf16[4096,2,256]{0,2,1:T(8,128)(2,1)} async-done(((bf16[128,2,256]{0,2,1:T(8,128)(2,1)}), bf16[4096,2,256]{0,2,1:T(8,128)(2,1)}) %all-gather.5.cloned.1.call-update) | async-done | bytes 4194320 | tf_op jit(solution)/shard_map/all_gather | solution.py:104
  328.4 2.8 while.31
  328.8 1.1 constant_dynamic-slice_fusion.10
  331.6 1.3 collective-permute-start.11
  332.8 4.0 collective-permute-done.11
  336.9 2.8 collective-permute-start.12
  339.7 6.0 %collective-permute-done.12 = bf16[128,1024]{1,0:T(8,128)(2,1)S(1)} collective-permute-done((bf16[128,1024]{1,0:T(8,128)(2,1)S(1)}, bf16[128,1024]{1,0:T(8,128)(2,1)S(1)}, u32[]{:S(2)}, u32[]{:S(2)}) %collective-permute-start.12) | collective-permute-done | bytes 262176 | tf_op jit(solution)/shard_map/ppermute | solution.py:31
  347.1 56.2 %all_to_all.20 = bf16[32,1,20,1024]{3,2,1,0:T(8,128)(2,1)S(1)} all-to-all(bf16[32,1,20,1024]{3,2,1,0:T(8,128)(2,1)S(1)} %bitcast.234), channel_id=1, replica_groups=mesh['section'=2,'tok'=32,'rep'=4] {'tok'}, dimensions={0} | all-to-all | bytes 2621440 | tf_op jit(solution)/shard_map/all_to_all | solution.py:154
  403.3 1.8 convolution_bitcast_fusion
  406.1 2.0 copy.64
  408.1 6.3 %all-to-all-start.3 = ((bf16[32,1,20,1024]{3,2,1,0:T(8,128)(2,1)}), bf16[32,1,20,1024]{3,2,1,0:T(8,128)(2,1)S(1)}, u32[]{:S(2)}, u32[]{:S(2)}) async-start(bf16[32,1,20,1024]{3,2,1,0:T(8,128)(2,1)} %copy.64), calls=%async_computation.3 | async-start | bytes 3145728 | tf_op jit(solution)/shard_map/all_to_all | solution.py:159
  414.6 33.4 %all-to-all-done.3 = bf16[32,1,20,1024]{3,2,1,0:T(8,128)(2,1)S(1)} async-done(((bf16[32,1,20,1024]{3,2,1,0:T(8,128)(2,1)}), bf16[32,1,20,1024]{3,2,1,0:T(8,128)(2,1)S(1)}, u32[]{:S(2)}, u32[]{:S(2)}) %all-to-all-start.3) | async-done | bytes 1310752 | tf_op jit(solution)/shard_map/all_to_all | solution.py:159
  449.9 1.3 collective-permute-start.13
  451.3 4.0 collective-permute-done.13
  455.3 2.8 collective-permute-start.14
  460.4 11.7 %collective-permute-start.16 = (bf16[1,128,2,256]{1,3,2,0:T(8,128)(2,1)S(1)}, bf16[1,128,2,256]{1,3,2,0:T(8,128)(2,1)S(1)}, u32[]{:S(2)}, u32[]{:S(2)}) collective-permute-start(bf16[1,128,2,256]{1,3,2,0:T(8,128)(2,1)S(1)} %get-tuple-element.248), channel_id=1, source_target_pairs={{128,0},{129,1},{130,2},{131,3},{132,4},{133,5},{134,6},{135,7},{1... | collective-permute-start | bytes 393224 | tf_op jit(solution)/shard_map/ppermute | solution.py:219
  472.1 1.3 collective-permute-start.10
  473.7 1.3 collective-permute-start.15
  476.0 1.3 collective-permute-start.17
  477.4 1.9 collective-permute-done.17
  (162 shorter events, 22.2 us)
Async XLA Ops:
  7.2 5.9 %copy-start.16 = (f32[1,2,1024]{2,1,0:T(2,128)S(1)}, f32[1,2,1024]{2,1,0:T(2,128)}, u32[]{:S(2)}) copy-start(f32[1,2,1024]{2,1,0:T(2,128)} %param.20) | copy-start | bytes 24580
  7.2 5.9 %copy-start.10 = (bf16[2,128,1024]{2,1,0:T(8,128)(2,1)S(1)}, bf16[2,128,1024]{2,1,0:T(8,128)(2,1)}, u32[]{:S(2)}) copy-start(bf16[2,128,1024]{2,1,0:T(8,128)(2,1)} %param.16) | copy-start | bytes 1572868
  7.2 94.5 %all-gather.3.cloned.1.call-start = ((), (), s32[]{:S(2)}) async-start(), calls=%async_computation.4 | async-start | bytes 4325376 | tf_op jit(solution)/shard_map/all_gather | solution.py:104
  9.9 6.5 %collective-permute-start.1 = (bf16[1024,768]{0,1:T(8,128)(2,1)}, bf16[1024,768]{0,1:T(8,128)(2,1)S(1)}, u32[]{:S(2)}, u32[]{:S(2)}) collective-permute-start(bf16[1024,768]{0,1:T(8,128)(2,1)} %bitcast.7), channel_id=1, source_target_pairs={{0,128},{128,0},{1,129},{129,1},{2,130},{130,2},{3,131},{131,3},{4... | collective-permute-start | bytes 4718600 | tf_op jit(solution)/shard_map/ppermute | solution.py:203
  13.1 3.3 collective-permute-start
  16.4 1.2 copy-start.19
  17.6 3.0 copy-start.6
  17.6 3.5 copy-start.15
  17.6 6.9 %copy-start.17 = (s32[2,128,2]{1,2,0:T(2,128)S(1)}, s32[2,128,2]{1,2,0:T(2,128)}, u32[]{:S(2)}) copy-start(s32[2,128,2]{1,2,0:T(2,128)} %param.18) | copy-start | bytes 6148
  20.6 83.9 %collective-permute-start.2 = (bf16[256,1024]{1,0:T(8,128)(2,1)S(1)}, bf16[256,1024]{1,0:T(8,128)(2,1)S(1)}, u32[]{:S(2)}, u32[]{:S(2)}) collective-permute-start(bf16[256,1024]{1,0:T(8,128)(2,1)S(1)} %bitcast.239), channel_id=1, source_target_pairs={{0,128},{128,0},{1,129},{129,1},{2,130},{130,2},{3,131},{131,3},{4... | collective-permute-start | bytes 1572872 | tf_op jit(solution)/shard_map/ppermute | solution.py:203
  104.5 14.6 %copy-start.8 = (bf16[256,1024]{1,0:T(8,128)(2,1)}, bf16[256,1024]{1,0:T(8,128)(2,1)S(1)}, u32[]{:S(2)}) copy-start(bf16[256,1024]{1,0:T(8,128)(2,1)S(1)} %collective-permute-done.2) | copy-start | bytes 1572868
  104.8 5.3 %collective-permute-start.3 = (bf16[128,1024]{1,0:T(8,128)(2,1)S(1)}, bf16[128,1024]{1,0:T(8,128)(2,1)S(1)}, u32[]{:S(2)}, u32[]{:S(2)}) collective-permute-start(bf16[128,1024]{1,0:T(8,128)(2,1)S(1)} %convolution_convert_fusion.5), channel_id=1, source_target_pairs={{0,1},{1,0},{2,3},{3,2},{4,5},{5,4},{6,7},{7,6},{8,9},{9,8},{10,11... | collective-permute-start | bytes 786440 | tf_op jit(solution)/shard_map/ppermute | solution.py:31
  110.2 8.8 %collective-permute-start.4 = (bf16[128,1024]{1,0:T(8,128)(2,1)S(1)}, bf16[128,1024]{1,0:T(8,128)(2,1)S(1)}, u32[]{:S(2)}, u32[]{:S(2)}) collective-permute-start(bf16[128,1024]{1,0:T(8,128)(2,1)S(1)} %add_convert_fusion.5), channel_id=1, source_target_pairs={{0,2},{1,3},{2,0},{3,1},{4,6},{5,7},{6,4},{7,5},{8,10},{9,11},{10,... | collective-permute-start | bytes 786440 | tf_op jit(solution)/shard_map/ppermute | solution.py:31
  113.0 7.1 %copy-start.12 = (s32[128,320]{0,1:T(8,128)}, s32[128,320]{0,1:T(8,128)S(1)}, u32[]{:S(2)}) copy-start(s32[128,320]{0,1:T(8,128)S(1)} %convert_reduce_fusion.2) | copy-start | bytes 491524
  118.9 0.7 copy-start.2
  121.5 21.8 %copy-start.22 = (bf16[1,1,352,1024]{3,2,1,0:T(8,128)(2,1)S(1)}, bf16[1,1,352,1024]{3,2,1,0:T(8,128)(2,1)}, u32[]{:S(2)}) copy-start(bf16[1,1,352,1024]{3,2,1,0:T(8,128)(2,1)} %param.25) | copy-start | bytes 2162692
  121.5 55.1 %all-to-all-start = ((bf16[32,1,20,1024]{3,2,1,0:T(8,128)(2,1)}), bf16[32,1,20,1024]{3,2,1,0:T(8,128)(2,1)S(1)}, u32[]{:S(2)}, u32[]{:S(2)}) async-start(bf16[32,1,20,1024]{3,2,1,0:T(8,128)(2,1)} %bitcast.30), calls=%async_computation | async-start | bytes 3145728 | tf_op jit(solution)/shard_map/all_to_all | solution.py:154
  140.8 5.7 %collective-permute-start.7 = (bf16[1,1024,2,352]{1,3,2,0:T(8,128)(2,1)}, bf16[1,1024,2,352]{1,3,2,0:T(8,128)(2,1)}, u32[]{:S(2)}, u32[]{:S(2)}) collective-permute-start(bf16[1,1024,2,352]{1,3,2,0:T(8,128)(2,1)} %bitcast.260), channel_id=1, source_target_pairs={{0,128},{128,0},{1,129},{129,1},{2,130},{130,2},{3,131},{131,3},{4... | collective-permute-start | bytes 4325384 | tf_op jit(solution)/shard_map/ppermute | solution.py:203
  143.3 36.9 %collective-permute-start.6 = (bf16[1,352,1024]{2,1,0:T(8,128)(2,1)S(1)}, bf16[1,352,1024]{2,1,0:T(8,128)(2,1)}, u32[]{:S(2)}, u32[]{:S(2)}) collective-permute-start(bf16[1,352,1024]{2,1,0:T(8,128)(2,1)S(1)} %bitcast.261), channel_id=1, source_target_pairs={{0,128},{128,0},{1,129},{129,1},{2,130},{130,2},{3,131},{131,3},{4... | collective-permute-start | bytes 2162696 | tf_op jit(solution)/shard_map/ppermute | solution.py:203
  184.5 7.5 %copy-start.14 = (bf16[1,1024,16]{1,2,0:T(8,128)(2,1)S(1)}, bf16[1,1024,16]{1,2,0:T(8,128)(2,1)}, u32[]{:S(2)}) copy-start(bf16[1,1024,16]{1,2,0:T(8,128)(2,1)} %param.23) | copy-start | bytes 98308
  184.5 43.3 %all-to-all-start.1 = ((bf16[32,1,20,1024]{3,2,1,0:T(8,128)(2,1)}), bf16[32,1,20,1024]{3,2,1,0:T(8,128)(2,1)S(1)}, u32[]{:S(2)}, u32[]{:S(2)}) async-start(bf16[32,1,20,1024]{3,2,1,0:T(8,128)(2,1)} %copy.59), calls=%async_computation.1 | async-start | bytes 3145728 | tf_op jit(solution)/shard_map/all_to_all | solution.py:159
  191.9 136.4 %all-gather.5.cloned.1.call-start = ((), (), s32[]{:S(2)}) async-start(), calls=%async_computation.5 | async-start | bytes 4325376 | tf_op jit(solution)/shard_map/all_gather | solution.py:104
  192.0 3.2 collective-permute-start.5
  229.5 15.0 %copy-start.3 = (bf16[128,1024]{1,0:T(8,128)(2,1)S(1)}, bf16[128,1024]{1,0:T(8,128)(2,1)}, u32[]{:S(2)}) copy-start(bf16[128,1024]{1,0:T(8,128)(2,1)} %copy-done.2) | copy-start | bytes 786436
  229.5 15.0 %copy-start.11 = (bf16[2,128,1024]{2,1,0:T(8,128)(2,1)S(1)}, bf16[2,128,1024]{2,1,0:T(8,128)(2,1)}, u32[]{:S(2)}) copy-start(bf16[2,128,1024]{2,1,0:T(8,128)(2,1)} %param.16) | copy-start | bytes 1572868
  229.5 15.4 %copy-start.20 = (bf16[1024,768]{0,1:T(8,128)(2,1)S(1)}, bf16[1024,768]{0,1:T(8,128)(2,1)}, u32[]{:S(2)}) copy-start(bf16[1024,768]{0,1:T(8,128)(2,1)} %copy-done.19) | copy-start | bytes 4718596
  229.7 5.3 %collective-permute-start.8 = (bf16[128,1024]{1,0:T(8,128)(2,1)S(1)}, bf16[128,1024]{1,0:T(8,128)(2,1)S(1)}, u32[]{:S(2)}, u32[]{:S(2)}) collective-permute-start(bf16[128,1024]{1,0:T(8,128)(2,1)S(1)} %multiply_reduce_fusion.1), channel_id=1, source_target_pairs={{0,1},{1,0},{2,3},{3,2},{4,5},{5,4},{6,7},{7,6},{8,9},{9,8},{10,11... | collective-permute-start | bytes 786440 | tf_op jit(solution)/shard_map/ppermute | solution.py:31
  235.1 9.5 %collective-permute-start.9 = (bf16[128,1024]{1,0:T(8,128)(2,1)S(1)}, bf16[128,1024]{1,0:T(8,128)(2,1)S(1)}, u32[]{:S(2)}, u32[]{:S(2)}) collective-permute-start(bf16[128,1024]{1,0:T(8,128)(2,1)S(1)} %add_convert_fusion.4), channel_id=1, source_target_pairs={{0,2},{1,3},{2,0},{3,1},{4,6},{5,7},{6,4},{7,5},{8,10},{9,11},{10,... | collective-permute-start | bytes 786440 | tf_op jit(solution)/shard_map/ppermute | solution.py:31
  328.4 2.9 copy-start.7
  328.4 2.8 copy-start.9
  331.5 14.9 %copy-start.13 = (s32[128,320]{0,1:T(8,128)S(1)}, s32[128,320]{0,1:T(8,128)}, u32[]{:S(2)}) copy-start(s32[128,320]{0,1:T(8,128)} %copy-done.12) | copy-start | bytes 491524
  331.6 5.3 %collective-permute-start.11 = (bf16[128,1024]{1,0:T(8,128)(2,1)S(1)}, bf16[128,1024]{1,0:T(8,128)(2,1)S(1)}, u32[]{:S(2)}, u32[]{:S(2)}) collective-permute-start(bf16[128,1024]{1,0:T(8,128)(2,1)S(1)} %convolution_convert_fusion.4), channel_id=1, source_target_pairs={{0,1},{1,0},{2,3},{3,2},{4,5},{5,4},{6,7},{7,6},{8,9},{9,8},{10,11... | collective-permute-start | bytes 786440 | tf_op jit(solution)/shard_map/ppermute | solution.py:31
  336.9 9.0 %copy-start = (bf16[128,1024]{1,0:T(8,128)(2,1)}, bf16[128,1024]{1,0:T(8,128)(2,1)S(1)}, u32[]{:S(2)}) copy-start(bf16[128,1024]{1,0:T(8,128)(2,1)S(1)} %add_convert_fusion.2) | copy-start | bytes 786436
  336.9 8.7 %collective-permute-start.12 = (bf16[128,1024]{1,0:T(8,128)(2,1)S(1)}, bf16[128,1024]{1,0:T(8,128)(2,1)S(1)}, u32[]{:S(2)}, u32[]{:S(2)}) collective-permute-start(bf16[128,1024]{1,0:T(8,128)(2,1)S(1)} %add_convert_fusion.2), channel_id=1, source_target_pairs={{0,2},{1,3},{2,0},{3,1},{4,6},{5,7},{6,4},{7,5},{8,10},{9,11},{10,... | collective-permute-start | bytes 786440 | tf_op jit(solution)/shard_map/ppermute | solution.py:31
  345.7 0.7 copy-start.4
  347.0 56.2 %copy-start.21 = (bf16[1,1,1024,2,352]{2,4,3,1,0:T(8,128)(2,1)S(1)}, bf16[1,1,1024,2,352]{2,4,3,1,0:T(8,128)(2,1)}, u32[]{:S(2)}) copy-start(bf16[1,1,1024,2,352]{2,4,3,1,0:T(8,128)(2,1)} %param.24) | copy-start | bytes 4325380
  403.3 1.8 copy-start.23
  408.1 40.0 %all-to-all-start.3 = ((bf16[32,1,20,1024]{3,2,1,0:T(8,128)(2,1)}), bf16[32,1,20,1024]{3,2,1,0:T(8,128)(2,1)S(1)}, u32[]{:S(2)}, u32[]{:S(2)}) async-start(bf16[32,1,20,1024]{3,2,1,0:T(8,128)(2,1)} %copy.64), calls=%async_computation.3 | async-start | bytes 3145728 | tf_op jit(solution)/shard_map/all_to_all | solution.py:159
  449.8 8.3 %copy-start.18 = (s32[2,32]{1,0:T(2,128)S(1)}, s32[2,32]{1,0:T(2,128)}, u32[]{:S(2)}) copy-start(s32[2,32]{1,0:T(2,128)} %param.19) | copy-start | bytes 772
  449.8 23.6 %copy-start.1 = (bf16[128,1024]{1,0:T(8,128)(2,1)S(1)}, bf16[128,1024]{1,0:T(8,128)(2,1)}, u32[]{:S(2)}) copy-start(bf16[128,1024]{1,0:T(8,128)(2,1)} %copy-done) | copy-start | bytes 786436
  449.8 23.6 %copy-start.5 = (bf16[128,1024]{1,0:T(8,128)(2,1)S(1)}, bf16[128,1024]{1,0:T(8,128)(2,1)}, u32[]{:S(2)}) copy-start(bf16[128,1024]{1,0:T(8,128)(2,1)} %copy-done.4) | copy-start | bytes 786436
  449.9 5.3 %collective-permute-start.13 = (bf16[128,1024]{1,0:T(8,128)(2,1)S(1)}, bf16[128,1024]{1,0:T(8,128)(2,1)S(1)}, u32[]{:S(2)}, u32[]{:S(2)}) collective-permute-start(bf16[128,1024]{1,0:T(8,128)(2,1)S(1)} %multiply_reduce_fusion), channel_id=1, source_target_pairs={{0,1},{1,0},{2,3},{3,2},{4,5},{5,4},{6,7},{7,6},{8,9},{9,8},{10,11... | collective-permute-start | bytes 786440 | tf_op jit(solution)/shard_map/ppermute | solution.py:31
  455.3 18.1 %collective-permute-start.14 = (bf16[128,1024]{1,0:T(8,128)(2,1)S(1)}, bf16[128,1024]{1,0:T(8,128)(2,1)S(1)}, u32[]{:S(2)}, u32[]{:S(2)}) collective-permute-start(bf16[128,1024]{1,0:T(8,128)(2,1)S(1)} %add_convert_fusion.1), channel_id=1, source_target_pairs={{0,2},{1,3},{2,0},{3,1},{4,6},{5,7},{6,4},{7,5},{8,10},{9,11},{10,... | collective-permute-start | bytes 786440 | tf_op jit(solution)/shard_map/ppermute | solution.py:31
  460.4 17.0 %collective-permute-start.16 = (bf16[1,128,2,256]{1,3,2,0:T(8,128)(2,1)S(1)}, bf16[1,128,2,256]{1,3,2,0:T(8,128)(2,1)S(1)}, u32[]{:S(2)}, u32[]{:S(2)}) collective-permute-start(bf16[1,128,2,256]{1,3,2,0:T(8,128)(2,1)S(1)} %get-tuple-element.248), channel_id=1, source_target_pairs={{128,0},{129,1},{130,2},{131,3},{132,4},{133,5},{134,6},{135,7},{1... | collective-permute-start | bytes 393224 | tf_op jit(solution)/shard_map/ppermute | solution.py:219
  472.1 8.1 %collective-permute-start.10 = (bf16[128,1024]{1,0:T(8,128)(2,1)S(1)}, bf16[128,1024]{1,0:T(8,128)(2,1)S(1)}, u32[]{:S(2)}, u32[]{:S(2)}) collective-permute-start(bf16[128,1024]{1,0:T(8,128)(2,1)S(1)} %get-tuple-element.234), channel_id=1, source_target_pairs={{128,0},{129,1},{130,2},{131,3},{132,4},{133,5},{134,6},{135,7},{1... | collective-permute-start | bytes 786440 | tf_op jit(solution)/shard_map/ppermute | solution.py:218
  473.7 6.6 %collective-permute-start.15 = (bf16[128,1024]{1,0:T(8,128)(2,1)S(1)}, bf16[128,1024]{1,0:T(8,128)(2,1)S(1)}, u32[]{:S(2)}, u32[]{:S(2)}) collective-permute-start(bf16[128,1024]{1,0:T(8,128)(2,1)S(1)} %add_convert_fusion), channel_id=1, source_target_pairs={{0,128},{1,129},{2,130},{3,131},{4,132},{5,133},{6,134},{7,135},{8... | collective-permute-start | bytes 786440 | tf_op jit(solution)/shard_map/ppermute | solution.py:220
  476.0 3.3 collective-permute-start.17
Sparse Core Ops, SparseCore 0:
  20.7 80.8 all-gather.2
  248.0 80.3 all-gather.4

commit v5 on v4

--- a/solution.py
+++ b/solution.py
@@ -1,7 +1,7 @@
 import jax
 import jax.numpy as jnp
 from jax import lax
-from jax.sharding import PartitionSpec as P
+from jax.sharding import Mesh, PartitionSpec as P
 
 HEAD_DIM = 64
 TOP = 2
@@ -20,6 +20,14 @@
 
 def rms_scale(values, gains):
     return values * lax.rsqrt(jnp.mean(values * values, axis=-1, keepdims=True) + 1e-06) * gains
+
+
+def tok_place():
+    return lax.axis_index("tz") * lax.axis_size("tp") + lax.axis_index("tp")
+
+
+def tok_size():
+    return lax.axis_size("tz") * lax.axis_size("tp")
 
 
 def rep_sum(values):
@@ -76,8 +84,8 @@
 def one_layer(
     layer_in, seg_all, table_row, pick_rows, gains, w_qkv, w_out, w_router, w_in, w_down
 ):
-    tok_index = lax.axis_index("tok")
-    tok_count = lax.axis_size("tok")
+    tok_index = tok_place()
+    tok_count = tok_size()
     tok_rows = layer_in.shape[0]
     width = layer_in.shape[1]
     col_width = w_qkv.shape[1] // 3
@@ -101,7 +109,7 @@
         jnp.zeros((head_count, tok_rows, HEAD_DIM), jnp.float32),
     )
     empty_pages = jnp.zeros((blocks_dev, PAGE, 2, col_width), jnp.bfloat16)
-    piece = lax.all_gather(keys_vals, "tok", axis=0, tiled=True)
+    piece = lax.all_gather(keys_vals, ("tz", "tp"), axis=0, tiled=True)
     rows_key = piece.shape[0]
     step_rows = 512
     while rows_key % step_rows != 0:
@@ -145,30 +153,20 @@
     dispatch = lax.dot_general(
         hits, normed_mid, (((0,), (0,)), ((), ())), preferred_element_type=jnp.float32
     ).astype(jnp.bfloat16)
-    copies = jnp.broadcast_to(
-        dispatch.reshape(experts_all, 1, CAP, width), (experts_all, split_count, CAP, width)
-    )
-    copies = copies.reshape(tok_count, local_pieces, CAP, width)
-    act = jnp.einsum(
-        "secd,edgf->secgf",
-        lax.all_to_all(copies, "tok", split_axis=0, concat_axis=0, tiled=True),
-        w_in,
-        preferred_element_type=jnp.float32,
-    )
-    hidden = (jax.nn.gelu(act[..., 0, :]) * act[..., 1, :]).astype(jnp.bfloat16)
-    returned = lax.all_to_all(
-        jnp.einsum("secf,efd->secd", hidden, w_down, preferred_element_type=jnp.float32).astype(
-            jnp.bfloat16
-        ),
-        "tok",
-        split_axis=0,
-        concat_axis=0,
-        tiled=True,
-    )
-    summed = jnp.sum(
-        returned.reshape(experts_all, split_count, CAP, width).astype(jnp.float32), axis=1
-    )
-    summed = summed.reshape(experts_all * CAP, width)
+    pair_swap = [(0, 1), (1, 0)]
+    own_rows = lax.all_to_all(
+        dispatch.reshape(experts_all, CAP, width), "tz", split_axis=0, concat_axis=0, tiled=True
+    )
+    pair_rows = lax.ppermute(own_rows, "tp", pair_swap)
+    rows_all = jnp.stack([own_rows, pair_rows]).reshape(-1, width)
+    act = jnp.einsum("rd,dgf->rgf", rows_all, w_in[0], preferred_element_type=jnp.float32)
+    hidden = (jax.nn.gelu(act[:, 0, :]) * act[:, 1, :]).astype(jnp.bfloat16)
+    share_out = jnp.dot(hidden, w_down[0], preferred_element_type=jnp.float32).astype(jnp.bfloat16)
+    share_out = share_out.reshape(2, experts_all, CAP, width)
+    pair_out = lax.ppermute(share_out[1], "tp", pair_swap)
+    halves = (share_out[0].astype(jnp.float32) + pair_out.astype(jnp.float32)).astype(jnp.bfloat16)
+    returned = lax.all_to_all(halves, "tz", split_axis=0, concat_axis=0, tiled=True)
+    summed = returned.astype(jnp.float32).reshape(experts_all * CAP, width)
     gathered = jnp.take(summed, flat_slot, axis=0).reshape(TOP, tok_rows, width)
     expert_local = jnp.sum(gate_vals.T[:, :, None] * gathered, axis=0)
     expert_total = rep_sum(expert_local)
@@ -225,21 +223,26 @@
 
 
 def solution(mesh):
+    sizes = mesh.shape
+    pair = 2
+    grid = mesh.devices.reshape(sizes["section"], sizes["tok"] // pair, pair, sizes["rep"])
+    split_mesh = Mesh(grid, ("section", "tz", "tp", "rep"))
+    tok = ("tz", "tp")
     return jax.shard_map(
         per_device,
-        mesh=mesh,
+        mesh=split_mesh,
         in_specs=(
-            P(None, "tok", None),
+            P(None, tok, None),
             P(),
-            P(None, "tok", None),
+            P(None, tok, None),
             P(),
             P("section", None, None),
             P("section", None, None, "rep"),
             P("section", "rep", None),
             P("section", None, None),
-            P("section", "tok", None, None, "rep"),
-            P("section", "tok", "rep", None),
+            P("section", tok, None, None, "rep"),
+            P("section", tok, "rep", None),
         ),
-        out_specs=(P("section", None, "tok", None), P("section", None, "tok", None, None, "rep")),
+        out_specs=(P("section", None, tok, None), P("section", None, tok, None, None, "rep")),
         check_vma=False,
     )

time: 479 us -> 467 us (0.975); the launches traced: 488 us -> 465 us
  waiting for transfers between devices: 296 us -> 255 us
  starting transfers between devices: 73.4 us -> 107 us
  blocking collectives: 56.2 us -> 31.4 us
  other arithmetic: 9.1 us -> 14 us
    all_to_all x3, waiting for transfers between devices: 95.8 us -> 30 us  [the longest x2 23.4 us: one_layer(): lax.all_to_all(halves, 'tz', split_axis=0, concat_axis=0, tiled=True)]
    ppermute x0 -> x4, waiting for transfers between devices: none -> 27 us  [the longest x2 17.2 us: one_layer(): pair_out = lax.ppermute(share_out[1], 'tp', pair_swap)]
    all_to_all x1, blocking collectives: 56.2 us -> 31.4 us  [one_layer(): lax.all_to_all(dispatch.reshape(experts_all, CAP, width), 'tz', split_axi...]
    ppermute x6, starting transfers between devices: 8.64 us -> 31.2 us  [per_device(): other = tuple((lax.ppermute(w, 'section', swap) for w in own))]
    ppermute x8, starting transfers between devices: 16.2 us -> 26.6 us  [rep_sum(): partner = lax.ppermute(total, 'rep', pairs)]
    all_to_all x3, starting transfers between devices: 33 us -> 26.3 us  [the longest x1 14.3 us: one_layer(): lax.all_to_all(dispatch.reshape(experts_all, CAP, width), 'tz', split_axi...]
    convert_element_type x0 -> x2, other arithmetic: none -> 4.86 us  [one_layer(): (share_out[0].astype(jnp.float32) + pair_out.astype(jnp.float32)).astype(...]
  transfers between devices with their start and end apart: 23 -> 27, of which waited for: 16 -> 18; matrix products, arithmetic and copies ran while one was open for 3% -> 4% of each run, Pallas kernels for 0% -> 0%
where the time goes in v5:
time: 467 us; the launch traced here: 465 us
  waiting for transfers between devices  255 us (55%)
  starting transfers between devices  107 us (23%)
  blocking collectives  31.4 us (7%)
  local copies, waits for them, and re-layouts  21.6 us (5%)
  between operations  18.1 us (4%)
  matrix products  17.3 us (4%)
  other arithmetic  14 us (3%)
    all_gather x2, waiting for transfers between devices, one_layer(): piece = lax.all_gather(keys_vals, ('tz', 'tp'), axis=0, tiled=True)  158 us
    ppermute x8, waiting for transfers between devices, rep_sum(): partner = lax.ppermute(total, 'rep', pairs)  34.7 us
    all_to_all x1, blocking collectives, one_layer(): lax.all_to_all(dispatch.reshape(experts_all, CAP, width), 'tz', split_axi...  31.4 us
    ppermute x6, starting transfers between devices, per_device(): other = tuple((lax.ppermute(w, 'section', swap) for w in own))  31.2 us
    ppermute x8, starting transfers between devices, rep_sum(): partner = lax.ppermute(total, 'rep', pairs)  26.6 us
    all_to_all x2, waiting for transfers between devices, one_layer(): lax.all_to_all(halves, 'tz', split_axis=0, concat_axis=0, tiled=True)  23.4 us
    ppermute x2, waiting for transfers between devices, one_layer(): pair_out = lax.ppermute(share_out[1], 'tp', pair_swap)  17.2 us
    ppermute x1, starting transfers between devices, per_device(): gotp0 = lax.ppermute(pages0, 'section', [(1, 0)])  14.9 us
  transfers between devices with their start and end apart: 27, of which 18 were waited for; matrix products, arithmetic and copies ran while one was open for 4% of the time, Pallas kernels for 0%

profile of v5, /device:TPU:1, one launch (start us, length us, event | category | flops | bytes accessed | tf_op | source)
XLA Modules:
  0.0 465.2 jit_solution(13585468877278558792)
XLA Ops:
  7.2 1.8 copy.51
  9.0 3.3 collective-permute-start.1
  12.6 2.9 collective-permute-done
  16.1 2.1 fusion.32
  24.8 1.2 fusion.111
  26.0 73.9 %all-gather.3.cloned.1.call-done = bf16[4096,2,256]{0,2,1:T(8,128)(2,1)} async-done(((bf16[128,2,256]{0,2,1:T(8,128)(2,1)}), bf16[4096,2,256]{0,2,1:T(8,128)(2,1)}) %all-gather.3.cloned.1.call-update) | async-done | bytes 4194320 | tf_op jit(solution)/shard_map/all_gather | solution.py:112
  99.9 2.8 while.30
  103.6 1.3 collective-permute-start.3
  105.8 3.1 collective-permute-done.3
  109.0 2.8 collective-permute-start.4
  111.8 5.9 %collective-permute-done.4 = bf16[128,1024]{1,0:T(8,128)(2,1)S(1)} collective-permute-done((bf16[128,1024]{1,0:T(8,128)(2,1)S(1)}, bf16[128,1024]{1,0:T(8,128)(2,1)S(1)}, u32[]{:S(2)}, u32[]{:S(2)}) %collective-permute-start.4) | collective-permute-done | bytes 262176 | tf_op jit(solution)/shard_map/ppermute | solution.py:39
  119.5 14.3 %all-to-all-start = ((bf16[16,20,1024]{2,1,0:T(8,128)(2,1)}), bf16[16,20,1024]{2,1,0:T(8,128)(2,1)S(1)}, u32[]{:S(2)}, u32[]{:S(2)}) async-start(bf16[16,20,1024]{2,1,0:T(8,128)(2,1)} %reshape.412), calls=%async_computation | async-start | bytes 1572864 | tf_op jit(solution)/shard_map/all_to_all | solution.py:157
  133.8 9.5 %collective-permute-start.7 = (bf16[1,1024,2,352]{1,3,2,0:T(8,128)(2,1)}, bf16[1,1024,2,352]{1,3,2,0:T(8,128)(2,1)}, u32[]{:S(2)}, u32[]{:S(2)}) collective-permute-start(bf16[1,1024,2,352]{1,3,2,0:T(8,128)(2,1)} %bitcast.232), channel_id=1, source_target_pairs={{0,128},{128,0},{1,129},{129,1},{2,130},{130,2},{3,131},{131,3},{4... | collective-permute-start | bytes 4325384 | tf_op jit(solution)/shard_map/ppermute | solution.py:201
  143.3 6.6 %all-to-all-done = bf16[16,20,1024]{2,1,0:T(8,128)(2,1)S(1)} async-done(((bf16[16,20,1024]{2,1,0:T(8,128)(2,1)}), bf16[16,20,1024]{2,1,0:T(8,128)(2,1)S(1)}, u32[]{:S(2)}, u32[]{:S(2)}) %all-to-all-start) | async-done | bytes 655392 | tf_op jit(solution)/shard_map/all_to_all | solution.py:157
  150.3 1.3 collective-permute-start.6
  151.6 10.7 %collective-permute-start.8 = (bf16[1,352,1024]{2,1,0:T(8,128)(2,1)}, bf16[1,352,1024]{2,1,0:T(8,128)(2,1)}, u32[]{:S(2)}, u32[]{:S(2)}) collective-permute-start(bf16[1,352,1024]{2,1,0:T(8,128)(2,1)} %bitcast.28), channel_id=1, source_target_pairs={{0,128},{128,0},{1,129},{129,1},{2,130},{130,2},{3,131},{131,3},{4... | collective-permute-start | bytes 2162696 | tf_op jit(solution)/shard_map/ppermute | solution.py:201
  164.1 3.5 fusion.26
  167.6 2.4 convolution_convert_fusion.1
  172.7 8.6 %collective-permute-done.9 = bf16[16,20,1024]{2,0,1:T(8,128)(2,1)} collective-permute-done((bf16[16,20,1024]{2,0,1:T(8,128)(2,1)}, bf16[16,20,1024]{2,0,1:T(8,128)(2,1)}, u32[]{:S(2)}, u32[]{:S(2)}) %collective-permute-start.9) | collective-permute-done | bytes 655392 | tf_op jit(solution)/shard_map/ppermute | solution.py:166
  181.3 2.4 add_convert_fusion.1
  183.7 6.2 %all-to-all-start.1 = ((bf16[16,20,1024]{2,1,0:T(8,128)(2,1)}), bf16[16,20,1024]{2,1,0:T(8,128)(2,1)S(1)}, u32[]{:S(2)}, u32[]{:S(2)}) async-start(bf16[16,20,1024]{2,1,0:T(8,128)(2,1)} %add_convert_fusion.1), calls=%async_computation.1 | async-start | bytes 1572864 | tf_op jit(solution)/shard_map/all_to_all | solution.py:168
  190.0 7.4 %collective-permute-start.5 = (bf16[1024,16]{0,1:T(8,128)(2,1)S(1)}, bf16[1024,16]{0,1:T(8,128)(2,1)S(1)}, u32[]{:S(2)}, u32[]{:S(2)}) collective-permute-start(bf16[1024,16]{0,1:T(8,128)(2,1)S(1)} %bitcast.225), channel_id=1, source_target_pairs={{0,128},{128,0},{1,129},{129,1},{2,130},{130,2},{3,131},{131,3},{4... | collective-permute-start | bytes 98312 | tf_op jit(solution)/shard_map/ppermute | solution.py:201
  198.5 7.5 %all-to-all-done.1 = bf16[16,20,1024]{2,1,0:T(8,128)(2,1)S(1)} async-done(((bf16[16,20,1024]{2,1,0:T(8,128)(2,1)}), bf16[16,20,1024]{2,1,0:T(8,128)(2,1)S(1)}, u32[]{:S(2)}, u32[]{:S(2)}) %all-to-all-start.1) | async-done | bytes 655392 | tf_op jit(solution)/shard_map/all_to_all | solution.py:168
  207.6 11.3 %collective-permute-start.10 = (bf16[128,1024]{1,0:T(8,128)(2,1)S(1)}, bf16[128,1024]{1,0:T(8,128)(2,1)S(1)}, u32[]{:S(2)}, u32[]{:S(2)}) collective-permute-start(bf16[128,1024]{1,0:T(8,128)(2,1)S(1)} %multiply_reduce_fusion.1), channel_id=1, source_target_pairs={{0,1},{1,0},{2,3},{3,2},{4,5},{5,4},{6,7},{7,6},{8,9},{9,8},{10,11... | collective-permute-start | bytes 786440 | tf_op jit(solution)/shard_map/ppermute | solution.py:39
  218.9 3.8 collective-permute-done.10
  222.8 8.3 %collective-permute-done.11 = bf16[128,1024]{1,0:T(8,128)(2,1)S(1)} collective-permute-done((bf16[128,1024]{1,0:T(8,128)(2,1)S(1)}, bf16[128,1024]{1,0:T(8,128)(2,1)S(1)}, u32[]{:S(2)}, u32[]{:S(2)}) %collective-permute-start.11) | collective-permute-done | bytes 262176 | tf_op jit(solution)/shard_map/ppermute | solution.py:39
  233.1 83.9 %all-gather.5.cloned.1.call-done = bf16[4096,2,256]{0,2,1:T(8,128)(2,1)} async-done(((bf16[128,2,256]{0,2,1:T(8,128)(2,1)}), bf16[4096,2,256]{0,2,1:T(8,128)(2,1)}) %all-gather.5.cloned.1.call-update) | async-done | bytes 4194320 | tf_op jit(solution)/shard_map/all_gather | solution.py:112
  317.0 2.8 while.31
  320.2 1.3 collective-permute-start.13
  321.4 4.0 collective-permute-done.13
  325.5 3.0 collective-permute-start.14
  328.5 5.8 %collective-permute-done.14 = bf16[128,1024]{1,0:T(8,128)(2,1)S(1)} collective-permute-done((bf16[128,1024]{1,0:T(8,128)(2,1)S(1)}, bf16[128,1024]{1,0:T(8,128)(2,1)S(1)}, u32[]{:S(2)}, u32[]{:S(2)}) %collective-permute-start.14) | collective-permute-done | bytes 262176 | tf_op jit(solution)/shard_map/ppermute | solution.py:39
  335.6 31.4 %all_to_all.20 = bf16[16,20,1024]{2,1,0:T(8,128)(2,1)S(1)} all-to-all(bf16[16,20,1024]{2,1,0:T(8,128)(2,1)S(1)} %reshape.418), channel_id=1, replica_groups=mesh['section'=2,'tz'=16,'tp'=2,'rep'=4] {'tz'}, dimensions={0} | all-to-all | bytes 1310720 | tf_op jit(solution)/shard_map/all_to_all | solution.py:157
  368.6 9.8 %collective-permute-done.15 = bf16[16,20,1024]{2,0,1:T(8,128)(2,1)S(1)} collective-permute-done((bf16[16,20,1024]{2,0,1:T(8,128)(2,1)S(1)}, bf16[16,20,1024]{2,0,1:T(8,128)(2,1)S(1)}, u32[]{:S(2)}, u32[]{:S(2)}) %collective-permute-start.15) | collective-permute-done | bytes 655392 | tf_op jit(solution)/shard_map/ppermute | solution.py:160
  379.3 2.7 fusion.24
  382.0 2.2 convolution_convert_fusion
  384.5 1.3 copy.61
  386.9 8.6 %collective-permute-done.16 = bf16[16,20,1024]{2,0,1:T(8,128)(2,1)} collective-permute-done((bf16[16,20,1024]{2,0,1:T(8,128)(2,1)}, bf16[16,20,1024]{2,0,1:T(8,128)(2,1)}, u32[]{:S(2)}, u32[]{:S(2)}) %collective-permute-start.16) | collective-permute-done | bytes 655392 | tf_op jit(solution)/shard_map/ppermute | solution.py:166
  395.5 2.5 add_convert_fusion
  397.9 5.7 %all-to-all-start.3 = ((bf16[16,20,1024]{2,1,0:T(8,128)(2,1)}), bf16[16,20,1024]{2,1,0:T(8,128)(2,1)S(1)}, u32[]{:S(2)}, u32[]{:S(2)}) async-start(bf16[16,20,1024]{2,1,0:T(8,128)(2,1)} %add_convert_fusion), calls=%async_computation.3 | async-start | bytes 1572864 | tf_op jit(solution)/shard_map/all_to_all | solution.py:168
  404.0 15.9 %all-to-all-done.3 = bf16[16,20,1024]{2,1,0:T(8,128)(2,1)S(1)} async-done(((bf16[16,20,1024]{2,1,0:T(8,128)(2,1)}), bf16[16,20,1024]{2,1,0:T(8,128)(2,1)S(1)}, u32[]{:S(2)}, u32[]{:S(2)}) %all-to-all-start.3) | async-done | bytes 655392 | tf_op jit(solution)/shard_map/all_to_all | solution.py:168
  421.3 6.8 %collective-permute-start.17 = (bf16[128,1024]{1,0:T(8,128)(2,1)S(1)}, bf16[128,1024]{1,0:T(8,128)(2,1)S(1)}, u32[]{:S(2)}, u32[]{:S(2)}) collective-permute-start(bf16[128,1024]{1,0:T(8,128)(2,1)S(1)} %multiply_reduce_fusion), channel_id=1, source_target_pairs={{0,1},{1,0},{2,3},{3,2},{4,5},{5,4},{6,7},{7,6},{8,9},{9,8},{10,11... | collective-permute-start | bytes 786440 | tf_op jit(solution)/shard_map/ppermute | solution.py:39
  428.1 3.8 collective-permute-done.17
  434.5 14.9 %collective-permute-start.20 = (bf16[1,128,2,256]{1,3,2,0:T(8,128)(2,1)S(1)}, bf16[1,128,2,256]{1,3,2,0:T(8,128)(2,1)S(1)}, u32[]{:S(2)}, u32[]{:S(2)}) collective-permute-start(bf16[1,128,2,256]{1,3,2,0:T(8,128)(2,1)S(1)} %get-tuple-element.248), channel_id=1, source_target_pairs={{128,0},{129,1},{130,2},{131,3},{132,4},{133,5},{134,6},{135,7},{1... | collective-permute-start | bytes 393224 | tf_op jit(solution)/shard_map/ppermute | solution.py:217
  449.4 1.3 collective-permute-start.12
  450.9 1.3 collective-permute-start.19
  453.3 1.3 collective-permute-start.21
  454.6 1.9 collective-permute-done.21
  (188 shorter events, 35.5 us)
Async XLA Ops:
  7.2 5.1 %copy-start.24 = (f32[1,2,1024]{2,1,0:T(2,128)S(1)}, f32[1,2,1024]{2,1,0:T(2,128)}, u32[]{:S(2)}) copy-start(f32[1,2,1024]{2,1,0:T(2,128)} %param.20) | copy-start | bytes 24580
  7.2 5.2 %copy-start.10 = (bf16[2,128,1024]{2,1,0:T(8,128)(2,1)S(1)}, bf16[2,128,1024]{2,1,0:T(8,128)(2,1)}, u32[]{:S(2)}) copy-start(bf16[2,128,1024]{2,1,0:T(8,128)(2,1)} %param.16) | copy-start | bytes 1572868
  7.2 92.7 %all-gather.3.cloned.1.call-start = ((), (), s32[]{:S(2)}) async-start(), calls=%async_computation.4 | async-start | bytes 4325376 | tf_op jit(solution)/shard_map/all_gather | solution.py:112
  9.0 9.2 %copy-start.12 = (bf16[1,1024,3,256]{1,3,2,0:T(8,128)(2,1)}, bf16[1,1024,3,256]{1,3,2,0:T(8,128)(2,1)S(1)}, u32[]{:S(2)}) copy-start(bf16[1,1024,3,256]{1,3,2,0:T(8,128)(2,1)S(1)} %copy.51) | copy-start | bytes 4718596
  9.0 7.1 %collective-permute-start.1 = (bf16[1024,768]{0,1:T(8,128)(2,1)S(1)}, bf16[1024,768]{0,1:T(8,128)(2,1)}, u32[]{:S(2)}, u32[]{:S(2)}) collective-permute-start(bf16[1024,768]{0,1:T(8,128)(2,1)S(1)} %bitcast.209), channel_id=1, source_target_pairs={{0,128},{128,0},{1,129},{129,1},{2,130},{130,2},{3,131},{131,3},{4... | collective-permute-start | bytes 4718600 | tf_op jit(solution)/shard_map/ppermute | solution.py:201
  12.3 3.2 collective-permute-start
  19.1 83.7 %collective-permute-start.2 = (bf16[256,1024]{1,0:T(8,128)(2,1)S(1)}, bf16[256,1024]{1,0:T(8,128)(2,1)S(1)}, u32[]{:S(2)}, u32[]{:S(2)}) collective-permute-start(bf16[256,1024]{1,0:T(8,128)(2,1)S(1)} %bitcast.208), channel_id=1, source_target_pairs={{0,128},{128,0},{1,129},{129,1},{2,130},{130,2},{3,131},{131,3},{4... | collective-permute-start | bytes 1572872 | tf_op jit(solution)/shard_map/ppermute | solution.py:201
  26.0 79.6 %copy-start.22 = (s32[256]{0:T(256)}, s32[256]{0:T(256)S(1)}, u32[]{:S(2)}) copy-start(s32[256]{0:T(256)S(1)} %get-tuple-element.261) | copy-start | bytes 3076
  103.3 14.6 %copy-start.8 = (bf16[256,1024]{1,0:T(8,128)(2,1)}, bf16[256,1024]{1,0:T(8,128)(2,1)S(1)}, u32[]{:S(2)}) copy-start(bf16[256,1024]{1,0:T(8,128)(2,1)S(1)} %collective-permute-done.2) | copy-start | bytes 1572868
  103.3 14.6 %copy-start.20 = (f32[1,1024]{1,0:T(1,128)S(1)}, f32[1,1024]{1,0:T(1,128)}, u32[]{:S(2)}) copy-start(f32[1,1024]{1,0:T(1,128)} %get-tuple-element.262) | copy-start | bytes 12292
  103.6 5.3 %collective-permute-start.3 = (bf16[128,1024]{1,0:T(8,128)(2,1)S(1)}, bf16[128,1024]{1,0:T(8,128)(2,1)S(1)}, u32[]{:S(2)}, u32[]{:S(2)}) collective-permute-start(bf16[128,1024]{1,0:T(8,128)(2,1)S(1)} %convolution_convert_fusion.5), channel_id=1, source_target_pairs={{0,1},{1,0},{2,3},{3,2},{4,5},{5,4},{6,7},{7,6},{8,9},{9,8},{10,11... | collective-permute-start | bytes 786440 | tf_op jit(solution)/shard_map/ppermute | solution.py:39
  109.0 8.8 %collective-permute-start.4 = (bf16[128,1024]{1,0:T(8,128)(2,1)S(1)}, bf16[128,1024]{1,0:T(8,128)(2,1)S(1)}, u32[]{:S(2)}, u32[]{:S(2)}) collective-permute-start(bf16[128,1024]{1,0:T(8,128)(2,1)S(1)} %add_convert_fusion.7), channel_id=1, source_target_pairs={{0,2},{1,3},{2,0},{3,1},{4,6},{5,7},{6,4},{7,5},{8,10},{9,11},{10,... | collective-permute-start | bytes 786440 | tf_op jit(solution)/shard_map/ppermute | solution.py:39
  111.8 7.7 %copy-start.14 = (s32[128,320]{0,1:T(8,128)}, s32[128,320]{0,1:T(8,128)S(1)}, u32[]{:S(2)}) copy-start(s32[128,320]{0,1:T(8,128)S(1)} %convert_reduce_fusion) | copy-start | bytes 491524
  119.5 30.5 %all-to-all-start = ((bf16[16,20,1024]{2,1,0:T(8,128)(2,1)}), bf16[16,20,1024]{2,1,0:T(8,128)(2,1)S(1)}, u32[]{:S(2)}, u32[]{:S(2)}) async-start(bf16[16,20,1024]{2,1,0:T(8,128)(2,1)} %reshape.412), calls=%async_computation | async-start | bytes 1572864 | tf_op jit(solution)/shard_map/all_to_all | solution.py:157
  133.8 30.2 %collective-permute-start.7 = (bf16[1,1024,2,352]{1,3,2,0:T(8,128)(2,1)}, bf16[1,1024,2,352]{1,3,2,0:T(8,128)(2,1)}, u32[]{:S(2)}, u32[]{:S(2)}) collective-permute-start(bf16[1,1024,2,352]{1,3,2,0:T(8,128)(2,1)} %bitcast.232), channel_id=1, source_target_pairs={{0,128},{128,0},{1,129},{129,1},{2,130},{130,2},{3,131},{131,3},{4... | collective-permute-start | bytes 4325384 | tf_op jit(solution)/shard_map/ppermute | solution.py:201
  150.3 12.0 %collective-permute-start.6 = (bf16[16,20,1024]{2,0,1:T(8,128)(2,1)S(1)}, bf16[16,20,1024]{2,0,1:T(8,128)(2,1)S(1)}, u32[]{:S(2)}, u32[]{:S(2)}) collective-permute-start(bf16[16,20,1024]{2,0,1:T(8,128)(2,1)S(1)} %copy.54), channel_id=1, source_target_pairs={{0,4},{4,0},{1,5},{5,1},{2,6},{6,2},{3,7},{7,3},{8,12},{12,8},{9,1... | collective-permute-start | bytes 1966088 | tf_op jit(solution)/shard_map/ppermute | solution.py:160
  151.6 16.0 %collective-permute-start.8 = (bf16[1,352,1024]{2,1,0:T(8,128)(2,1)}, bf16[1,352,1024]{2,1,0:T(8,128)(2,1)}, u32[]{:S(2)}, u32[]{:S(2)}) collective-permute-start(bf16[1,352,1024]{2,1,0:T(8,128)(2,1)} %bitcast.28), channel_id=1, source_target_pairs={{0,128},{128,0},{1,129},{129,1},{2,130},{130,2},{3,131},{131,3},{4... | collective-permute-start | bytes 2162696 | tf_op jit(solution)/shard_map/ppermute | solution.py:201
  171.5 9.8 %collective-permute-start.9 = (bf16[16,20,1024]{2,0,1:T(8,128)(2,1)}, bf16[16,20,1024]{2,0,1:T(8,128)(2,1)}, u32[]{:S(2)}, u32[]{:S(2)}) collective-permute-start(bf16[16,20,1024]{2,0,1:T(8,128)(2,1)} %copy.56), channel_id=1, source_target_pairs={{0,4},{4,0},{1,5},{5,1},{2,6},{6,2},{3,7},{7,3},{8,12},{12,8},{9,1... | collective-permute-start | bytes 1966088 | tf_op jit(solution)/shard_map/ppermute | solution.py:166
  172.7 17.3 %copy-start.16 = (bf16[1,1024,16]{1,2,0:T(8,128)(2,1)S(1)}, bf16[1,1024,16]{1,2,0:T(8,128)(2,1)}, u32[]{:S(2)}) copy-start(bf16[1,1024,16]{1,2,0:T(8,128)(2,1)} %param.23) | copy-start | bytes 98308
  172.7 24.7 %copy-start.23 = (s32[256]{0:T(256)S(1)}, s32[256]{0:T(256)}, u32[]{:S(2)}) copy-start(s32[256]{0:T(256)} %copy-done.22) | copy-start | bytes 3076
  172.7 25.6 %copy-start.1 = (bf16[128,1024]{1,0:T(8,128)(2,1)S(1)}, bf16[128,1024]{1,0:T(8,128)(2,1)}, u32[]{:S(2)}) copy-start(bf16[128,1024]{1,0:T(8,128)(2,1)} %copy-done) | copy-start | bytes 786436
  183.7 14.8 %copy-start.21 = (s32[128,2]{0,1:T(2,128)S(1)}, s32[128,2]{0,1:T(2,128)}, u32[]{:S(2)}) copy-start(s32[128,2]{0,1:T(2,128)} %get-tuple-element.259) | copy-start | bytes 3076
  183.7 22.4 %all-to-all-start.1 = ((bf16[16,20,1024]{2,1,0:T(8,128)(2,1)}), bf16[16,20,1024]{2,1,0:T(8,128)(2,1)S(1)}, u32[]{:S(2)}, u32[]{:S(2)}) async-start(bf16[16,20,1024]{2,1,0:T(8,128)(2,1)} %add_convert_fusion.1), calls=%async_computation.1 | async-start | bytes 1572864 | tf_op jit(solution)/shard_map/all_to_all | solution.py:168
  189.9 127.1 %all-gather.5.cloned.1.call-start = ((), (), s32[]{:S(2)}) async-start(), calls=%async_computation.5 | async-start | bytes 4325376 | tf_op jit(solution)/shard_map/all_gather | solution.py:112
  190.0 8.3 %collective-permute-start.5 = (bf16[1024,16]{0,1:T(8,128)(2,1)S(1)}, bf16[1024,16]{0,1:T(8,128)(2,1)S(1)}, u32[]{:S(2)}, u32[]{:S(2)}) collective-permute-start(bf16[1024,16]{0,1:T(8,128)(2,1)S(1)} %bitcast.225), channel_id=1, source_target_pairs={{0,128},{128,0},{1,129},{129,1},{2,130},{130,2},{3,131},{131,3},{4... | collective-permute-start | bytes 98312 | tf_op jit(solution)/shard_map/ppermute | solution.py:201
  207.4 23.7 %copy-start.11 = (bf16[2,128,1024]{2,1,0:T(8,128)(2,1)S(1)}, bf16[2,128,1024]{2,1,0:T(8,128)(2,1)}, u32[]{:S(2)}) copy-start(bf16[2,128,1024]{2,1,0:T(8,128)(2,1)} %param.16) | copy-start | bytes 1572868
  207.4 24.1 %copy-start.13 = (bf16[1,1024,3,256]{1,3,2,0:T(8,128)(2,1)S(1)}, bf16[1,1024,3,256]{1,3,2,0:T(8,128)(2,1)}, u32[]{:S(2)}) copy-start(bf16[1,1024,3,256]{1,3,2,0:T(8,128)(2,1)} %copy-done.12) | copy-start | bytes 4718596
  207.4 24.1 %copy-start.25 = (f32[1,1024]{1,0:T(1,128)S(1)}, f32[1,1024]{1,0:T(1,128)}, u32[]{:S(2)}) copy-start(f32[1,1024]{1,0:T(1,128)} %get-tuple-element.255) | copy-start | bytes 12292
  207.6 15.1 %collective-permute-start.10 = (bf16[128,1024]{1,0:T(8,128)(2,1)S(1)}, bf16[128,1024]{1,0:T(8,128)(2,1)S(1)}, u32[]{:S(2)}, u32[]{:S(2)}) collective-permute-start(bf16[128,1024]{1,0:T(8,128)(2,1)S(1)} %multiply_reduce_fusion.1), channel_id=1, source_target_pairs={{0,1},{1,0},{2,3},{3,2},{4,5},{5,4},{6,7},{7,6},{8,9},{9,8},{10,11... | collective-permute-start | bytes 786440 | tf_op jit(solution)/shard_map/ppermute | solution.py:39
  222.7 8.4 %collective-permute-start.11 = (bf16[128,1024]{1,0:T(8,128)(2,1)S(1)}, bf16[128,1024]{1,0:T(8,128)(2,1)S(1)}, u32[]{:S(2)}, u32[]{:S(2)}) collective-permute-start(bf16[128,1024]{1,0:T(8,128)(2,1)S(1)} %add_convert_fusion.6), channel_id=1, source_target_pairs={{0,2},{1,3},{2,0},{3,1},{4,6},{5,7},{6,4},{7,5},{8,10},{9,11},{10,... | collective-permute-start | bytes 786440 | tf_op jit(solution)/shard_map/ppermute | solution.py:39
  231.5 85.5 %copy-start.18 = (s32[128]{0:T(128)S(1)}, s32[128]{0:T(128)}, u32[]{:S(2)}) copy-start(s32[128]{0:T(128)} %copy-done.17) | copy-start | bytes 1540
  319.8 15.2 %copy-start.19 = (f32[1,1024]{1,0:T(1,128)S(1)}, f32[1,1024]{1,0:T(1,128)}, u32[]{:S(2)}) copy-start(f32[1,1024]{1,0:T(1,128)} %get-tuple-element.256) | copy-start | bytes 12292
  320.1 15.0 %copy-start.15 = (s32[128,320]{0,1:T(8,128)S(1)}, s32[128,320]{0,1:T(8,128)}, u32[]{:S(2)}) copy-start(s32[128,320]{0,1:T(8,128)} %copy-done.14) | copy-start | bytes 491524
  320.2 5.3 %collective-permute-start.13 = (bf16[128,1024]{1,0:T(8,128)(2,1)S(1)}, bf16[128,1024]{1,0:T(8,128)(2,1)S(1)}, u32[]{:S(2)}, u32[]{:S(2)}) collective-permute-start(bf16[128,1024]{1,0:T(8,128)(2,1)S(1)} %convolution_convert_fusion.4), channel_id=1, source_target_pairs={{0,1},{1,0},{2,3},{3,2},{4,5},{5,4},{6,7},{7,6},{8,9},{9,8},{10,11... | collective-permute-start | bytes 786440 | tf_op jit(solution)/shard_map/ppermute | solution.py:39
  325.5 8.8 %collective-permute-start.14 = (bf16[128,1024]{1,0:T(8,128)(2,1)S(1)}, bf16[128,1024]{1,0:T(8,128)(2,1)S(1)}, u32[]{:S(2)}, u32[]{:S(2)}) collective-permute-start(bf16[128,1024]{1,0:T(8,128)(2,1)S(1)} %add_convert_fusion.4), channel_id=1, source_target_pairs={{0,2},{1,3},{2,0},{3,1},{4,6},{5,7},{6,4},{7,5},{8,10},{9,11},{10,... | collective-permute-start | bytes 786440 | tf_op jit(solution)/shard_map/ppermute | solution.py:39
  335.1 31.9 %copy-start.2 = (bf16[128,1024]{1,0:T(8,128)(2,1)}, bf16[128,1024]{1,0:T(8,128)(2,1)S(1)}, u32[]{:S(2)}) copy-start(bf16[128,1024]{1,0:T(8,128)(2,1)S(1)} %multiply_convert_fusion) | copy-start | bytes 786436
  367.4 11.0 %collective-permute-start.15 = (bf16[16,20,1024]{2,0,1:T(8,128)(2,1)S(1)}, bf16[16,20,1024]{2,0,1:T(8,128)(2,1)S(1)}, u32[]{:S(2)}, u32[]{:S(2)}) collective-permute-start(bf16[16,20,1024]{2,0,1:T(8,128)(2,1)S(1)} %copy.59), channel_id=1, source_target_pairs={{0,4},{4,0},{1,5},{5,1},{2,6},{6,2},{3,7},{7,3},{8,12},{12,8},{9,1... | collective-permute-start | bytes 1966088 | tf_op jit(solution)/shard_map/ppermute | solution.py:160
  385.7 9.8 %collective-permute-start.16 = (bf16[16,20,1024]{2,0,1:T(8,128)(2,1)}, bf16[16,20,1024]{2,0,1:T(8,128)(2,1)}, u32[]{:S(2)}, u32[]{:S(2)}) collective-permute-start(bf16[16,20,1024]{2,0,1:T(8,128)(2,1)} %copy.61), channel_id=1, source_target_pairs={{0,4},{4,0},{1,5},{5,1},{2,6},{6,2},{3,7},{7,3},{8,12},{12,8},{9,1... | collective-permute-start | bytes 1966088 | tf_op jit(solution)/shard_map/ppermute | solution.py:166
  386.9 16.8 %copy-start.3 = (bf16[128,1024]{1,0:T(8,128)(2,1)S(1)}, bf16[128,1024]{1,0:T(8,128)(2,1)}, u32[]{:S(2)}) copy-start(bf16[128,1024]{1,0:T(8,128)(2,1)} %copy-done.2) | copy-start | bytes 786436
  397.9 21.9 %all-to-all-start.3 = ((bf16[16,20,1024]{2,1,0:T(8,128)(2,1)}), bf16[16,20,1024]{2,1,0:T(8,128)(2,1)S(1)}, u32[]{:S(2)}, u32[]{:S(2)}) async-start(bf16[16,20,1024]{2,1,0:T(8,128)(2,1)} %add_convert_fusion), calls=%async_computation.3 | async-start | bytes 1572864 | tf_op jit(solution)/shard_map/all_to_all | solution.py:168
  421.2 10.9 %copy-start.26 = (s32[2,32]{1,0:T(2,128)S(1)}, s32[2,32]{1,0:T(2,128)}, u32[]{:S(2)}) copy-start(s32[2,32]{1,0:T(2,128)} %param.19) | copy-start | bytes 772
  421.2 29.5 %copy-start.5 = (bf16[128,1024]{1,0:T(8,128)(2,1)S(1)}, bf16[128,1024]{1,0:T(8,128)(2,1)}, u32[]{:S(2)}) copy-start(bf16[128,1024]{1,0:T(8,128)(2,1)} %copy-done.4) | copy-start | bytes 786436
  421.3 10.6 %collective-permute-start.17 = (bf16[128,1024]{1,0:T(8,128)(2,1)S(1)}, bf16[128,1024]{1,0:T(8,128)(2,1)S(1)}, u32[]{:S(2)}, u32[]{:S(2)}) collective-permute-start(bf16[128,1024]{1,0:T(8,128)(2,1)S(1)} %multiply_reduce_fusion), channel_id=1, source_target_pairs={{0,1},{1,0},{2,3},{3,2},{4,5},{5,4},{6,7},{7,6},{8,9},{9,8},{10,11... | collective-permute-start | bytes 786440 | tf_op jit(solution)/shard_map/ppermute | solution.py:39
  432.0 18.7 %collective-permute-start.18 = (bf16[128,1024]{1,0:T(8,128)(2,1)S(1)}, bf16[128,1024]{1,0:T(8,128)(2,1)S(1)}, u32[]{:S(2)}, u32[]{:S(2)}) collective-permute-start(bf16[128,1024]{1,0:T(8,128)(2,1)S(1)} %add_convert_fusion.3), channel_id=1, source_target_pairs={{0,2},{1,3},{2,0},{3,1},{4,6},{5,7},{6,4},{7,5},{8,10},{9,11},{10,... | collective-permute-start | bytes 786440 | tf_op jit(solution)/shard_map/ppermute | solution.py:39
  434.5 20.2 %collective-permute-start.20 = (bf16[1,128,2,256]{1,3,2,0:T(8,128)(2,1)S(1)}, bf16[1,128,2,256]{1,3,2,0:T(8,128)(2,1)S(1)}, u32[]{:S(2)}, u32[]{:S(2)}) collective-permute-start(bf16[1,128,2,256]{1,3,2,0:T(8,128)(2,1)S(1)} %get-tuple-element.248), channel_id=1, source_target_pairs={{128,0},{129,1},{130,2},{131,3},{132,4},{133,5},{134,6},{135,7},{1... | collective-permute-start | bytes 393224 | tf_op jit(solution)/shard_map/ppermute | solution.py:217
  449.4 8.1 %collective-permute-start.12 = (bf16[128,1024]{1,0:T(8,128)(2,1)S(1)}, bf16[128,1024]{1,0:T(8,128)(2,1)S(1)}, u32[]{:S(2)}, u32[]{:S(2)}) collective-permute-start(bf16[128,1024]{1,0:T(8,128)(2,1)S(1)} %get-tuple-element.234), channel_id=1, source_target_pairs={{128,0},{129,1},{130,2},{131,3},{132,4},{133,5},{134,6},{135,7},{1... | collective-permute-start | bytes 786440 | tf_op jit(solution)/shard_map/ppermute | solution.py:216
  450.9 6.6 %collective-permute-start.19 = (bf16[128,1024]{1,0:T(8,128)(2,1)S(1)}, bf16[128,1024]{1,0:T(8,128)(2,1)S(1)}, u32[]{:S(2)}, u32[]{:S(2)}) collective-permute-start(bf16[128,1024]{1,0:T(8,128)(2,1)S(1)} %add_convert_fusion.2), channel_id=1, source_target_pairs={{0,128},{1,129},{2,130},{3,131},{4,132},{5,133},{6,134},{7,135},{8... | collective-permute-start | bytes 786440 | tf_op jit(solution)/shard_map/ppermute | solution.py:218
  453.3 3.3 collective-permute-start.21
  (6 other events, 11.4 us)
Sparse Core Ops, SparseCore 0:
  19.2 80.6 all-gather.2
  233.2 83.7 all-gather.4

commit v6 on v5

--- a/solution.py
+++ b/solution.py
@@ -7,6 +7,7 @@
 TOP = 2
 PAGE = 128
 CAP = 20
+LONGEST = 2048
 
 
 NEG_FILL = -1e30
@@ -111,21 +112,13 @@
     empty_pages = jnp.zeros((blocks_dev, PAGE, 2, col_width), jnp.bfloat16)
     piece = lax.all_gather(keys_vals, ("tz", "tp"), axis=0, tiled=True)
     rows_key = piece.shape[0]
-    step_rows = 512
-    while rows_key % step_rows != 0:
-        step_rows = step_rows // 2
+    window = min(rows_key, -(-(LONGEST + tok_rows) // 256) * 256)
     seg_start = jnp.sum((seg_all < seg_query[0]).astype(jnp.int32))
-    first_turn = seg_start // step_rows
-    last_turn = (tok_index * tok_rows + tok_rows - 1) // step_rows
-
-    def key_block(index, soft_now):
-        start = index * step_rows
-        block = lax.dynamic_slice_in_dim(piece, start, step_rows, 0)
-        seg_key = lax.dynamic_slice_in_dim(seg_all, start, step_rows)
-        pos_key = start + jnp.arange(step_rows, dtype=jnp.int32)
-        return attend(soft_now, queries, block, seg_query, pos_query, seg_key, pos_key)
-
-    soft_next = lax.fori_loop(first_turn, last_turn + 1, key_block, soft_init)
+    window_at = jnp.clip(seg_start, 0, rows_key - window)
+    block = lax.dynamic_slice_in_dim(piece, window_at, window, 0)
+    seg_key = lax.dynamic_slice_in_dim(seg_all, window_at, window)
+    pos_key = window_at + jnp.arange(window, dtype=jnp.int32)
+    soft_next = attend(soft_init, queries, block, seg_query, pos_query, seg_key, pos_key)
     pages = place_pages(empty_pages, piece, table_row, tok_index)
     run_max, run_sum, run_acc = soft_next
     context = (

time: 467 us -> 465 us (level); the launches traced: 465 us -> 456 us
  starting transfers between devices: 107 us -> 86 us
  waiting for transfers between devices: 255 us -> 267 us
  blocking collectives: 31.4 us -> 23.4 us
  matrix products: 17.3 us -> 24.5 us
    ppermute x8, starting transfers between devices: 26.6 us -> 12.5 us  [rep_sum(): partner = lax.ppermute(total, 'rep', pairs)]
    all_to_all x1, blocking collectives: 31.4 us -> 23.4 us  [one_layer(): lax.all_to_all(dispatch.reshape(experts_all, CAP, width), 'tz', split_axi...]
    all_to_all x1, starting transfers between devices: 14.3 us -> 7.16 us  [one_layer(): lax.all_to_all(dispatch.reshape(experts_all, CAP, width), 'tz', split_axi...]
    dot_general x2, matrix products: 1.47 us -> 7.34 us  [attend(): jnp.einsum('htn,nhd->htd', weights, val_part, precision=lax.Precision.HIG...]
    all_to_all x2, starting transfers between devices: 12 us -> 17.4 us  [one_layer(): lax.all_to_all(halves, 'tz', split_axis=0, concat_axis=0, tiled=True)]
  transfers between devices with their start and end apart: 27 -> 27, of which waited for: 18 -> 19; matrix products, arithmetic and copies ran while one was open for 4% -> 5% of each run, Pallas kernels for 0% -> 0%
where the time goes in v6:
time: 465 us; the launch traced here: 456 us
  waiting for transfers between devices  267 us (57%)
  starting transfers between devices  86 us (18%)
  matrix products  24.5 us (5%)
  blocking collectives  23.4 us (5%)
  local copies, waits for them, and re-layouts  22.1 us (5%)
  between operations  16.6 us (4%)
  other arithmetic  15.6 us (3%)
    all_gather x2, waiting for transfers between devices, one_layer(): piece = lax.all_gather(keys_vals, ('tz', 'tp'), axis=0, tiled=True)  159 us
    ppermute x8, waiting for transfers between devices, rep_sum(): partner = lax.ppermute(total, 'rep', pairs)  38.4 us
    all_to_all x2, waiting for transfers between devices, one_layer(): lax.all_to_all(halves, 'tz', split_axis=0, concat_axis=0, tiled=True)  27.6 us
    ppermute x6, starting transfers between devices, per_device(): other = tuple((lax.ppermute(w, 'section', swap) for w in own))  26.7 us
    all_to_all x1, blocking collectives, one_layer(): lax.all_to_all(dispatch.reshape(experts_all, CAP, width), 'tz', split_axi...  23.4 us
    ppermute x2, waiting for transfers between devices, one_layer(): pair_out = lax.ppermute(share_out[1], 'tp', pair_swap)  17.7 us
    all_to_all x2, starting transfers between devices, one_layer(): lax.all_to_all(halves, 'tz', split_axis=0, concat_axis=0, tiled=True)  17.4 us
    ppermute x1, starting transfers between devices, per_device(): gotp0 = lax.ppermute(pages0, 'section', [(1, 0)])  15.7 us
  transfers between devices with their start and end apart: 27, of which 19 were waited for; matrix products, arithmetic and copies ran while one was open for 5% of the time, Pallas kernels for 0%

profile of v6, /device:TPU:1, one launch (start us, length us, event | category | flops | bytes accessed | tf_op | source)
XLA Modules:
  0.0 455.6 jit_solution(13563228096919998756)
XLA Ops:
  7.2 2.7 copy.45
  9.9 3.2 collective-permute-start.1
  13.3 3.1 collective-permute-done
  17.6 2.1 fusion.26
  23.1 78.6 %all-gather.3.cloned.1.call-done = bf16[4096,2,256]{0,2,1:T(8,128)(2,1)} async-done(((bf16[128,2,256]{0,2,1:T(8,128)(2,1)}), bf16[4096,2,256]{0,2,1:T(8,128)(2,1)}) %all-gather.3.cloned.1.call-update) | async-done | bytes 4194320 | tf_op jit(solution)/shard_map/all_gather | solution.py:113
  101.7 3.2 constant_dynamic-slice_fusion.1
  107.1 3.7 fusion.39
  111.1 1.3 collective-permute-start.3
  113.3 3.1 collective-permute-done.3
  116.5 3.0 collective-permute-start.4
  119.5 5.7 %collective-permute-done.4 = bf16[128,1024]{1,0:T(8,128)(2,1)S(1)} collective-permute-done((bf16[128,1024]{1,0:T(8,128)(2,1)S(1)}, bf16[128,1024]{1,0:T(8,128)(2,1)S(1)}, u32[]{:S(2)}, u32[]{:S(2)}) %collective-permute-start.4) | collective-permute-done | bytes 262176 | tf_op jit(solution)/shard_map/ppermute | solution.py:40
  127.0 7.2 %all-to-all-start = ((bf16[16,20,1024]{2,1,0:T(8,128)(2,1)}), bf16[16,20,1024]{2,1,0:T(8,128)(2,1)S(1)}, u32[]{:S(2)}, u32[]{:S(2)}) async-start(bf16[16,20,1024]{2,1,0:T(8,128)(2,1)} %reshape.388), calls=%async_computation | async-start | bytes 1572864 | tf_op jit(solution)/shard_map/all_to_all | solution.py:150
  134.1 7.9 %collective-permute-start.7 = (bf16[1,1024,2,352]{1,3,2,0:T(8,128)(2,1)}, bf16[1,1024,2,352]{1,3,2,0:T(8,128)(2,1)}, u32[]{:S(2)}, u32[]{:S(2)}) collective-permute-start(bf16[1,1024,2,352]{1,3,2,0:T(8,128)(2,1)} %bitcast.222), channel_id=1, source_target_pairs={{0,128},{128,0},{1,129},{129,1},{2,130},{130,2},{3,131},{131,3},{4... | collective-permute-start | bytes 4325384 | tf_op jit(solution)/shard_map/ppermute | solution.py:194
  142.0 8.3 %all-to-all-done = bf16[16,20,1024]{2,1,0:T(8,128)(2,1)S(1)} async-done(((bf16[16,20,1024]{2,1,0:T(8,128)(2,1)}), bf16[16,20,1024]{2,1,0:T(8,128)(2,1)S(1)}, u32[]{:S(2)}, u32[]{:S(2)}) %all-to-all-start) | async-done | bytes 655392 | tf_op jit(solution)/shard_map/all_to_all | solution.py:150
  150.9 10.1 %collective-permute-start.8 = (bf16[1,352,1024]{2,1,0:T(8,128)(2,1)}, bf16[1,352,1024]{2,1,0:T(8,128)(2,1)}, u32[]{:S(2)}, u32[]{:S(2)}) collective-permute-start(bf16[1,352,1024]{2,1,0:T(8,128)(2,1)} %bitcast.223), channel_id=1, source_target_pairs={{0,128},{128,0},{1,129},{129,1},{2,130},{130,2},{3,131},{131,3},{4... | collective-permute-start | bytes 2162696 | tf_op jit(solution)/shard_map/ppermute | solution.py:194
  162.4 3.2 fusion.20
  165.7 2.2 convolution_convert_fusion.1
  168.2 1.2 copy.50
  170.6 8.5 %collective-permute-done.9 = bf16[16,20,1024]{2,0,1:T(8,128)(2,1)} collective-permute-done((bf16[16,20,1024]{2,0,1:T(8,128)(2,1)}, bf16[16,20,1024]{2,0,1:T(8,128)(2,1)}, u32[]{:S(2)}, u32[]{:S(2)}) %collective-permute-start.9) | collective-permute-done | bytes 655392 | tf_op jit(solution)/shard_map/ppermute | solution.py:159
  179.1 2.4 add_convert_fusion.1
  181.5 11.4 %all-to-all-start.1 = ((bf16[16,20,1024]{2,1,0:T(8,128)(2,1)}), bf16[16,20,1024]{2,1,0:T(8,128)(2,1)S(1)}, u32[]{:S(2)}, u32[]{:S(2)}) async-start(bf16[16,20,1024]{2,1,0:T(8,128)(2,1)} %add_convert_fusion.1), calls=%async_computation.1 | async-start | bytes 1572864 | tf_op jit(solution)/shard_map/all_to_all | solution.py:161
  193.0 5.0 %collective-permute-start.5 = (bf16[1024,16]{0,1:T(8,128)(2,1)S(1)}, bf16[1024,16]{0,1:T(8,128)(2,1)S(1)}, u32[]{:S(2)}, u32[]{:S(2)}) collective-permute-start(bf16[1024,16]{0,1:T(8,128)(2,1)S(1)} %bitcast.213), channel_id=1, source_target_pairs={{0,128},{128,0},{1,129},{129,1},{2,130},{130,2},{3,131},{131,3},{4... | collective-permute-start | bytes 98312 | tf_op jit(solution)/shard_map/ppermute | solution.py:194
  199.2 11.7 %all-to-all-done.1 = bf16[16,20,1024]{2,1,0:T(8,128)(2,1)S(1)} async-done(((bf16[16,20,1024]{2,1,0:T(8,128)(2,1)}), bf16[16,20,1024]{2,1,0:T(8,128)(2,1)S(1)}, u32[]{:S(2)}, u32[]{:S(2)}) %all-to-all-start.1) | async-done | bytes 655392 | tf_op jit(solution)/shard_map/all_to_all | solution.py:161
  212.5 5.5 %collective-permute-done.10 = bf16[128,1024]{1,0:T(8,128)(2,1)S(1)} collective-permute-done((bf16[128,1024]{1,0:T(8,128)(2,1)S(1)}, bf16[128,1024]{1,0:T(8,128)(2,1)S(1)}, u32[]{:S(2)}, u32[]{:S(2)}) %collective-permute-start.10) | collective-permute-done | bytes 262176 | tf_op jit(solution)/shard_map/ppermute | solution.py:40
  218.4 9.3 %collective-permute-done.11 = bf16[128,1024]{1,0:T(8,128)(2,1)S(1)} collective-permute-done((bf16[128,1024]{1,0:T(8,128)(2,1)S(1)}, bf16[128,1024]{1,0:T(8,128)(2,1)S(1)}, u32[]{:S(2)}, u32[]{:S(2)}) %collective-permute-start.11) | collective-permute-done | bytes 262176 | tf_op jit(solution)/shard_map/ppermute | solution.py:40
  228.1 2.1 fusion.29
  231.0 80.4 %all-gather.5.cloned.1.call-done = bf16[4096,2,256]{0,2,1:T(8,128)(2,1)} async-done(((bf16[128,2,256]{0,2,1:T(8,128)(2,1)}), bf16[4096,2,256]{0,2,1:T(8,128)(2,1)}) %all-gather.5.cloned.1.call-update) | async-done | bytes 4194320 | tf_op jit(solution)/shard_map/all_gather | solution.py:113
  311.4 3.2 constant_dynamic-slice_fusion
  316.9 3.7 fusion.37
  320.8 1.3 collective-permute-start.13
  322.1 4.0 collective-permute-done.13
  326.2 2.8 collective-permute-start.14
  329.0 6.0 %collective-permute-done.14 = bf16[128,1024]{1,0:T(8,128)(2,1)S(1)} collective-permute-done((bf16[128,1024]{1,0:T(8,128)(2,1)S(1)}, bf16[128,1024]{1,0:T(8,128)(2,1)S(1)}, u32[]{:S(2)}, u32[]{:S(2)}) %collective-permute-start.14) | collective-permute-done | bytes 262176 | tf_op jit(solution)/shard_map/ppermute | solution.py:40
  335.8 23.4 %all_to_all.20 = bf16[16,20,1024]{2,1,0:T(8,128)(2,1)S(1)} all-to-all(bf16[16,20,1024]{2,1,0:T(8,128)(2,1)S(1)} %reshape.394), channel_id=1, replica_groups=mesh['section'=2,'tz'=16,'tp'=2,'rep'=4] {'tz'}, dimensions={0} | all-to-all | bytes 1310720 | tf_op jit(solution)/shard_map/all_to_all | solution.py:150
  360.2 9.9 %collective-permute-done.15 = bf16[16,20,1024]{2,0,1:T(8,128)(2,1)S(1)} collective-permute-done((bf16[16,20,1024]{2,0,1:T(8,128)(2,1)S(1)}, bf16[16,20,1024]{2,0,1:T(8,128)(2,1)S(1)}, u32[]{:S(2)}, u32[]{:S(2)}) %collective-permute-start.15) | collective-permute-done | bytes 655392 | tf_op jit(solution)/shard_map/ppermute | solution.py:153
  371.0 2.8 fusion.18
  375.2 1.3 copy.55
  377.3 9.2 %collective-permute-done.16 = bf16[16,20,1024]{2,0,1:T(8,128)(2,1)} collective-permute-done((bf16[16,20,1024]{2,0,1:T(8,128)(2,1)}, bf16[16,20,1024]{2,0,1:T(8,128)(2,1)}, u32[]{:S(2)}, u32[]{:S(2)}) %collective-permute-start.16) | collective-permute-done | bytes 655392 | tf_op jit(solution)/shard_map/ppermute | solution.py:159
  386.5 2.4 add_convert_fusion
  389.0 6.0 %all-to-all-start.3 = ((bf16[16,20,1024]{2,1,0:T(8,128)(2,1)}), bf16[16,20,1024]{2,1,0:T(8,128)(2,1)S(1)}, u32[]{:S(2)}, u32[]{:S(2)}) async-start(bf16[16,20,1024]{2,1,0:T(8,128)(2,1)} %add_convert_fusion), calls=%async_computation.3 | async-start | bytes 1572864 | tf_op jit(solution)/shard_map/all_to_all | solution.py:161
  395.2 15.9 %all-to-all-done.3 = bf16[16,20,1024]{2,1,0:T(8,128)(2,1)S(1)} async-done(((bf16[16,20,1024]{2,1,0:T(8,128)(2,1)}), bf16[16,20,1024]{2,1,0:T(8,128)(2,1)S(1)}, u32[]{:S(2)}, u32[]{:S(2)}) %all-to-all-start.3) | async-done | bytes 655392 | tf_op jit(solution)/shard_map/all_to_all | solution.py:161
  413.5 4.7 %collective-permute-done.17 = bf16[128,1024]{1,0:T(8,128)(2,1)S(1)} collective-permute-done((bf16[128,1024]{1,0:T(8,128)(2,1)S(1)}, bf16[128,1024]{1,0:T(8,128)(2,1)S(1)}, u32[]{:S(2)}, u32[]{:S(2)}) %collective-permute-start.17) | collective-permute-done | bytes 262176 | tf_op jit(solution)/shard_map/ppermute | solution.py:40
  418.3 2.9 collective-permute-start.18
  423.6 15.7 %collective-permute-start.20 = (bf16[1,128,2,256]{1,3,2,0:T(8,128)(2,1)S(1)}, bf16[1,128,2,256]{1,3,2,0:T(8,128)(2,1)S(1)}, u32[]{:S(2)}, u32[]{:S(2)}) collective-permute-start(bf16[1,128,2,256]{1,3,2,0:T(8,128)(2,1)S(1)} %get-tuple-element.16), channel_id=1, source_target_pairs={{128,0},{129,1},{130,2},{131,3},{132,4},{133,5},{134,6},{135,7},{1... | collective-permute-start | bytes 393224 | tf_op jit(solution)/shard_map/ppermute | solution.py:210
  439.3 1.3 collective-permute-start.12
  440.9 1.3 collective-permute-start.19
  443.3 1.3 collective-permute-start.21
  444.6 1.9 collective-permute-done.21
  (167 shorter events, 31.9 us)
Async XLA Ops:
  7.2 6.0 %copy-start.18 = (f32[1,2,1024]{2,1,0:T(2,128)S(1)}, f32[1,2,1024]{2,1,0:T(2,128)}, u32[]{:S(2)}) copy-start(f32[1,2,1024]{2,1,0:T(2,128)} %param.16) | copy-start | bytes 24580
  7.2 6.0 %copy-start.12 = (bf16[2,128,1024]{2,1,0:T(8,128)(2,1)S(1)}, bf16[2,128,1024]{2,1,0:T(8,128)(2,1)}, u32[]{:S(2)}) copy-start(bf16[2,128,1024]{2,1,0:T(8,128)(2,1)} %param.12) | copy-start | bytes 1572868
  7.2 94.5 %all-gather.3.cloned.1.call-start = ((), (), s32[]{:S(2)}) async-start(), calls=%async_computation.4 | async-start | bytes 4325376 | tf_op jit(solution)/shard_map/all_gather | solution.py:113
  9.9 6.5 %collective-permute-start.1 = (bf16[1024,768]{0,1:T(8,128)(2,1)}, bf16[1024,768]{0,1:T(8,128)(2,1)S(1)}, u32[]{:S(2)}, u32[]{:S(2)}) collective-permute-start(bf16[1024,768]{0,1:T(8,128)(2,1)} %bitcast.6), channel_id=1, source_target_pairs={{0,128},{128,0},{1,129},{129,1},{2,130},{130,2},{3,131},{131,3},{4... | collective-permute-start | bytes 4718600 | tf_op jit(solution)/shard_map/ppermute | solution.py:194
  13.1 3.3 collective-permute-start
  17.6 3.0 copy-start.8
  17.6 3.5 copy-start.17
  17.6 5.1 %copy-start.19 = (s32[2,128,2]{1,2,0:T(2,128)S(1)}, s32[2,128,2]{1,2,0:T(2,128)}, u32[]{:S(2)}) copy-start(s32[2,128,2]{1,2,0:T(2,128)} %param.14) | copy-start | bytes 6148
  20.6 90.2 %collective-permute-start.2 = (bf16[256,1024]{1,0:T(8,128)(2,1)S(1)}, bf16[256,1024]{1,0:T(8,128)(2,1)S(1)}, u32[]{:S(2)}, u32[]{:S(2)}) collective-permute-start(bf16[256,1024]{1,0:T(8,128)(2,1)S(1)} %bitcast.199), channel_id=1, source_target_pairs={{0,128},{128,0},{1,129},{129,1},{2,130},{130,2},{3,131},{131,3},{4... | collective-permute-start | bytes 1572872 | tf_op jit(solution)/shard_map/ppermute | solution.py:194
  110.8 14.6 %copy-start.10 = (bf16[256,1024]{1,0:T(8,128)(2,1)}, bf16[256,1024]{1,0:T(8,128)(2,1)S(1)}, u32[]{:S(2)}) copy-start(bf16[256,1024]{1,0:T(8,128)(2,1)S(1)} %collective-permute-done.2) | copy-start | bytes 1572868
  111.1 5.3 %collective-permute-start.3 = (bf16[128,1024]{1,0:T(8,128)(2,1)S(1)}, bf16[128,1024]{1,0:T(8,128)(2,1)S(1)}, u32[]{:S(2)}, u32[]{:S(2)}) collective-permute-start(bf16[128,1024]{1,0:T(8,128)(2,1)S(1)} %convolution_convert_fusion.5), channel_id=1, source_target_pairs={{0,1},{1,0},{2,3},{3,2},{4,5},{5,4},{6,7},{7,6},{8,9},{9,8},{10,11... | collective-permute-start | bytes 786440 | tf_op jit(solution)/shard_map/ppermute | solution.py:40
  116.5 8.8 %collective-permute-start.4 = (bf16[128,1024]{1,0:T(8,128)(2,1)S(1)}, bf16[128,1024]{1,0:T(8,128)(2,1)S(1)}, u32[]{:S(2)}, u32[]{:S(2)}) collective-permute-start(bf16[128,1024]{1,0:T(8,128)(2,1)S(1)} %add_convert_fusion.7), channel_id=1, source_target_pairs={{0,2},{1,3},{2,0},{3,1},{4,6},{5,7},{6,4},{7,5},{8,10},{9,11},{10,... | collective-permute-start | bytes 786440 | tf_op jit(solution)/shard_map/ppermute | solution.py:40
  119.5 7.5 %copy-start.14 = (s32[128,320]{0,1:T(8,128)}, s32[128,320]{0,1:T(8,128)S(1)}, u32[]{:S(2)}) copy-start(s32[128,320]{0,1:T(8,128)S(1)} %convert_reduce_fusion) | copy-start | bytes 491524
  127.0 23.4 %all-to-all-start = ((bf16[16,20,1024]{2,1,0:T(8,128)(2,1)}), bf16[16,20,1024]{2,1,0:T(8,128)(2,1)S(1)}, u32[]{:S(2)}, u32[]{:S(2)}) async-start(bf16[16,20,1024]{2,1,0:T(8,128)(2,1)} %reshape.388), calls=%async_computation | async-start | bytes 1572864 | tf_op jit(solution)/shard_map/all_to_all | solution.py:150
  134.1 28.3 %collective-permute-start.7 = (bf16[1,1024,2,352]{1,3,2,0:T(8,128)(2,1)}, bf16[1,1024,2,352]{1,3,2,0:T(8,128)(2,1)}, u32[]{:S(2)}, u32[]{:S(2)}) collective-permute-start(bf16[1,1024,2,352]{1,3,2,0:T(8,128)(2,1)} %bitcast.222), channel_id=1, source_target_pairs={{0,128},{128,0},{1,129},{129,1},{2,130},{130,2},{3,131},{131,3},{4... | collective-permute-start | bytes 4325384 | tf_op jit(solution)/shard_map/ppermute | solution.py:194
  150.7 10.8 %collective-permute-start.6 = (bf16[16,20,1024]{2,0,1:T(8,128)(2,1)S(1)}, bf16[16,20,1024]{2,0,1:T(8,128)(2,1)S(1)}, u32[]{:S(2)}, u32[]{:S(2)}) collective-permute-start(bf16[16,20,1024]{2,0,1:T(8,128)(2,1)S(1)} %copy.48), channel_id=1, source_target_pairs={{0,4},{4,0},{1,5},{5,1},{2,6},{6,2},{3,7},{7,3},{8,12},{12,8},{9,1... | collective-permute-start | bytes 1966088 | tf_op jit(solution)/shard_map/ppermute | solution.py:153
  150.9 14.8 %collective-permute-start.8 = (bf16[1,352,1024]{2,1,0:T(8,128)(2,1)}, bf16[1,352,1024]{2,1,0:T(8,128)(2,1)}, u32[]{:S(2)}, u32[]{:S(2)}) collective-permute-start(bf16[1,352,1024]{2,1,0:T(8,128)(2,1)} %bitcast.223), channel_id=1, source_target_pairs={{0,128},{128,0},{1,129},{129,1},{2,130},{130,2},{3,131},{131,3},{4... | collective-permute-start | bytes 2162696 | tf_op jit(solution)/shard_map/ppermute | solution.py:194
  162.4 3.2 copy-start.23
  169.4 9.8 %collective-permute-start.9 = (bf16[16,20,1024]{2,0,1:T(8,128)(2,1)}, bf16[16,20,1024]{2,0,1:T(8,128)(2,1)}, u32[]{:S(2)}, u32[]{:S(2)}) collective-permute-start(bf16[16,20,1024]{2,0,1:T(8,128)(2,1)} %copy.50), channel_id=1, source_target_pairs={{0,4},{4,0},{1,5},{5,1},{2,6},{6,2},{3,7},{7,3},{8,12},{12,8},{9,1... | collective-permute-start | bytes 1966088 | tf_op jit(solution)/shard_map/ppermute | solution.py:159
  170.6 22.4 %copy-start.16 = (bf16[1,1024,16]{1,2,0:T(8,128)(2,1)S(1)}, bf16[1,1024,16]{1,2,0:T(8,128)(2,1)}, u32[]{:S(2)}) copy-start(bf16[1,1024,16]{1,2,0:T(8,128)(2,1)} %param.19) | copy-start | bytes 98308
  170.6 28.3 %copy-start.3 = (bf16[128,1024]{1,0:T(8,128)(2,1)S(1)}, bf16[128,1024]{1,0:T(8,128)(2,1)}, u32[]{:S(2)}) copy-start(bf16[128,1024]{1,0:T(8,128)(2,1)} %copy-done.2) | copy-start | bytes 786436
  181.5 29.4 %all-to-all-start.1 = ((bf16[16,20,1024]{2,1,0:T(8,128)(2,1)}), bf16[16,20,1024]{2,1,0:T(8,128)(2,1)S(1)}, u32[]{:S(2)}, u32[]{:S(2)}) async-start(bf16[16,20,1024]{2,1,0:T(8,128)(2,1)} %add_convert_fusion.1), calls=%async_computation.1 | async-start | bytes 1572864 | tf_op jit(solution)/shard_map/all_to_all | solution.py:161
  193.0 118.4 %all-gather.5.cloned.1.call-start = ((), (), s32[]{:S(2)}) async-start(), calls=%async_computation.5 | async-start | bytes 4325376 | tf_op jit(solution)/shard_map/all_gather | solution.py:113
  193.0 5.9 %collective-permute-start.5 = (bf16[1024,16]{0,1:T(8,128)(2,1)S(1)}, bf16[1024,16]{0,1:T(8,128)(2,1)S(1)}, u32[]{:S(2)}, u32[]{:S(2)}) collective-permute-start(bf16[1024,16]{0,1:T(8,128)(2,1)S(1)} %bitcast.213), channel_id=1, source_target_pairs={{0,128},{128,0},{1,129},{129,1},{2,130},{130,2},{3,131},{131,3},{4... | collective-permute-start | bytes 98312 | tf_op jit(solution)/shard_map/ppermute | solution.py:194
  212.3 15.4 %copy-start.1 = (bf16[128,1024]{1,0:T(8,128)(2,1)S(1)}, bf16[128,1024]{1,0:T(8,128)(2,1)}, u32[]{:S(2)}) copy-start(bf16[128,1024]{1,0:T(8,128)(2,1)} %copy-done) | copy-start | bytes 786436
  212.3 15.4 %copy-start.13 = (bf16[2,128,1024]{2,1,0:T(8,128)(2,1)S(1)}, bf16[2,128,1024]{2,1,0:T(8,128)(2,1)}, u32[]{:S(2)}) copy-start(bf16[2,128,1024]{2,1,0:T(8,128)(2,1)} %param.12) | copy-start | bytes 1572868
  212.3 15.8 %copy-start.22 = (bf16[1024,768]{0,1:T(8,128)(2,1)S(1)}, bf16[1024,768]{0,1:T(8,128)(2,1)}, u32[]{:S(2)}) copy-start(bf16[1024,768]{0,1:T(8,128)(2,1)} %copy-done.21) | copy-start | bytes 4718596
  212.4 5.6 %collective-permute-start.10 = (bf16[128,1024]{1,0:T(8,128)(2,1)S(1)}, bf16[128,1024]{1,0:T(8,128)(2,1)S(1)}, u32[]{:S(2)}, u32[]{:S(2)}) collective-permute-start(bf16[128,1024]{1,0:T(8,128)(2,1)S(1)} %multiply_reduce_fusion.1), channel_id=1, source_target_pairs={{0,1},{1,0},{2,3},{3,2},{4,5},{5,4},{6,7},{7,6},{8,9},{9,8},{10,11... | collective-permute-start | bytes 786440 | tf_op jit(solution)/shard_map/ppermute | solution.py:40
  218.1 9.6 %collective-permute-start.11 = (bf16[128,1024]{1,0:T(8,128)(2,1)S(1)}, bf16[128,1024]{1,0:T(8,128)(2,1)S(1)}, u32[]{:S(2)}, u32[]{:S(2)}) collective-permute-start(bf16[128,1024]{1,0:T(8,128)(2,1)S(1)} %add_convert_fusion.6), channel_id=1, source_target_pairs={{0,2},{1,3},{2,0},{3,1},{4,6},{5,7},{6,4},{7,5},{8,10},{9,11},{10,... | collective-permute-start | bytes 786440 | tf_op jit(solution)/shard_map/ppermute | solution.py:40
  316.8 3.7 copy-start.9
  316.8 3.7 copy-start.11
  320.8 14.5 %copy-start.15 = (s32[128,320]{0,1:T(8,128)S(1)}, s32[128,320]{0,1:T(8,128)}, u32[]{:S(2)}) copy-start(s32[128,320]{0,1:T(8,128)} %copy-done.14) | copy-start | bytes 491524
  320.8 5.3 %collective-permute-start.13 = (bf16[128,1024]{1,0:T(8,128)(2,1)S(1)}, bf16[128,1024]{1,0:T(8,128)(2,1)S(1)}, u32[]{:S(2)}, u32[]{:S(2)}) collective-permute-start(bf16[128,1024]{1,0:T(8,128)(2,1)S(1)} %convolution_convert_fusion.4), channel_id=1, source_target_pairs={{0,1},{1,0},{2,3},{3,2},{4,5},{5,4},{6,7},{7,6},{8,9},{9,8},{10,11... | collective-permute-start | bytes 786440 | tf_op jit(solution)/shard_map/ppermute | solution.py:40
  326.2 8.8 %collective-permute-start.14 = (bf16[128,1024]{1,0:T(8,128)(2,1)S(1)}, bf16[128,1024]{1,0:T(8,128)(2,1)S(1)}, u32[]{:S(2)}, u32[]{:S(2)}) collective-permute-start(bf16[128,1024]{1,0:T(8,128)(2,1)S(1)} %add_convert_fusion.4), channel_id=1, source_target_pairs={{0,2},{1,3},{2,0},{3,1},{4,6},{5,7},{6,4},{7,5},{8,10},{9,11},{10,... | collective-permute-start | bytes 786440 | tf_op jit(solution)/shard_map/ppermute | solution.py:40
  335.3 23.9 %copy-start.4 = (bf16[128,1024]{1,0:T(8,128)(2,1)}, bf16[128,1024]{1,0:T(8,128)(2,1)S(1)}, u32[]{:S(2)}) copy-start(bf16[128,1024]{1,0:T(8,128)(2,1)S(1)} %multiply_convert_fusion) | copy-start | bytes 786436
  359.6 10.5 %collective-permute-start.15 = (bf16[16,20,1024]{2,0,1:T(8,128)(2,1)S(1)}, bf16[16,20,1024]{2,0,1:T(8,128)(2,1)S(1)}, u32[]{:S(2)}, u32[]{:S(2)}) collective-permute-start(bf16[16,20,1024]{2,0,1:T(8,128)(2,1)S(1)} %copy.53), channel_id=1, source_target_pairs={{0,4},{4,0},{1,5},{5,1},{2,6},{6,2},{3,7},{7,3},{8,12},{12,8},{9,1... | collective-permute-start | bytes 1966088 | tf_op jit(solution)/shard_map/ppermute | solution.py:153
  371.0 2.8 copy-start.24
  376.4 10.1 %collective-permute-start.16 = (bf16[16,20,1024]{2,0,1:T(8,128)(2,1)}, bf16[16,20,1024]{2,0,1:T(8,128)(2,1)}, u32[]{:S(2)}, u32[]{:S(2)}) collective-permute-start(bf16[16,20,1024]{2,0,1:T(8,128)(2,1)} %copy.55), channel_id=1, source_target_pairs={{0,4},{4,0},{1,5},{5,1},{2,6},{6,2},{3,7},{7,3},{8,12},{12,8},{9,1... | collective-permute-start | bytes 1966088 | tf_op jit(solution)/shard_map/ppermute | solution.py:159
  377.3 17.6 %copy-start.5 = (bf16[128,1024]{1,0:T(8,128)(2,1)S(1)}, bf16[128,1024]{1,0:T(8,128)(2,1)}, u32[]{:S(2)}) copy-start(bf16[128,1024]{1,0:T(8,128)(2,1)} %copy-done.4) | copy-start | bytes 786436
  389.0 22.1 %all-to-all-start.3 = ((bf16[16,20,1024]{2,1,0:T(8,128)(2,1)}), bf16[16,20,1024]{2,1,0:T(8,128)(2,1)S(1)}, u32[]{:S(2)}, u32[]{:S(2)}) async-start(bf16[16,20,1024]{2,1,0:T(8,128)(2,1)} %add_convert_fusion), calls=%async_computation.3 | async-start | bytes 1572864 | tf_op jit(solution)/shard_map/all_to_all | solution.py:161
  412.5 8.8 %copy-start.20 = (s32[2,32]{1,0:T(2,128)S(1)}, s32[2,32]{1,0:T(2,128)}, u32[]{:S(2)}) copy-start(s32[2,32]{1,0:T(2,128)} %param.15) | copy-start | bytes 772
  412.5 28.2 %copy-start.7 = (bf16[128,1024]{1,0:T(8,128)(2,1)S(1)}, bf16[128,1024]{1,0:T(8,128)(2,1)}, u32[]{:S(2)}) copy-start(bf16[128,1024]{1,0:T(8,128)(2,1)} %copy-done.6) | copy-start | bytes 786436
  412.6 5.6 %collective-permute-start.17 = (bf16[128,1024]{1,0:T(8,128)(2,1)S(1)}, bf16[128,1024]{1,0:T(8,128)(2,1)S(1)}, u32[]{:S(2)}, u32[]{:S(2)}) collective-permute-start(bf16[128,1024]{1,0:T(8,128)(2,1)S(1)} %multiply_reduce_fusion), channel_id=1, source_target_pairs={{0,1},{1,0},{2,3},{3,2},{4,5},{5,4},{6,7},{7,6},{8,9},{9,8},{10,11... | collective-permute-start | bytes 786440 | tf_op jit(solution)/shard_map/ppermute | solution.py:40
  418.3 22.4 %collective-permute-start.18 = (bf16[128,1024]{1,0:T(8,128)(2,1)S(1)}, bf16[128,1024]{1,0:T(8,128)(2,1)S(1)}, u32[]{:S(2)}, u32[]{:S(2)}) collective-permute-start(bf16[128,1024]{1,0:T(8,128)(2,1)S(1)} %add_convert_fusion.3), channel_id=1, source_target_pairs={{0,2},{1,3},{2,0},{3,1},{4,6},{5,7},{6,4},{7,5},{8,10},{9,11},{10,... | collective-permute-start | bytes 786440 | tf_op jit(solution)/shard_map/ppermute | solution.py:40
  423.6 21.0 %collective-permute-start.20 = (bf16[1,128,2,256]{1,3,2,0:T(8,128)(2,1)S(1)}, bf16[1,128,2,256]{1,3,2,0:T(8,128)(2,1)S(1)}, u32[]{:S(2)}, u32[]{:S(2)}) collective-permute-start(bf16[1,128,2,256]{1,3,2,0:T(8,128)(2,1)S(1)} %get-tuple-element.16), channel_id=1, source_target_pairs={{128,0},{129,1},{130,2},{131,3},{132,4},{133,5},{134,6},{135,7},{1... | collective-permute-start | bytes 393224 | tf_op jit(solution)/shard_map/ppermute | solution.py:210
  439.3 8.1 %collective-permute-start.12 = (bf16[128,1024]{1,0:T(8,128)(2,1)S(1)}, bf16[128,1024]{1,0:T(8,128)(2,1)S(1)}, u32[]{:S(2)}, u32[]{:S(2)}) collective-permute-start(bf16[128,1024]{1,0:T(8,128)(2,1)S(1)} %get-tuple-element.10), channel_id=1, source_target_pairs={{128,0},{129,1},{130,2},{131,3},{132,4},{133,5},{134,6},{135,7},{1... | collective-permute-start | bytes 786440 | tf_op jit(solution)/shard_map/ppermute | solution.py:209
  440.9 6.6 %collective-permute-start.19 = (bf16[128,1024]{1,0:T(8,128)(2,1)S(1)}, bf16[128,1024]{1,0:T(8,128)(2,1)S(1)}, u32[]{:S(2)}, u32[]{:S(2)}) collective-permute-start(bf16[128,1024]{1,0:T(8,128)(2,1)S(1)} %add_convert_fusion.2), channel_id=1, source_target_pairs={{0,128},{1,129},{2,130},{3,131},{4,132},{5,133},{6,134},{7,135},{8... | collective-permute-start | bytes 786440 | tf_op jit(solution)/shard_map/ppermute | solution.py:211
  443.3 3.3 collective-permute-start.21
  (4 other events, 5.1 us)
Sparse Core Ops, SparseCore 0:
  20.7 80.8 all-gather.2
  231.1 80.1 all-gather.4

commit v7 on v6

--- a/solution.py
+++ b/solution.py
@@ -33,15 +33,14 @@
 
 def rep_sum(values):
     count = lax.axis_size("rep")
-    total = values.astype(jnp.bfloat16)
-    stride = 1
-    while stride < count:
-        pairs = [(index, index ^ stride) for index in range(count)]
-        partner = lax.ppermute(total, "rep", pairs)
-        summed = total.astype(jnp.float32) + partner.astype(jnp.float32)
-        stride = stride * 2
-        total = summed.astype(jnp.bfloat16) if stride < count else summed
-    return total
+    own = values.astype(jnp.bfloat16)
+    if count != 4:
+        return lax.psum(own.astype(jnp.float32), "rep")
+    heard = [
+        lax.ppermute(own, "rep", [(index, index ^ mask) for index in range(count)]).astype(jnp.float32)
+        for mask in (1, 2, 3)
+    ]
+    return (own.astype(jnp.float32) + heard[0]) + (heard[1] + heard[2])
 
 
 def attend(carry, queries, keys_vals, seg_query, pos_query, seg_key, pos_key):

time: 465 us -> 462 us (level)
  starting transfers between devices: 86 us -> 92.8 us
  waiting for transfers between devices: 267 us -> 262 us
    ppermute x8 -> x12, starting transfers between devices: 12.5 us -> 23.7 us  [rep_sum(): lax.ppermute(own, 'rep', [(index, index ^ mask) for index in range(count)])]
    ppermute x8 -> x12, waiting for transfers between devices: 38.4 us -> 27.7 us  [rep_sum(): lax.ppermute(own, 'rep', [(index, index ^ mask) for index in range(count)])]
    ppermute x1, starting transfers between devices: 15.7 us -> 10.9 us  [per_device(): gotp0 = lax.ppermute(pages0, 'section', [(1, 0)])]
    ppermute x6, starting transfers between devices: 26.7 us -> 22 us  [per_device(): other = tuple((lax.ppermute(w, 'section', swap) for w in own))]
    all_to_all x2, starting transfers between devices: 17.4 us -> 22.1 us  [one_layer(): lax.all_to_all(halves, 'tz', split_axis=0, concat_axis=0, tiled=True)]
  transfers between devices with their start and end apart: 27 -> 31, of which waited for: 19 -> 17; matrix products, arithmetic and copies ran while one was open for 5% -> 5% of each run, Pallas kernels for 0% -> 0%
where the time goes in v7:
time: 462 us; the launch traced here: 454 us
  waiting for transfers between devices  262 us (57%)
  starting transfers between devices  92.8 us (20%)
  matrix products  23.7 us (5%)
  blocking collectives  22 us (5%)
  local copies, waits for them, and re-layouts  21.2 us (5%)
  between operations  16.6 us (4%)
  other arithmetic  16.4 us (4%)
    all_gather x2, waiting for transfers between devices, one_layer(): piece = lax.all_gather(keys_vals, ('tz', 'tp'), axis=0, tiled=True)  160 us
    all_to_all x2, waiting for transfers between devices, one_layer(): lax.all_to_all(halves, 'tz', split_axis=0, concat_axis=0, tiled=True)  31.9 us
    ppermute x12, waiting for transfers between devices, rep_sum(): lax.ppermute(own, 'rep', [(index, index ^ mask) for index in range(count)])  27.7 us
    ppermute x12, starting transfers between devices, rep_sum(): lax.ppermute(own, 'rep', [(index, index ^ mask) for index in range(count)])  23.7 us
    all_to_all x2, starting transfers between devices, one_layer(): lax.all_to_all(halves, 'tz', split_axis=0, concat_axis=0, tiled=True)  22.1 us
    all_to_all x1, blocking collectives, one_layer(): lax.all_to_all(dispatch.reshape(experts_all, CAP, width), 'tz', split_axi...  22 us
    ppermute x6, starting transfers between devices, per_device(): other = tuple((lax.ppermute(w, 'section', swap) for w in own))  22 us
    ppermute x2, waiting for transfers between devices, one_layer(): pair_out = lax.ppermute(share_out[1], 'tp', pair_swap)  15.5 us
  transfers between devices with their start and end apart: 31, of which 17 were waited for; matrix products, arithmetic and copies ran while one was open for 5% of the time, Pallas kernels for 0%

profile of v7, /device:TPU:1, one launch (start us, length us, event | category | flops | bytes accessed | tf_op | source)
XLA Modules:
  0.0 454.4 jit_solution(4019332737204072410)
XLA Ops:
  7.2 1.8 copy.45
  9.0 3.3 collective-permute-start.1
  12.6 2.9 collective-permute-done
  15.5 2.1 fusion.26
  21.6 77.8 %all-gather.3.cloned.1.call-done = bf16[4096,2,256]{0,2,1:T(8,128)(2,1)} async-done(((bf16[128,2,256]{0,2,1:T(8,128)(2,1)}), bf16[4096,2,256]{0,2,1:T(8,128)(2,1)}) %all-gather.3.cloned.1.call-update) | async-done | bytes 4194320 | tf_op jit(solution)/shard_map/all_gather | solution.py:112
  99.4 3.2 constant_dynamic-slice_fusion.1
  104.8 3.7 fusion.39
  108.8 2.5 collective-permute-start.5
  112.3 9.5 %collective-permute-done.5 = bf16[128,1024]{1,0:T(8,128)(2,1)S(1)} collective-permute-done((bf16[128,1024]{1,0:T(8,128)(2,1)S(1)}, bf16[128,1024]{1,0:T(8,128)(2,1)S(1)}, u32[]{:S(2)}, u32[]{:S(2)}) %collective-permute-start.5) | collective-permute-done | bytes 262176 | tf_op jit(solution)/shard_map/ppermute | solution.py:40
  123.6 4.3 all-to-all-start
  127.9 6.4 %collective-permute-start.8 = (bf16[1,1024,2,352]{1,3,2,0:T(8,128)(2,1)}, bf16[1,1024,2,352]{1,3,2,0:T(8,128)(2,1)}, u32[]{:S(2)}, u32[]{:S(2)}) collective-permute-start(bf16[1,1024,2,352]{1,3,2,0:T(8,128)(2,1)} %bitcast.28), channel_id=1, source_target_pairs={{0,128},{128,0},{1,129},{129,1},{2,130},{130,2},{3,131},{131,3},{4... | collective-permute-start | bytes 4325384 | tf_op jit(solution)/shard_map/ppermute | solution.py:193
  134.3 10.8 %all-to-all-done = bf16[16,20,1024]{2,1,0:T(8,128)(2,1)S(1)} async-done(((bf16[16,20,1024]{2,1,0:T(8,128)(2,1)}), bf16[16,20,1024]{2,1,0:T(8,128)(2,1)S(1)}, u32[]{:S(2)}, u32[]{:S(2)}) %all-to-all-start) | async-done | bytes 655392 | tf_op jit(solution)/shard_map/all_to_all | solution.py:149
  146.3 8.3 %collective-permute-start.9 = (bf16[1,352,1024]{2,1,0:T(8,128)(2,1)}, bf16[1,352,1024]{2,1,0:T(8,128)(2,1)}, u32[]{:S(2)}, u32[]{:S(2)}) collective-permute-start(bf16[1,352,1024]{2,1,0:T(8,128)(2,1)} %bitcast.217), channel_id=1, source_target_pairs={{0,128},{128,0},{1,129},{129,1},{2,130},{130,2},{3,131},{131,3},{4... | collective-permute-start | bytes 2162696 | tf_op jit(solution)/shard_map/ppermute | solution.py:193
  156.2 1.2 reshape.428
  157.5 3.6 fusion.20
  161.1 2.2 convolution_convert_fusion.1
  163.2 1.3 fusion.134
  165.9 1.4 reshape.400
  167.3 7.4 %collective-permute-done.10 = bf16[16,20,1024]{2,0,1:T(8,128)(2,1)} collective-permute-done((bf16[16,20,1024]{2,0,1:T(8,128)(2,1)S(1)}, bf16[16,20,1024]{2,0,1:T(8,128)(2,1)}, u32[]{:S(2)}, u32[]{:S(2)}) %collective-permute-start.10) | collective-permute-done | bytes 655392 | tf_op jit(solution)/shard_map/ppermute | solution.py:158
  174.6 2.4 add_convert_fusion.1
  177.0 15.1 %all-to-all-start.1 = ((bf16[16,20,1024]{2,1,0:T(8,128)(2,1)}), bf16[16,20,1024]{2,1,0:T(8,128)(2,1)S(1)}, u32[]{:S(2)}, u32[]{:S(2)}) async-start(bf16[16,20,1024]{2,1,0:T(8,128)(2,1)} %add_convert_fusion.1), calls=%async_computation.1 | async-start | bytes 1572864 | tf_op jit(solution)/shard_map/all_to_all | solution.py:160
  192.2 3.7 collective-permute-start.6
  197.1 16.1 %all-to-all-done.1 = bf16[16,20,1024]{2,1,0:T(8,128)(2,1)S(1)} async-done(((bf16[16,20,1024]{2,1,0:T(8,128)(2,1)}), bf16[16,20,1024]{2,1,0:T(8,128)(2,1)S(1)}, u32[]{:S(2)}, u32[]{:S(2)}) %all-to-all-start.1) | async-done | bytes 655392 | tf_op jit(solution)/shard_map/all_to_all | solution.py:160
  214.7 5.7 %collective-permute-start.11 = (bf16[128,1024]{1,0:T(8,128)(2,1)S(1)}, bf16[128,1024]{1,0:T(8,128)(2,1)S(1)}, u32[]{:S(2)}, u32[]{:S(2)}) collective-permute-start(bf16[128,1024]{1,0:T(8,128)(2,1)S(1)} %multiply_reduce_fusion.1), channel_id=1, source_target_pairs={{0,1},{1,0},{2,3},{3,2},{4,5},{5,4},{6,7},{7,6},{8,9},{9,8},{10,11... | collective-permute-start | bytes 786440 | tf_op jit(solution)/shard_map/ppermute | solution.py:40
  221.4 6.5 %collective-permute-done.11 = bf16[128,1024]{1,0:T(8,128)(2,1)S(1)} collective-permute-done((bf16[128,1024]{1,0:T(8,128)(2,1)S(1)}, bf16[128,1024]{1,0:T(8,128)(2,1)S(1)}, u32[]{:S(2)}, u32[]{:S(2)}) %collective-permute-start.11) | collective-permute-done | bytes 262176 | tf_op jit(solution)/shard_map/ppermute | solution.py:40
  227.9 1.3 collective-permute-done.13
  231.1 82.3 %all-gather.5.cloned.1.call-done = bf16[4096,2,256]{0,2,1:T(8,128)(2,1)} async-done(((bf16[128,2,256]{0,2,1:T(8,128)(2,1)}), bf16[4096,2,256]{0,2,1:T(8,128)(2,1)}) %all-gather.5.cloned.1.call-update) | async-done | bytes 4194320 | tf_op jit(solution)/shard_map/all_gather | solution.py:112
  313.4 3.2 constant_dynamic-slice_fusion
  318.9 3.7 fusion.37
  322.8 2.5 collective-permute-start.17
  326.2 9.7 %collective-permute-done.17 = bf16[128,1024]{1,0:T(8,128)(2,1)S(1)} collective-permute-done((bf16[128,1024]{1,0:T(8,128)(2,1)S(1)}, bf16[128,1024]{1,0:T(8,128)(2,1)S(1)}, u32[]{:S(2)}, u32[]{:S(2)}) %collective-permute-start.17) | collective-permute-done | bytes 262176 | tf_op jit(solution)/shard_map/ppermute | solution.py:40
  336.7 22.0 %all_to_all.20 = bf16[16,20,1024]{2,1,0:T(8,128)(2,1)S(1)} all-to-all(bf16[16,20,1024]{2,1,0:T(8,128)(2,1)S(1)} %reshape.394), channel_id=1, replica_groups=mesh['section'=2,'tz'=16,'tp'=2,'rep'=4] {'tz'}, dimensions={0} | all-to-all | bytes 1310720 | tf_op jit(solution)/shard_map/all_to_all | solution.py:149
  359.1 2.3 collective-permute-start.18
  361.4 8.2 %collective-permute-done.18 = bf16[16,20,1024]{2,0,1:T(8,128)(2,1)S(1)} collective-permute-done((bf16[16,20,1024]{2,0,1:T(8,128)(2,1)S(1)}, bf16[16,20,1024]{2,0,1:T(8,128)(2,1)S(1)}, u32[]{:S(2)}, u32[]{:S(2)}) %collective-permute-start.18) | collective-permute-done | bytes 655392 | tf_op jit(solution)/shard_map/ppermute | solution.py:152
  370.5 2.8 fusion.18
  374.6 1.3 copy.55
  375.9 1.8 collective-permute-start.19
  377.9 8.1 %collective-permute-done.19 = bf16[16,20,1024]{2,0,1:T(8,128)(2,1)} collective-permute-done((bf16[16,20,1024]{2,0,1:T(8,128)(2,1)}, bf16[16,20,1024]{2,0,1:T(8,128)(2,1)}, u32[]{:S(2)}, u32[]{:S(2)}) %collective-permute-start.19) | collective-permute-done | bytes 655392 | tf_op jit(solution)/shard_map/ppermute | solution.py:158
  386.0 2.5 add_convert_fusion
  388.5 7.0 %all-to-all-start.3 = ((bf16[16,20,1024]{2,1,0:T(8,128)(2,1)}), bf16[16,20,1024]{2,1,0:T(8,128)(2,1)S(1)}, u32[]{:S(2)}, u32[]{:S(2)}) async-start(bf16[16,20,1024]{2,1,0:T(8,128)(2,1)} %add_convert_fusion), calls=%async_computation.3 | async-start | bytes 1572864 | tf_op jit(solution)/shard_map/all_to_all | solution.py:160
  395.8 15.8 %all-to-all-done.3 = bf16[16,20,1024]{2,1,0:T(8,128)(2,1)S(1)} async-done(((bf16[16,20,1024]{2,1,0:T(8,128)(2,1)}), bf16[16,20,1024]{2,1,0:T(8,128)(2,1)S(1)}, u32[]{:S(2)}, u32[]{:S(2)}) %all-to-all-start.3) | async-done | bytes 655392 | tf_op jit(solution)/shard_map/all_to_all | solution.py:160
  413.2 1.4 collective-permute-start.21
  414.6 9.5 %collective-permute-start.20 = (bf16[128,1024]{1,0:T(8,128)(2,1)S(1)}, bf16[128,1024]{1,0:T(8,128)(2,1)S(1)}, u32[]{:S(2)}, u32[]{:S(2)}) collective-permute-start(bf16[128,1024]{1,0:T(8,128)(2,1)S(1)} %multiply_reduce_fusion), channel_id=1, source_target_pairs={{0,1},{1,0},{2,3},{3,2},{4,5},{5,4},{6,7},{7,6},{8,9},{9,8},{10,11... | collective-permute-start | bytes 786440 | tf_op jit(solution)/shard_map/ppermute | solution.py:40
  426.4 10.9 %collective-permute-start.24 = (bf16[1,128,2,256]{1,3,2,0:T(8,128)(2,1)S(1)}, bf16[1,128,2,256]{1,3,2,0:T(8,128)(2,1)S(1)}, u32[]{:S(2)}, u32[]{:S(2)}) collective-permute-start(bf16[1,128,2,256]{1,3,2,0:T(8,128)(2,1)S(1)} %get-tuple-element.20), channel_id=1, source_target_pairs={{128,0},{129,1},{130,2},{131,3},{132,4},{133,5},{134,6},{135,7},{1... | collective-permute-start | bytes 393224 | tf_op jit(solution)/shard_map/ppermute | solution.py:209
  437.3 1.3 collective-permute-start.14
  438.9 1.3 collective-permute-start.23
  441.2 1.3 collective-permute-start.25
  442.5 2.8 collective-permute-done.25
  (151 shorter events, 32.0 us)
Async XLA Ops:
  7.2 5.1 %copy-start.11 = (f32[1,2,1024]{2,1,0:T(2,128)S(1)}, f32[1,2,1024]{2,1,0:T(2,128)}, u32[]{:S(2)}) copy-start(f32[1,2,1024]{2,1,0:T(2,128)} %param.16) | copy-start | bytes 24580
  7.2 5.2 %copy-start.8 = (bf16[2,128,1024]{2,1,0:T(8,128)(2,1)S(1)}, bf16[2,128,1024]{2,1,0:T(8,128)(2,1)}, u32[]{:S(2)}) copy-start(bf16[2,128,1024]{2,1,0:T(8,128)(2,1)} %param.12) | copy-start | bytes 1572868
  7.2 92.2 %all-gather.3.cloned.1.call-start = ((), (), s32[]{:S(2)}) async-start(), calls=%async_computation.4 | async-start | bytes 4325376 | tf_op jit(solution)/shard_map/all_gather | solution.py:112
  9.0 8.7 %copy-start.6 = (bf16[1,1024,3,256]{1,3,2,0:T(8,128)(2,1)}, bf16[1,1024,3,256]{1,3,2,0:T(8,128)(2,1)S(1)}, u32[]{:S(2)}) copy-start(bf16[1,1024,3,256]{1,3,2,0:T(8,128)(2,1)S(1)} %copy.45) | copy-start | bytes 4718596
  9.0 6.5 %collective-permute-start.1 = (bf16[1024,768]{0,1:T(8,128)(2,1)S(1)}, bf16[1024,768]{0,1:T(8,128)(2,1)}, u32[]{:S(2)}, u32[]{:S(2)}) collective-permute-start(bf16[1024,768]{0,1:T(8,128)(2,1)S(1)} %bitcast.190), channel_id=1, source_target_pairs={{0,128},{128,0},{1,129},{129,1},{2,130},{130,2},{3,131},{131,3},{4... | collective-permute-start | bytes 4718600 | tf_op jit(solution)/shard_map/ppermute | solution.py:193
  12.3 3.2 collective-permute-start
  15.5 3.0 copy-start.2
  15.5 3.2 copy-start.10
  15.5 4.6 %copy-start.12 = (s32[2,128,2]{1,2,0:T(2,128)S(1)}, s32[2,128,2]{1,2,0:T(2,128)}, u32[]{:S(2)}) copy-start(s32[2,128,2]{1,2,0:T(2,128)} %param.14) | copy-start | bytes 6148
  18.6 89.9 %collective-permute-start.2 = (bf16[256,1024]{1,0:T(8,128)(2,1)S(1)}, bf16[256,1024]{1,0:T(8,128)(2,1)S(1)}, u32[]{:S(2)}, u32[]{:S(2)}) collective-permute-start(bf16[256,1024]{1,0:T(8,128)(2,1)S(1)} %bitcast.189), channel_id=1, source_target_pairs={{0,128},{128,0},{1,129},{129,1},{2,130},{130,2},{3,131},{131,3},{4... | collective-permute-start | bytes 1572872 | tf_op jit(solution)/shard_map/ppermute | solution.py:193
  108.5 13.6 %copy-start.4 = (bf16[256,1024]{1,0:T(8,128)(2,1)}, bf16[256,1024]{1,0:T(8,128)(2,1)S(1)}, u32[]{:S(2)}) copy-start(bf16[256,1024]{1,0:T(8,128)(2,1)S(1)} %collective-permute-done.2) | copy-start | bytes 1572868
  108.8 13.0 %collective-permute-start.5 = (bf16[128,1024]{1,0:T(8,128)(2,1)S(1)}, bf16[128,1024]{1,0:T(8,128)(2,1)S(1)}, u32[]{:S(2)}, u32[]{:S(2)}) collective-permute-start(bf16[128,1024]{1,0:T(8,128)(2,1)S(1)} %convolution_convert_fusion.5), channel_id=1, source_target_pairs={{0,3},{1,2},{2,1},{3,0},{4,7},{5,6},{6,5},{7,4},{8,11},{9,10},{10,... | collective-permute-start | bytes 786440 | tf_op jit(solution)/shard_map/ppermute | solution.py:40
  111.3 10.5 %collective-permute-start.4 = (bf16[128,1024]{1,0:T(8,128)(2,1)S(1)}, bf16[128,1024]{1,0:T(8,128)(2,1)S(1)}, u32[]{:S(2)}, u32[]{:S(2)}) collective-permute-start(bf16[128,1024]{1,0:T(8,128)(2,1)S(1)} %convolution_convert_fusion.5), channel_id=1, source_target_pairs={{0,2},{1,3},{2,0},{3,1},{4,6},{5,7},{6,4},{7,5},{8,10},{9,11},{10,... | collective-permute-start | bytes 786440 | tf_op jit(solution)/shard_map/ppermute | solution.py:40
  111.9 10.0 %collective-permute-start.3 = (bf16[128,1024]{1,0:T(8,128)(2,1)S(1)}, bf16[128,1024]{1,0:T(8,128)(2,1)S(1)}, u32[]{:S(2)}, u32[]{:S(2)}) collective-permute-start(bf16[128,1024]{1,0:T(8,128)(2,1)S(1)} %convolution_convert_fusion.5), channel_id=1, source_target_pairs={{0,1},{1,0},{2,3},{3,2},{4,5},{5,4},{6,7},{7,6},{8,9},{9,8},{10,11... | collective-permute-start | bytes 786440 | tf_op jit(solution)/shard_map/ppermute | solution.py:40
  123.6 21.5 %all-to-all-start = ((bf16[16,20,1024]{2,1,0:T(8,128)(2,1)}), bf16[16,20,1024]{2,1,0:T(8,128)(2,1)S(1)}, u32[]{:S(2)}, u32[]{:S(2)}) async-start(bf16[16,20,1024]{2,1,0:T(8,128)(2,1)} %reshape.388), calls=%async_computation | async-start | bytes 1572864 | tf_op jit(solution)/shard_map/all_to_all | solution.py:149
  127.9 29.6 %collective-permute-start.8 = (bf16[1,1024,2,352]{1,3,2,0:T(8,128)(2,1)}, bf16[1,1024,2,352]{1,3,2,0:T(8,128)(2,1)}, u32[]{:S(2)}, u32[]{:S(2)}) collective-permute-start(bf16[1,1024,2,352]{1,3,2,0:T(8,128)(2,1)} %bitcast.28), channel_id=1, source_target_pairs={{0,128},{128,0},{1,129},{129,1},{2,130},{130,2},{3,131},{131,3},{4... | collective-permute-start | bytes 4325384 | tf_op jit(solution)/shard_map/ppermute | solution.py:193
  145.4 10.2 %collective-permute-start.7 = (bf16[16,20,1024]{2,0,1:T(8,128)(2,1)S(1)}, bf16[16,20,1024]{2,0,1:T(8,128)(2,1)S(1)}, u32[]{:S(2)}, u32[]{:S(2)}) collective-permute-start(bf16[16,20,1024]{2,0,1:T(8,128)(2,1)S(1)} %copy.48), channel_id=1, source_target_pairs={{0,4},{4,0},{1,5},{5,1},{2,6},{6,2},{3,7},{7,3},{8,12},{12,8},{9,1... | collective-permute-start | bytes 1966088 | tf_op jit(solution)/shard_map/ppermute | solution.py:152
  146.3 14.8 %collective-permute-start.9 = (bf16[1,352,1024]{2,1,0:T(8,128)(2,1)}, bf16[1,352,1024]{2,1,0:T(8,128)(2,1)}, u32[]{:S(2)}, u32[]{:S(2)}) collective-permute-start(bf16[1,352,1024]{2,1,0:T(8,128)(2,1)} %bitcast.217), channel_id=1, source_target_pairs={{0,128},{128,0},{1,129},{129,1},{2,130},{130,2},{3,131},{131,3},{4... | collective-permute-start | bytes 2162696 | tf_op jit(solution)/shard_map/ppermute | solution.py:193
  157.4 3.6 copy-start.14
  165.0 9.6 %collective-permute-start.10 = (bf16[16,20,1024]{2,0,1:T(8,128)(2,1)S(1)}, bf16[16,20,1024]{2,0,1:T(8,128)(2,1)}, u32[]{:S(2)}, u32[]{:S(2)}) collective-permute-start(bf16[16,20,1024]{2,0,1:T(8,128)(2,1)S(1)} %copy.50), channel_id=1, source_target_pairs={{0,4},{4,0},{1,5},{5,1},{2,6},{6,2},{3,7},{7,3},{8,12},{12,8},{9,1... | collective-permute-start | bytes 1966088 | tf_op jit(solution)/shard_map/ppermute | solution.py:158
  167.2 24.9 %copy-start.9 = (bf16[1,1024,16]{1,2,0:T(8,128)(2,1)S(1)}, bf16[1,1024,16]{1,2,0:T(8,128)(2,1)}, u32[]{:S(2)}) copy-start(bf16[1,1024,16]{1,2,0:T(8,128)(2,1)} %param.19) | copy-start | bytes 98308
  177.0 36.1 %all-to-all-start.1 = ((bf16[16,20,1024]{2,1,0:T(8,128)(2,1)}), bf16[16,20,1024]{2,1,0:T(8,128)(2,1)S(1)}, u32[]{:S(2)}, u32[]{:S(2)}) async-start(bf16[16,20,1024]{2,1,0:T(8,128)(2,1)} %add_convert_fusion.1), calls=%async_computation.1 | async-start | bytes 1572864 | tf_op jit(solution)/shard_map/all_to_all | solution.py:160
  192.1 121.3 %all-gather.5.cloned.1.call-start = ((), (), s32[]{:S(2)}) async-start(), calls=%async_computation.5 | async-start | bytes 4325376 | tf_op jit(solution)/shard_map/all_gather | solution.py:112
  192.2 4.6 %collective-permute-start.6 = (bf16[1024,16]{0,1:T(8,128)(2,1)S(1)}, bf16[1024,16]{0,1:T(8,128)(2,1)S(1)}, u32[]{:S(2)}, u32[]{:S(2)}) collective-permute-start(bf16[1024,16]{0,1:T(8,128)(2,1)S(1)} %bitcast.204), channel_id=1, source_target_pairs={{0,128},{128,0},{1,129},{129,1},{2,130},{130,2},{3,131},{131,3},{4... | collective-permute-start | bytes 98312 | tf_op jit(solution)/shard_map/ppermute | solution.py:193
  214.5 15.1 %copy-start.7 = (bf16[1,1024,3,256]{1,3,2,0:T(8,128)(2,1)S(1)}, bf16[1,1024,3,256]{1,3,2,0:T(8,128)(2,1)}, u32[]{:S(2)}) copy-start(bf16[1,1024,3,256]{1,3,2,0:T(8,128)(2,1)} %copy-done.6) | copy-start | bytes 4718596
  214.6 6.8 %collective-permute-start.12 = (bf16[128,1024]{1,0:T(8,128)(2,1)S(1)}, bf16[128,1024]{1,0:T(8,128)(2,1)S(1)}, u32[]{:S(2)}, u32[]{:S(2)}) collective-permute-start(bf16[128,1024]{1,0:T(8,128)(2,1)S(1)} %multiply_reduce_fusion.1), channel_id=1, source_target_pairs={{0,2},{1,3},{2,0},{3,1},{4,6},{5,7},{6,4},{7,5},{8,10},{9,11},{10,... | collective-permute-start | bytes 786440 | tf_op jit(solution)/shard_map/ppermute | solution.py:40
  214.7 13.2 %collective-permute-start.11 = (bf16[128,1024]{1,0:T(8,128)(2,1)S(1)}, bf16[128,1024]{1,0:T(8,128)(2,1)S(1)}, u32[]{:S(2)}, u32[]{:S(2)}) collective-permute-start(bf16[128,1024]{1,0:T(8,128)(2,1)S(1)} %multiply_reduce_fusion.1), channel_id=1, source_target_pairs={{0,1},{1,0},{2,3},{3,2},{4,5},{5,4},{6,7},{7,6},{8,9},{9,8},{10,11... | collective-permute-start | bytes 786440 | tf_op jit(solution)/shard_map/ppermute | solution.py:40
  220.5 8.8 %collective-permute-start.13 = (bf16[128,1024]{1,0:T(8,128)(2,1)S(1)}, bf16[128,1024]{1,0:T(8,128)(2,1)S(1)}, u32[]{:S(2)}, u32[]{:S(2)}) collective-permute-start(bf16[128,1024]{1,0:T(8,128)(2,1)S(1)} %multiply_reduce_fusion.1), channel_id=1, source_target_pairs={{0,3},{1,2},{2,1},{3,0},{4,7},{5,6},{6,5},{7,4},{8,11},{9,10},{10,... | collective-permute-start | bytes 786440 | tf_op jit(solution)/shard_map/ppermute | solution.py:40
  229.5 106.3 %copy-start = (bf16[128,1024]{1,0:T(8,128)(2,1)}, bf16[128,1024]{1,0:T(8,128)(2,1)S(1)}, u32[]{:S(2)}) copy-start(bf16[128,1024]{1,0:T(8,128)(2,1)S(1)} %get-tuple-element.12) | copy-start | bytes 786436
  318.8 3.7 copy-start.3
  318.8 3.7 copy-start.5
  322.8 13.0 %collective-permute-start.17 = (bf16[128,1024]{1,0:T(8,128)(2,1)S(1)}, bf16[128,1024]{1,0:T(8,128)(2,1)S(1)}, u32[]{:S(2)}, u32[]{:S(2)}) collective-permute-start(bf16[128,1024]{1,0:T(8,128)(2,1)S(1)} %convolution_convert_fusion.4), channel_id=1, source_target_pairs={{0,3},{1,2},{2,1},{3,0},{4,7},{5,6},{6,5},{7,4},{8,11},{9,10},{10,... | collective-permute-start | bytes 786440 | tf_op jit(solution)/shard_map/ppermute | solution.py:40
  325.3 10.5 %collective-permute-start.16 = (bf16[128,1024]{1,0:T(8,128)(2,1)S(1)}, bf16[128,1024]{1,0:T(8,128)(2,1)S(1)}, u32[]{:S(2)}, u32[]{:S(2)}) collective-permute-start(bf16[128,1024]{1,0:T(8,128)(2,1)S(1)} %convolution_convert_fusion.4), channel_id=1, source_target_pairs={{0,2},{1,3},{2,0},{3,1},{4,6},{5,7},{6,4},{7,5},{8,10},{9,11},{10,... | collective-permute-start | bytes 786440 | tf_op jit(solution)/shard_map/ppermute | solution.py:40
  325.9 9.9 %collective-permute-start.15 = (bf16[128,1024]{1,0:T(8,128)(2,1)S(1)}, bf16[128,1024]{1,0:T(8,128)(2,1)S(1)}, u32[]{:S(2)}, u32[]{:S(2)}) collective-permute-start(bf16[128,1024]{1,0:T(8,128)(2,1)S(1)} %convolution_convert_fusion.4), channel_id=1, source_target_pairs={{0,1},{1,0},{2,3},{3,2},{4,5},{5,4},{6,7},{7,6},{8,9},{9,8},{10,11... | collective-permute-start | bytes 786440 | tf_op jit(solution)/shard_map/ppermute | solution.py:40
  359.1 10.5 %collective-permute-start.18 = (bf16[16,20,1024]{2,0,1:T(8,128)(2,1)S(1)}, bf16[16,20,1024]{2,0,1:T(8,128)(2,1)S(1)}, u32[]{:S(2)}, u32[]{:S(2)}) collective-permute-start(bf16[16,20,1024]{2,0,1:T(8,128)(2,1)S(1)} %copy.53), channel_id=1, source_target_pairs={{0,4},{4,0},{1,5},{5,1},{2,6},{6,2},{3,7},{7,3},{8,12},{12,8},{9,1... | collective-permute-start | bytes 1966088 | tf_op jit(solution)/shard_map/ppermute | solution.py:152
  370.4 2.8 copy-start.15
  375.9 10.1 %collective-permute-start.19 = (bf16[16,20,1024]{2,0,1:T(8,128)(2,1)}, bf16[16,20,1024]{2,0,1:T(8,128)(2,1)}, u32[]{:S(2)}, u32[]{:S(2)}) collective-permute-start(bf16[16,20,1024]{2,0,1:T(8,128)(2,1)} %copy.55), channel_id=1, source_target_pairs={{0,4},{4,0},{1,5},{5,1},{2,6},{6,2},{3,7},{7,3},{8,12},{12,8},{9,1... | collective-permute-start | bytes 1966088 | tf_op jit(solution)/shard_map/ppermute | solution.py:158
  388.5 23.2 %all-to-all-start.3 = ((bf16[16,20,1024]{2,1,0:T(8,128)(2,1)}), bf16[16,20,1024]{2,1,0:T(8,128)(2,1)S(1)}, u32[]{:S(2)}, u32[]{:S(2)}) async-start(bf16[16,20,1024]{2,1,0:T(8,128)(2,1)} %add_convert_fusion), calls=%async_computation.3 | async-start | bytes 1572864 | tf_op jit(solution)/shard_map/all_to_all | solution.py:160
  412.9 11.2 %copy-start.13 = (s32[2,32]{1,0:T(2,128)S(1)}, s32[2,32]{1,0:T(2,128)}, u32[]{:S(2)}) copy-start(s32[2,32]{1,0:T(2,128)} %param.15) | copy-start | bytes 772
  412.9 24.4 %copy-start.1 = (bf16[128,1024]{1,0:T(8,128)(2,1)S(1)}, bf16[128,1024]{1,0:T(8,128)(2,1)}, u32[]{:S(2)}) copy-start(bf16[128,1024]{1,0:T(8,128)(2,1)} %copy-done) | copy-start | bytes 786436
  413.2 25.4 %collective-permute-start.21 = (bf16[128,1024]{1,0:T(8,128)(2,1)S(1)}, bf16[128,1024]{1,0:T(8,128)(2,1)S(1)}, u32[]{:S(2)}, u32[]{:S(2)}) collective-permute-start(bf16[128,1024]{1,0:T(8,128)(2,1)S(1)} %multiply_reduce_fusion), channel_id=1, source_target_pairs={{0,2},{1,3},{2,0},{3,1},{4,6},{5,7},{6,4},{7,5},{8,10},{9,11},{10,... | collective-permute-start | bytes 786440 | tf_op jit(solution)/shard_map/ppermute | solution.py:40
  414.6 24.1 %collective-permute-start.20 = (bf16[128,1024]{1,0:T(8,128)(2,1)S(1)}, bf16[128,1024]{1,0:T(8,128)(2,1)S(1)}, u32[]{:S(2)}, u32[]{:S(2)}) collective-permute-start(bf16[128,1024]{1,0:T(8,128)(2,1)S(1)} %multiply_reduce_fusion), channel_id=1, source_target_pairs={{0,1},{1,0},{2,3},{3,2},{4,5},{5,4},{6,7},{7,6},{8,9},{9,8},{10,11... | collective-permute-start | bytes 786440 | tf_op jit(solution)/shard_map/ppermute | solution.py:40
  424.1 14.6 %collective-permute-start.22 = (bf16[128,1024]{1,0:T(8,128)(2,1)S(1)}, bf16[128,1024]{1,0:T(8,128)(2,1)S(1)}, u32[]{:S(2)}, u32[]{:S(2)}) collective-permute-start(bf16[128,1024]{1,0:T(8,128)(2,1)S(1)} %multiply_reduce_fusion), channel_id=1, source_target_pairs={{0,3},{1,2},{2,1},{3,0},{4,7},{5,6},{6,5},{7,4},{8,11},{9,10},{10,... | collective-permute-start | bytes 786440 | tf_op jit(solution)/shard_map/ppermute | solution.py:40
  426.4 16.1 %collective-permute-start.24 = (bf16[1,128,2,256]{1,3,2,0:T(8,128)(2,1)S(1)}, bf16[1,128,2,256]{1,3,2,0:T(8,128)(2,1)S(1)}, u32[]{:S(2)}, u32[]{:S(2)}) collective-permute-start(bf16[1,128,2,256]{1,3,2,0:T(8,128)(2,1)S(1)} %get-tuple-element.20), channel_id=1, source_target_pairs={{128,0},{129,1},{130,2},{131,3},{132,4},{133,5},{134,6},{135,7},{1... | collective-permute-start | bytes 393224 | tf_op jit(solution)/shard_map/ppermute | solution.py:209
  437.3 8.9 %collective-permute-start.14 = (bf16[128,1024]{1,0:T(8,128)(2,1)S(1)}, bf16[128,1024]{1,0:T(8,128)(2,1)S(1)}, u32[]{:S(2)}, u32[]{:S(2)}) collective-permute-start(bf16[128,1024]{1,0:T(8,128)(2,1)S(1)} %copy-done.1), channel_id=1, source_target_pairs={{128,0},{129,1},{130,2},{131,3},{132,4},{133,5},{134,6},{135,7},{1... | collective-permute-start | bytes 786440 | tf_op jit(solution)/shard_map/ppermute | solution.py:208
  438.9 7.4 %collective-permute-start.23 = (bf16[128,1024]{1,0:T(8,128)(2,1)S(1)}, bf16[128,1024]{1,0:T(8,128)(2,1)S(1)}, u32[]{:S(2)}, u32[]{:S(2)}) collective-permute-start(bf16[128,1024]{1,0:T(8,128)(2,1)S(1)} %add_convert_fusion.2), channel_id=1, source_target_pairs={{0,128},{1,129},{2,130},{3,131},{4,132},{5,133},{6,134},{7,135},{8... | collective-permute-start | bytes 786440 | tf_op jit(solution)/shard_map/ppermute | solution.py:210
  441.2 4.1 collective-permute-start.25
Sparse Core Ops, SparseCore 0:
  18.7 80.6 all-gather.2
  231.2 82.1 all-gather.4

commit v8 on v7

--- a/solution.py
+++ b/solution.py
@@ -200,11 +200,22 @@
     seg_all = lax.dynamic_index_in_dim(segment_ids, micro, 0, keepdims=False)
     table_row = lax.dynamic_index_in_dim(page_table, micro, 0, keepdims=False)
     pick_rows = lax.dynamic_index_in_dim(picks, micro, 0, keepdims=False)
-    results = []
-    for layer in range(2):
-        hidden, pages = one_layer(hidden, seg_all, table_row, pick_rows, *weights_of[layer])
-        results.append((hidden, pages))
-    (res0, pages0), (res1, pages1) = results
+    stacked = tuple(jnp.stack([first, second]) for first, second in zip(*weights_of))
+    res_init = jnp.zeros((2,) + hidden.shape, hidden.dtype)
+    blocks_dev = hidden.shape[0] // PAGE
+    page_init = jnp.zeros((2, blocks_dev, PAGE, 2, stacked[1].shape[2] // 3), jnp.bfloat16)
+
+    def layer_step(layer, carry):
+        now, res_all, page_all = carry
+        chosen = tuple(lax.dynamic_index_in_dim(w, layer, 0, keepdims=False) for w in stacked)
+        now, pages = one_layer(now, seg_all, table_row, pick_rows, *chosen)
+        res_all = lax.dynamic_update_index_in_dim(res_all, now, layer, 0)
+        page_all = lax.dynamic_update_index_in_dim(page_all, pages, layer, 0)
+        return now, res_all, page_all
+
+    _, res_all, page_all = lax.fori_loop(0, 2, layer_step, (hidden, res_init, page_init))
+    res0, res1 = res_all[0], res_all[1]
+    pages0, pages1 = page_all[0], page_all[1]
     got0 = lax.ppermute(res0, "section", [(1, 0)])
     gotp0 = lax.ppermute(pages0, "section", [(1, 0)])
     got1 = lax.ppermute(res1, "section", [(0, 1)])

time: 462 us -> 472 us (1.022); the launches traced: 454 us -> 471 us
  starting transfers between devices: 92.8 us -> 67.1 us
  blocking collectives: 22 us -> 46 us
  other arithmetic: 16.4 us -> 27 us
    all_to_all x1 -> x2, blocking collectives: 22 us -> 46 us  [one_layer(): lax.all_to_all(dispatch.reshape(experts_all, CAP, width), 'tz', split_axi...]
    ppermute x6, starting transfers between devices: 22 us -> 4.58 us  [per_device(): other = tuple((lax.ppermute(w, 'section', swap) for w in own))]
    all_to_all x1 -> x0, waiting for transfers between devices: 10.8 us -> none  [one_layer(): lax.all_to_all(dispatch.reshape(experts_all, CAP, width), 'tz', split_axi...]
    ppermute x1, starting transfers between devices: 1.31 us -> 10.6 us  [per_device(): got0 = lax.ppermute(res0, 'section', [(1, 0)])]
    ppermute x2, waiting for transfers between devices: 9.21 us -> 17.6 us  [one_layer(): pair_rows = lax.ppermute(own_rows, 'tp', pair_swap)]
    ppermute x12, starting transfers between devices: 23.7 us -> 15.8 us  [rep_sum(): lax.ppermute(own, 'rep', [(index, index ^ mask) for index in range(count)])]
    ppermute x1, starting transfers between devices: 10.9 us -> 3.04 us  [per_device(): gotp0 = lax.ppermute(pages0, 'section', [(1, 0)])]
    ppermute x12, waiting for transfers between devices: 27.7 us -> 34.4 us  [rep_sum(): lax.ppermute(own, 'rep', [(index, index ^ mask) for index in range(count)])]
  transfers between devices with their start and end apart: 31 -> 30, of which waited for: 17 -> 19; matrix products, arithmetic and copies ran while one was open for 5% -> 4% of each run, Pallas kernels for 0% -> 0%
where the time goes in v8:
time: 472 us; the launch traced here: 471 us
  waiting for transfers between devices  263 us (56%)
  starting transfers between devices  67.1 us (14%)
  blocking collectives  46 us (10%)
  other arithmetic  27 us (6%)
  matrix products  25.2 us (5%)
  local copies, waits for them, and re-layouts  25.1 us (5%)
  between operations  14.2 us (3%)
    all_gather x2, waiting for transfers between devices, one_layer(): piece = lax.all_gather(keys_vals, ('tz', 'tp'), axis=0, tiled=True)  159 us
    all_to_all x2, blocking collectives, one_layer(): lax.all_to_all(dispatch.reshape(experts_all, CAP, width), 'tz', split_axi...  46 us
    all_to_all x2, waiting for transfers between devices, one_layer(): lax.all_to_all(halves, 'tz', split_axis=0, concat_axis=0, tiled=True)  35.4 us
    ppermute x12, waiting for transfers between devices, rep_sum(): lax.ppermute(own, 'rep', [(index, index ^ mask) for index in range(count)])  34.4 us
    all_to_all x2, starting transfers between devices, one_layer(): lax.all_to_all(halves, 'tz', split_axis=0, concat_axis=0, tiled=True)  24.1 us
    ppermute x2, waiting for transfers between devices, one_layer(): pair_rows = lax.ppermute(own_rows, 'tp', pair_swap)  17.6 us
    ppermute x2, waiting for transfers between devices, one_layer(): pair_out = lax.ppermute(share_out[1], 'tp', pair_swap)  16.4 us
    ppermute x12, starting transfers between devices, rep_sum(): lax.ppermute(own, 'rep', [(index, index ^ mask) for index in range(count)])  15.8 us
  transfers between devices with their start and end apart: 30, of which 19 were waited for; matrix products, arithmetic and copies ran while one was open for 4% of the time, Pallas kernels for 0%

profile of v8, /device:TPU:1, one launch (start us, length us, event | category | flops | bytes accessed | tf_op | source)
XLA Modules:
  0.0 471.1 jit_solution(4621550563898431123)
XLA Ops:
  7.2 3.3 collective-permute-start.8
  13.3 1.8 copy.55
  20.6 1.9 pad_maximum_fusion.2
  22.8 1.9 pad_maximum_fusion.1
  24.7 418.6 %while.19 = (s32[]{:T(128)}, bf16[128,1024]{1,0:T(8,128)(2,1)S(1)}, bf16[2,128,1024]{2,1,0:T(8,128)(2,1)}, bf16[2,1,128,2,256]{4,3,2,1,0:T(2,128)(2,1)}, s32[409...) while((s32[]{:T(128)}, bf16[128,1024]{1,0:T(8,128)(2,1)S(1)}, ...), condition=%wide.region_15.16_spmd, body=%wide.region_0.15_spmd.sunk | while | flops 2819336192 | bytes 107681936 | solution.py:216
  24.9 2.1 fusion.109
  30.6 78.4 %all-gather.2.cloned.1.call-done = bf16[4096,2,256]{0,2,1:T(8,128)(2,1)} async-done(((bf16[128,2,256]{0,2,1:T(8,128)(2,1)}), bf16[4096,2,256]{0,2,1:T(8,128)(2,1)}) %all-gather.2.cloned.1.call-update) | async-done | bytes 4194320 | tf_op jit(solution)/shard_map/while/body/eval_jaxpr/all_gather | solution.py:112
  108.9 3.2 constant_dynamic-slice_fusion.9
  114.4 3.7 fusion.112
  120.6 2.4 collective-permute-start.1
  124.7 6.7 %collective-permute-done.1 = bf16[128,1024]{1,0:T(8,128)(2,1)S(1)} collective-permute-done((bf16[128,1024]{1,0:T(8,128)(2,1)S(1)}, bf16[128,1024]{1,0:T(8,128)(2,1)S(1)}, u32[]{:S(2)}, u32[]{:S(2)}) %collective-permute-start.1) | collective-permute-done | bytes 262176 | tf_op jit(solution)/shard_map/while/body/eval_jaxpr/ppermute | solution.py:40
  131.4 5.0 %collective-permute-done = bf16[128,1024]{1,0:T(8,128)(2,1)S(1)} collective-permute-done((bf16[128,1024]{1,0:T(8,128)(2,1)S(1)}, bf16[128,1024]{1,0:T(8,128)(2,1)S(1)}, u32[]{:S(2)}, u32[]{:S(2)}) %collective-permute-start) | collective-permute-done | bytes 262176 | tf_op jit(solution)/shard_map/while/body/eval_jaxpr/ppermute | solution.py:40
  137.3 23.0 %all_to_all.26 = bf16[16,20,1024]{2,1,0:T(8,128)(2,1)S(1)} all-to-all(bf16[16,20,1024]{2,1,0:T(8,128)(2,1)S(1)} %reshape.494), channel_id=1, replica_groups=mesh['section'=2,'tz'=16,'tp'=2,'rep'=4] {'tz'}, dimensions={0} | all-to-all | bytes 1310720 | tf_op jit(solution)/shard_map/while/body/eval_jaxpr/all_to_all | solution.py:149
  160.6 1.8 collective-permute-start.3
  162.4 8.8 %collective-permute-done.3 = bf16[16,20,1024]{2,0,1:T(8,128)(2,1)S(1)} collective-permute-done((bf16[16,20,1024]{2,0,1:T(8,128)(2,1)S(1)}, bf16[16,20,1024]{2,0,1:T(8,128)(2,1)S(1)}, u32[]{:S(2)}, u32[]{:S(2)}) %collective-permute-start.3) | collective-permute-done | bytes 655392 | tf_op jit(solution)/shard_map/while/body/eval_jaxpr/ppermute | solution.py:152
  172.1 2.8 fusion.115
  177.5 1.5 collective-permute-start.4
  179.1 8.2 %collective-permute-done.4 = bf16[16,20,1024]{2,0,1:T(8,128)(2,1)} collective-permute-done((bf16[16,20,1024]{2,0,1:T(8,128)(2,1)}, bf16[16,20,1024]{2,0,1:T(8,128)(2,1)}, u32[]{:S(2)}, u32[]{:S(2)}) %collective-permute-start.4) | collective-permute-done | bytes 655392 | tf_op jit(solution)/shard_map/while/body/eval_jaxpr/ppermute | solution.py:158
  187.2 2.5 add_convert_fusion.4
  189.7 12.1 %all-to-all-start.1 = ((bf16[16,20,1024]{2,1,0:T(8,128)(2,1)}), bf16[16,20,1024]{2,1,0:T(8,128)(2,1)S(1)}, u32[]{:S(2)}, u32[]{:S(2)}) async-start(bf16[16,20,1024]{2,1,0:T(8,128)(2,1)} %add_convert_fusion.4), calls=%async_computation.1 | async-start | bytes 1572864 | tf_op jit(solution)/shard_map/while/body/eval_jaxpr/all_to_all | solution.py:160
  202.2 17.7 %all-to-all-done.1 = bf16[16,20,1024]{2,1,0:T(8,128)(2,1)S(1)} async-done(((bf16[16,20,1024]{2,1,0:T(8,128)(2,1)}), bf16[16,20,1024]{2,1,0:T(8,128)(2,1)S(1)}, u32[]{:S(2)}, u32[]{:S(2)}) %all-to-all-start.1) | async-done | bytes 655392 | tf_op jit(solution)/shard_map/while/body/eval_jaxpr/all_to_all | solution.py:160
  221.4 1.5 collective-permute-start.6
  222.9 2.4 collective-permute-start.5
  228.0 1.6 collective-permute-done.6
  229.5 2.6 collective-permute-done.5
  233.3 2.1 fusion.109
  239.0 80.2 %all-gather.2.cloned.1.call-done = bf16[4096,2,256]{0,2,1:T(8,128)(2,1)} async-done(((bf16[128,2,256]{0,2,1:T(8,128)(2,1)}), bf16[4096,2,256]{0,2,1:T(8,128)(2,1)}) %all-gather.2.cloned.1.call-update) | async-done | bytes 4194320 | tf_op jit(solution)/shard_map/while/body/eval_jaxpr/all_gather | solution.py:112
  319.1 3.2 constant_dynamic-slice_fusion.9
  324.6 3.7 fusion.112
  330.8 2.4 collective-permute-start.1
  334.9 6.7 %collective-permute-done.1 = bf16[128,1024]{1,0:T(8,128)(2,1)S(1)} collective-permute-done((bf16[128,1024]{1,0:T(8,128)(2,1)S(1)}, bf16[128,1024]{1,0:T(8,128)(2,1)S(1)}, u32[]{:S(2)}, u32[]{:S(2)}) %collective-permute-start.1) | collective-permute-done | bytes 262176 | tf_op jit(solution)/shard_map/while/body/eval_jaxpr/ppermute | solution.py:40
  341.6 5.0 %collective-permute-done = bf16[128,1024]{1,0:T(8,128)(2,1)S(1)} collective-permute-done((bf16[128,1024]{1,0:T(8,128)(2,1)S(1)}, bf16[128,1024]{1,0:T(8,128)(2,1)S(1)}, u32[]{:S(2)}, u32[]{:S(2)}) %collective-permute-start) | collective-permute-done | bytes 262176 | tf_op jit(solution)/shard_map/while/body/eval_jaxpr/ppermute | solution.py:40
  347.5 23.0 %all_to_all.26 = bf16[16,20,1024]{2,1,0:T(8,128)(2,1)S(1)} all-to-all(bf16[16,20,1024]{2,1,0:T(8,128)(2,1)S(1)} %reshape.494), channel_id=1, replica_groups=mesh['section'=2,'tz'=16,'tp'=2,'rep'=4] {'tz'}, dimensions={0} | all-to-all | bytes 1310720 | tf_op jit(solution)/shard_map/while/body/eval_jaxpr/all_to_all | solution.py:149
  370.8 1.8 collective-permute-start.3
  372.6 8.8 %collective-permute-done.3 = bf16[16,20,1024]{2,0,1:T(8,128)(2,1)S(1)} collective-permute-done((bf16[16,20,1024]{2,0,1:T(8,128)(2,1)S(1)}, bf16[16,20,1024]{2,0,1:T(8,128)(2,1)S(1)}, u32[]{:S(2)}, u32[]{:S(2)}) %collective-permute-start.3) | collective-permute-done | bytes 655392 | tf_op jit(solution)/shard_map/while/body/eval_jaxpr/ppermute | solution.py:152
  382.3 2.8 fusion.115
  387.7 1.4 collective-permute-start.4
  389.3 8.2 %collective-permute-done.4 = bf16[16,20,1024]{2,0,1:T(8,128)(2,1)} collective-permute-done((bf16[16,20,1024]{2,0,1:T(8,128)(2,1)}, bf16[16,20,1024]{2,0,1:T(8,128)(2,1)}, u32[]{:S(2)}, u32[]{:S(2)}) %collective-permute-start.4) | collective-permute-done | bytes 655392 | tf_op jit(solution)/shard_map/while/body/eval_jaxpr/ppermute | solution.py:158
  397.5 2.5 add_convert_fusion.4
  399.9 12.0 %all-to-all-start.1 = ((bf16[16,20,1024]{2,1,0:T(8,128)(2,1)}), bf16[16,20,1024]{2,1,0:T(8,128)(2,1)S(1)}, u32[]{:S(2)}, u32[]{:S(2)}) async-start(bf16[16,20,1024]{2,1,0:T(8,128)(2,1)} %add_convert_fusion.4), calls=%async_computation.1 | async-start | bytes 1572864 | tf_op jit(solution)/shard_map/while/body/eval_jaxpr/all_to_all | solution.py:160
  412.4 17.7 %all-to-all-done.1 = bf16[16,20,1024]{2,1,0:T(8,128)(2,1)S(1)} async-done(((bf16[16,20,1024]{2,1,0:T(8,128)(2,1)}), bf16[16,20,1024]{2,1,0:T(8,128)(2,1)S(1)}, u32[]{:S(2)}, u32[]{:S(2)}) %all-to-all-start.1) | async-done | bytes 655392 | tf_op jit(solution)/shard_map/while/body/eval_jaxpr/all_to_all | solution.py:160
  431.6 1.5 collective-permute-start.6
  433.0 2.4 collective-permute-start.5
  438.2 1.6 collective-permute-done.6
  439.7 2.6 collective-permute-done.5
  445.8 10.6 %collective-permute-start.14 = (bf16[128,1024]{1,0:T(8,128)(2,1)S(1)}, bf16[128,1024]{1,0:T(8,128)(2,1)S(1)}, u32[]{:S(2)}, u32[]{:S(2)}) collective-permute-start(bf16[128,1024]{1,0:T(8,128)(2,1)S(1)} %get-tuple-element.416), channel_id=1, source_target_pairs={{128,0},{129,1},{130,2},{131,3},{132,4},{133,5},{134,6},{135,7},{1... | collective-permute-start | bytes 786440 | tf_op jit(solution)/shard_map/ppermute | solution.py:219
  458.0 3.0 collective-permute-start.16
  462.0 1.4 broadcast_select_fusion
  (194 shorter events, 52.7 us)
Async XLA Ops:
  7.2 5.4 %copy-start = (bf16[2,128,1024]{2,1,0:T(8,128)(2,1)S(1)}, bf16[2,128,1024]{2,1,0:T(8,128)(2,1)}, u32[]{:S(2)}) copy-start(bf16[2,128,1024]{2,1,0:T(8,128)(2,1)} %param.12) | copy-start | bytes 1572868
  7.2 8.4 %collective-permute-start.8 = (f32[2,1024]{1,0:T(2,128)}, f32[2,1024]{1,0:T(2,128)S(1)}, u32[]{:S(2)}, u32[]{:S(2)}) collective-permute-start(f32[2,1024]{1,0:T(2,128)} %bitcast.264), channel_id=1, source_target_pairs={{0,128},{128,0},{1,129},{129,1},{2,130},{130,2},{3,131},{131,3},{4... | collective-permute-start | bytes 24584 | tf_op jit(solution)/shard_map/ppermute | solution.py:193
  10.5 5.3 %collective-permute-start.11 = (bf16[1024,16]{0,1:T(8,128)(2,1)}, bf16[1024,16]{0,1:T(8,128)(2,1)S(1)}, u32[]{:S(2)}, u32[]{:S(2)}) collective-permute-start(bf16[1024,16]{0,1:T(8,128)(2,1)} %bitcast.263), channel_id=1, source_target_pairs={{0,128},{128,0},{1,129},{129,1},{2,130},{130,2},{3,131},{131,3},{4... | collective-permute-start | bytes 98312 | tf_op jit(solution)/shard_map/ppermute | solution.py:193
  10.6 5.3 %collective-permute-start.10 = (bf16[256,1024]{1,0:T(8,128)(2,1)}, bf16[256,1024]{1,0:T(8,128)(2,1)S(1)}, u32[]{:S(2)}, u32[]{:S(2)}) collective-permute-start(bf16[256,1024]{1,0:T(8,128)(2,1)} %bitcast.253), channel_id=1, source_target_pairs={{0,128},{128,0},{1,129},{129,1},{2,130},{130,2},{3,131},{131,3},{4... | collective-permute-start | bytes 1572872 | tf_op jit(solution)/shard_map/ppermute | solution.py:193
  11.0 6.1 %collective-permute-start.13 = (bf16[1,352,1024]{2,1,0:T(8,128)(2,1)}, bf16[1,352,1024]{2,1,0:T(8,128)(2,1)}, u32[]{:S(2)}, u32[]{:S(2)}) collective-permute-start(bf16[1,352,1024]{2,1,0:T(8,128)(2,1)} %bitcast.250), channel_id=1, source_target_pairs={{0,128},{128,0},{1,129},{129,1},{2,130},{130,2},{3,131},{131,3},{4... | collective-permute-start | bytes 2162696 | tf_op jit(solution)/shard_map/ppermute | solution.py:193
  13.3 2.3 copy-start.12
  13.3 2.5 copy-start.11
  13.3 2.6 copy-start.5
  15.1 4.7 collective-permute-start.12
  15.6 6.8 %collective-permute-start.9 = (bf16[1024,768]{0,1:T(8,128)(2,1)S(1)}, bf16[1024,768]{0,1:T(8,128)(2,1)S(1)}, u32[]{:S(2)}, u32[]{:S(2)}) collective-permute-start(bf16[1024,768]{0,1:T(8,128)(2,1)S(1)} %bitcast.244), channel_id=1, source_target_pairs={{0,128},{128,0},{1,129},{129,1},{2,130},{130,2},{3,131},{131,3},{4... | collective-permute-start | bytes 4718600 | tf_op jit(solution)/shard_map/ppermute | solution.py:193
  15.9 1.4 copy-start.4
  18.5 1.9 copy-start.3
  24.7 84.2 %all-gather.2.cloned.1.call-start = ((), (), s32[]{:S(2)}) async-start(), calls=%async_computation.2 | async-start | bytes 4325376 | tf_op jit(solution)/shard_map/while/body/eval_jaxpr/all_gather | solution.py:112
  119.3 5.3 %collective-permute-start.2 = (bf16[128,1024]{1,0:T(8,128)(2,1)S(1)}, bf16[128,1024]{1,0:T(8,128)(2,1)S(1)}, u32[]{:S(2)}, u32[]{:S(2)}) collective-permute-start(bf16[128,1024]{1,0:T(8,128)(2,1)S(1)} %convolution_convert_fusion.6), channel_id=1, source_target_pairs={{0,1},{1,0},{2,3},{3,2},{4,5},{5,4},{6,7},{7,6},{8,9},{9,8},{10,11... | collective-permute-start | bytes 786440 | tf_op jit(solution)/shard_map/while/body/eval_jaxpr/ppermute | solution.py:40
  120.6 10.8 %collective-permute-start.1 = (bf16[128,1024]{1,0:T(8,128)(2,1)S(1)}, bf16[128,1024]{1,0:T(8,128)(2,1)S(1)}, u32[]{:S(2)}, u32[]{:S(2)}) collective-permute-start(bf16[128,1024]{1,0:T(8,128)(2,1)S(1)} %convolution_convert_fusion.6), channel_id=1, source_target_pairs={{0,2},{1,3},{2,0},{3,1},{4,6},{5,7},{6,4},{7,5},{8,10},{9,11},{10,... | collective-permute-start | bytes 786440 | tf_op jit(solution)/shard_map/while/body/eval_jaxpr/ppermute | solution.py:40
  123.0 13.4 %collective-permute-start = (bf16[128,1024]{1,0:T(8,128)(2,1)S(1)}, bf16[128,1024]{1,0:T(8,128)(2,1)S(1)}, u32[]{:S(2)}, u32[]{:S(2)}) collective-permute-start(bf16[128,1024]{1,0:T(8,128)(2,1)S(1)} %convolution_convert_fusion.6), channel_id=1, source_target_pairs={{0,3},{1,2},{2,1},{3,0},{4,7},{5,6},{6,5},{7,4},{8,11},{9,10},{10,... | collective-permute-start | bytes 786440 | tf_op jit(solution)/shard_map/while/body/eval_jaxpr/ppermute | solution.py:40
  160.6 10.6 %collective-permute-start.3 = (bf16[16,20,1024]{2,0,1:T(8,128)(2,1)S(1)}, bf16[16,20,1024]{2,0,1:T(8,128)(2,1)S(1)}, u32[]{:S(2)}, u32[]{:S(2)}) collective-permute-start(bf16[16,20,1024]{2,0,1:T(8,128)(2,1)S(1)} %copy.79), channel_id=1, source_target_pairs={{0,4},{4,0},{1,5},{5,1},{2,6},{6,2},{3,7},{7,3},{8,12},{12,8},{9,1... | collective-permute-start | bytes 1966088 | tf_op jit(solution)/shard_map/while/body/eval_jaxpr/ppermute | solution.py:152
  172.1 2.8 copy-start.2
  177.5 9.8 %collective-permute-start.4 = (bf16[16,20,1024]{2,0,1:T(8,128)(2,1)}, bf16[16,20,1024]{2,0,1:T(8,128)(2,1)}, u32[]{:S(2)}, u32[]{:S(2)}) collective-permute-start(bf16[16,20,1024]{2,0,1:T(8,128)(2,1)} %copy.81), channel_id=1, source_target_pairs={{0,4},{4,0},{1,5},{5,1},{2,6},{6,2},{3,7},{7,3},{8,12},{12,8},{9,1... | collective-permute-start | bytes 1966088 | tf_op jit(solution)/shard_map/while/body/eval_jaxpr/ppermute | solution.py:158
  189.7 30.2 %all-to-all-start.1 = ((bf16[16,20,1024]{2,1,0:T(8,128)(2,1)}), bf16[16,20,1024]{2,1,0:T(8,128)(2,1)S(1)}, u32[]{:S(2)}, u32[]{:S(2)}) async-start(bf16[16,20,1024]{2,1,0:T(8,128)(2,1)} %add_convert_fusion.4), calls=%async_computation.1 | async-start | bytes 1572864 | tf_op jit(solution)/shard_map/while/body/eval_jaxpr/all_to_all | solution.py:160
  221.1 6.7 %copy-start.8 = (bf16[2,1,128,2,256]{4,3,2,1,0:T(2,128)(2,1)S(1)}, bf16[2,1,128,2,256]{4,3,2,1,0:T(2,128)(2,1)}, u32[]{:S(2)}) copy-start(bf16[2,1,128,2,256]{4,3,2,1,0:T(2,128)(2,1)} %get-tuple-element.567) | copy-start | bytes 786436 | tf_op jit(solution)/shard_map/while
  221.1 11.0 %copy-start.6 = (bf16[2,128,1024]{2,1,0:T(8,128)(2,1)S(1)}, bf16[2,128,1024]{2,1,0:T(8,128)(2,1)}, u32[]{:S(2)}) copy-start(bf16[2,128,1024]{2,1,0:T(8,128)(2,1)} %get-tuple-element.566) | copy-start | bytes 1572868 | tf_op jit(solution)/shard_map/while
  221.3 6.7 %collective-permute-start.7 = (bf16[128,1024]{1,0:T(8,128)(2,1)S(1)}, bf16[128,1024]{1,0:T(8,128)(2,1)S(1)}, u32[]{:S(2)}, u32[]{:S(2)}) collective-permute-start(bf16[128,1024]{1,0:T(8,128)(2,1)S(1)} %multiply_reduce_fusion.8), channel_id=1, source_target_pairs={{0,1},{1,0},{2,3},{3,2},{4,5},{5,4},{6,7},{7,6},{8,9},{9,8},{10,11... | collective-permute-start | bytes 786440 | tf_op jit(solution)/shard_map/while/body/eval_jaxpr/ppermute | solution.py:40
  221.4 8.1 %collective-permute-start.6 = (bf16[128,1024]{1,0:T(8,128)(2,1)S(1)}, bf16[128,1024]{1,0:T(8,128)(2,1)S(1)}, u32[]{:S(2)}, u32[]{:S(2)}) collective-permute-start(bf16[128,1024]{1,0:T(8,128)(2,1)S(1)} %multiply_reduce_fusion.8), channel_id=1, source_target_pairs={{0,2},{1,3},{2,0},{3,1},{4,6},{5,7},{6,4},{7,5},{8,10},{9,11},{10,... | collective-permute-start | bytes 786440 | tf_op jit(solution)/shard_map/while/body/eval_jaxpr/ppermute | solution.py:40
  222.9 9.2 %collective-permute-start.5 = (bf16[128,1024]{1,0:T(8,128)(2,1)S(1)}, bf16[128,1024]{1,0:T(8,128)(2,1)S(1)}, u32[]{:S(2)}, u32[]{:S(2)}) collective-permute-start(bf16[128,1024]{1,0:T(8,128)(2,1)S(1)} %multiply_reduce_fusion.8), channel_id=1, source_target_pairs={{0,3},{1,2},{2,1},{3,0},{4,7},{5,6},{6,5},{7,4},{8,11},{9,10},{10,... | collective-permute-start | bytes 786440 | tf_op jit(solution)/shard_map/while/body/eval_jaxpr/ppermute | solution.py:40
  227.9 4.2 copy-start.9
  232.3 0.8 copy-start.7
  233.1 86.0 %all-gather.2.cloned.1.call-start = ((), (), s32[]{:S(2)}) async-start(), calls=%async_computation.2 | async-start | bytes 4325376 | tf_op jit(solution)/shard_map/while/body/eval_jaxpr/all_gather | solution.py:112
  329.5 5.3 %collective-permute-start.2 = (bf16[128,1024]{1,0:T(8,128)(2,1)S(1)}, bf16[128,1024]{1,0:T(8,128)(2,1)S(1)}, u32[]{:S(2)}, u32[]{:S(2)}) collective-permute-start(bf16[128,1024]{1,0:T(8,128)(2,1)S(1)} %convolution_convert_fusion.6), channel_id=1, source_target_pairs={{0,1},{1,0},{2,3},{3,2},{4,5},{5,4},{6,7},{7,6},{8,9},{9,8},{10,11... | collective-permute-start | bytes 786440 | tf_op jit(solution)/shard_map/while/body/eval_jaxpr/ppermute | solution.py:40
  330.8 10.8 %collective-permute-start.1 = (bf16[128,1024]{1,0:T(8,128)(2,1)S(1)}, bf16[128,1024]{1,0:T(8,128)(2,1)S(1)}, u32[]{:S(2)}, u32[]{:S(2)}) collective-permute-start(bf16[128,1024]{1,0:T(8,128)(2,1)S(1)} %convolution_convert_fusion.6), channel_id=1, source_target_pairs={{0,2},{1,3},{2,0},{3,1},{4,6},{5,7},{6,4},{7,5},{8,10},{9,11},{10,... | collective-permute-start | bytes 786440 | tf_op jit(solution)/shard_map/while/body/eval_jaxpr/ppermute | solution.py:40
  333.2 13.4 %collective-permute-start = (bf16[128,1024]{1,0:T(8,128)(2,1)S(1)}, bf16[128,1024]{1,0:T(8,128)(2,1)S(1)}, u32[]{:S(2)}, u32[]{:S(2)}) collective-permute-start(bf16[128,1024]{1,0:T(8,128)(2,1)S(1)} %convolution_convert_fusion.6), channel_id=1, source_target_pairs={{0,3},{1,2},{2,1},{3,0},{4,7},{5,6},{6,5},{7,4},{8,11},{9,10},{10,... | collective-permute-start | bytes 786440 | tf_op jit(solution)/shard_map/while/body/eval_jaxpr/ppermute | solution.py:40
  370.8 10.6 %collective-permute-start.3 = (bf16[16,20,1024]{2,0,1:T(8,128)(2,1)S(1)}, bf16[16,20,1024]{2,0,1:T(8,128)(2,1)S(1)}, u32[]{:S(2)}, u32[]{:S(2)}) collective-permute-start(bf16[16,20,1024]{2,0,1:T(8,128)(2,1)S(1)} %copy.79), channel_id=1, source_target_pairs={{0,4},{4,0},{1,5},{5,1},{2,6},{6,2},{3,7},{7,3},{8,12},{12,8},{9,1... | collective-permute-start | bytes 1966088 | tf_op jit(solution)/shard_map/while/body/eval_jaxpr/ppermute | solution.py:152
  382.3 2.8 copy-start.2
  387.7 9.8 %collective-permute-start.4 = (bf16[16,20,1024]{2,0,1:T(8,128)(2,1)}, bf16[16,20,1024]{2,0,1:T(8,128)(2,1)}, u32[]{:S(2)}, u32[]{:S(2)}) collective-permute-start(bf16[16,20,1024]{2,0,1:T(8,128)(2,1)} %copy.81), channel_id=1, source_target_pairs={{0,4},{4,0},{1,5},{5,1},{2,6},{6,2},{3,7},{7,3},{8,12},{12,8},{9,1... | collective-permute-start | bytes 1966088 | tf_op jit(solution)/shard_map/while/body/eval_jaxpr/ppermute | solution.py:158
  399.9 30.1 %all-to-all-start.1 = ((bf16[16,20,1024]{2,1,0:T(8,128)(2,1)}), bf16[16,20,1024]{2,1,0:T(8,128)(2,1)S(1)}, u32[]{:S(2)}, u32[]{:S(2)}) async-start(bf16[16,20,1024]{2,1,0:T(8,128)(2,1)} %add_convert_fusion.4), calls=%async_computation.1 | async-start | bytes 1572864 | tf_op jit(solution)/shard_map/while/body/eval_jaxpr/all_to_all | solution.py:160
  431.3 6.7 %copy-start.8 = (bf16[2,1,128,2,256]{4,3,2,1,0:T(2,128)(2,1)S(1)}, bf16[2,1,128,2,256]{4,3,2,1,0:T(2,128)(2,1)}, u32[]{:S(2)}) copy-start(bf16[2,1,128,2,256]{4,3,2,1,0:T(2,128)(2,1)} %get-tuple-element.567) | copy-start | bytes 786436 | tf_op jit(solution)/shard_map/while
  431.3 11.0 %copy-start.6 = (bf16[2,128,1024]{2,1,0:T(8,128)(2,1)S(1)}, bf16[2,128,1024]{2,1,0:T(8,128)(2,1)}, u32[]{:S(2)}) copy-start(bf16[2,128,1024]{2,1,0:T(8,128)(2,1)} %get-tuple-element.566) | copy-start | bytes 1572868 | tf_op jit(solution)/shard_map/while
  431.5 6.7 %collective-permute-start.7 = (bf16[128,1024]{1,0:T(8,128)(2,1)S(1)}, bf16[128,1024]{1,0:T(8,128)(2,1)S(1)}, u32[]{:S(2)}, u32[]{:S(2)}) collective-permute-start(bf16[128,1024]{1,0:T(8,128)(2,1)S(1)} %multiply_reduce_fusion.8), channel_id=1, source_target_pairs={{0,1},{1,0},{2,3},{3,2},{4,5},{5,4},{6,7},{7,6},{8,9},{9,8},{10,11... | collective-permute-start | bytes 786440 | tf_op jit(solution)/shard_map/while/body/eval_jaxpr/ppermute | solution.py:40
  431.6 8.1 %collective-permute-start.6 = (bf16[128,1024]{1,0:T(8,128)(2,1)S(1)}, bf16[128,1024]{1,0:T(8,128)(2,1)S(1)}, u32[]{:S(2)}, u32[]{:S(2)}) collective-permute-start(bf16[128,1024]{1,0:T(8,128)(2,1)S(1)} %multiply_reduce_fusion.8), channel_id=1, source_target_pairs={{0,2},{1,3},{2,0},{3,1},{4,6},{5,7},{6,4},{7,5},{8,10},{9,11},{10,... | collective-permute-start | bytes 786440 | tf_op jit(solution)/shard_map/while/body/eval_jaxpr/ppermute | solution.py:40
  433.0 9.2 %collective-permute-start.5 = (bf16[128,1024]{1,0:T(8,128)(2,1)S(1)}, bf16[128,1024]{1,0:T(8,128)(2,1)S(1)}, u32[]{:S(2)}, u32[]{:S(2)}) collective-permute-start(bf16[128,1024]{1,0:T(8,128)(2,1)S(1)} %multiply_reduce_fusion.8), channel_id=1, source_target_pairs={{0,3},{1,2},{2,1},{3,0},{4,7},{5,6},{6,5},{7,4},{8,11},{9,10},{10,... | collective-permute-start | bytes 786440 | tf_op jit(solution)/shard_map/while/body/eval_jaxpr/ppermute | solution.py:40
  438.1 4.2 copy-start.9
  442.5 0.8 copy-start.7
  443.3 13.1 %copy-start.10 = (bf16[2,1,128,2,256]{4,3,2,1,0:T(2,128)(2,1)S(1)}, bf16[2,1,128,2,256]{4,3,2,1,0:T(2,128)(2,1)}, u32[]{:S(2)}) copy-start(bf16[2,1,128,2,256]{4,3,2,1,0:T(2,128)(2,1)} %get-tuple-element.312) | copy-start | bytes 786436
  444.5 18.9 %collective-permute-start.15 = (bf16[128,1024]{1,0:T(8,128)(2,1)S(1)}, bf16[128,1024]{1,0:T(8,128)(2,1)S(1)}, u32[]{:S(2)}, u32[]{:S(2)}) collective-permute-start(bf16[128,1024]{1,0:T(8,128)(2,1)S(1)} %get-tuple-element.415), channel_id=1, source_target_pairs={{0,128},{1,129},{2,130},{3,131},{4,132},{5,133},{6,134},{7,135},{8... | collective-permute-start | bytes 786440 | tf_op jit(solution)/shard_map/ppermute | solution.py:221
  445.8 17.6 %collective-permute-start.14 = (bf16[128,1024]{1,0:T(8,128)(2,1)S(1)}, bf16[128,1024]{1,0:T(8,128)(2,1)S(1)}, u32[]{:S(2)}, u32[]{:S(2)}) collective-permute-start(bf16[128,1024]{1,0:T(8,128)(2,1)S(1)} %get-tuple-element.416), channel_id=1, source_target_pairs={{128,0},{129,1},{130,2},{131,3},{132,4},{133,5},{134,6},{135,7},{1... | collective-permute-start | bytes 786440 | tf_op jit(solution)/shard_map/ppermute | solution.py:219
  456.4 7.9 %copy-start.1 = (bf16[2,128,1024]{2,1,0:T(8,128)(2,1)S(1)}, bf16[2,128,1024]{2,1,0:T(8,128)(2,1)}, u32[]{:S(2)}) copy-start(bf16[2,128,1024]{2,1,0:T(8,128)(2,1)} %param.12) | copy-start | bytes 1572868
  456.7 4.4 collective-permute-start.17
  458.0 4.0 collective-permute-start.16
Sparse Core Ops, SparseCore 0:
  28.0 80.9 all-gather.1
  236.4 82.6 all-gather.1

commit v9 on v7

--- a/solution.py
+++ b/solution.py
@@ -205,10 +205,13 @@
         hidden, pages = one_layer(hidden, seg_all, table_row, pick_rows, *weights_of[layer])
         results.append((hidden, pages))
     (res0, pages0), (res1, pages1) = results
-    got0 = lax.ppermute(res0, "section", [(1, 0)])
-    gotp0 = lax.ppermute(pages0, "section", [(1, 0)])
-    got1 = lax.ppermute(res1, "section", [(0, 1)])
-    gotp1 = lax.ppermute(pages1, "section", [(0, 1)])
+    def packed_send(res, pages, pairs):
+        flat = jnp.concatenate([res.reshape(-1), pages.reshape(-1)])
+        got = lax.ppermute(flat, "section", pairs)
+        return got[: res.size].reshape(res.shape), got[res.size :].reshape(pages.shape)
+
+    got0, gotp0 = packed_send(res0, pages0, [(1, 0)])
+    got1, gotp1 = packed_send(res1, pages1, [(0, 1)])
     outputs = jnp.where(is_first, jnp.stack([res0, got0]), jnp.stack([got1, res1]))
     page_out = jnp.where(is_first, jnp.stack([pages0, gotp0]), jnp.stack([gotp1, pages1]))
     return (outputs[None], page_out[None])

time: 462 us -> 460 us (level)
    ppermute x4 -> x2, starting transfers between devices: 14.8 us -> 12.2 us  [packed_send(): got = lax.ppermute(flat, 'section', pairs)]
  transfers between devices with their start and end apart: 31 -> 29, of which waited for: 17 -> 17; matrix products, arithmetic and copies ran while one was open for 5% -> 6% of each run, Pallas kernels for 0% -> 0%
where the time goes in v9:
time: 460 us; the launch traced here: 453 us
  waiting for transfers between devices  260 us (57%)
  starting transfers between devices  90.1 us (20%)
  matrix products  23.7 us (5%)
  local copies, waits for them, and re-layouts  22.6 us (5%)
  blocking collectives  22 us (5%)
  other arithmetic  18.6 us (4%)
  between operations  16.7 us (4%)
    all_gather x2, waiting for transfers between devices, one_layer(): piece = lax.all_gather(keys_vals, ('tz', 'tp'), axis=0, tiled=True)  160 us
    all_to_all x2, waiting for transfers between devices, one_layer(): lax.all_to_all(halves, 'tz', split_axis=0, concat_axis=0, tiled=True)  29.2 us
    ppermute x12, waiting for transfers between devices, rep_sum(): lax.ppermute(own, 'rep', [(index, index ^ mask) for index in range(count)])  27.9 us
    ppermute x12, starting transfers between devices, rep_sum(): lax.ppermute(own, 'rep', [(index, index ^ mask) for index in range(count)])  23.7 us
    all_to_all x1, blocking collectives, one_layer(): lax.all_to_all(dispatch.reshape(experts_all, CAP, width), 'tz', split_axi...  22 us
    all_to_all x2, starting transfers between devices, one_layer(): lax.all_to_all(halves, 'tz', split_axis=0, concat_axis=0, tiled=True)  22 us
    ppermute x6, starting transfers between devices, per_device(): other = tuple((lax.ppermute(w, 'section', swap) for w in own))  21.9 us
    ppermute x2, waiting for transfers between devices, one_layer(): pair_out = lax.ppermute(share_out[1], 'tp', pair_swap)  15.5 us
  transfers between devices with their start and end apart: 29, of which 17 were waited for; matrix products, arithmetic and copies ran while one was open for 6% of the time, Pallas kernels for 0%

profile of v9, /device:TPU:1, one launch (start us, length us, event | category | flops | bytes accessed | tf_op | source)
XLA Modules:
  0.0 453.2 jit_solution(16764261562553239557)
XLA Ops:
  7.2 1.8 copy.61
  9.0 3.3 collective-permute-start.1
  12.6 2.9 collective-permute-done
  15.5 2.1 fusion.26
  21.6 77.8 %all-gather.3.cloned.1.call-done = bf16[4096,2,256]{0,2,1:T(8,128)(2,1)} async-done(((bf16[128,2,256]{0,2,1:T(8,128)(2,1)}), bf16[4096,2,256]{0,2,1:T(8,128)(2,1)}) %all-gather.3.cloned.1.call-update) | async-done | bytes 4194320 | tf_op jit(solution)/shard_map/all_gather | solution.py:112
  99.4 3.2 constant_dynamic-slice_fusion.1
  102.6 1.1 fusion.133
  104.8 3.7 fusion.39
  108.8 2.5 collective-permute-start.5
  112.3 9.5 %collective-permute-done.5 = bf16[128,1024]{1,0:T(8,128)(2,1)S(1)} collective-permute-done((bf16[128,1024]{1,0:T(8,128)(2,1)S(1)}, bf16[128,1024]{1,0:T(8,128)(2,1)S(1)}, u32[]{:S(2)}, u32[]{:S(2)}) %collective-permute-start.5) | collective-permute-done | bytes 262176 | tf_op jit(solution)/shard_map/ppermute | solution.py:40
  123.6 4.3 all-to-all-start
  127.8 6.4 %collective-permute-start.8 = (bf16[1,1024,2,352]{1,3,2,0:T(8,128)(2,1)}, bf16[1,1024,2,352]{1,3,2,0:T(8,128)(2,1)}, u32[]{:S(2)}, u32[]{:S(2)}) collective-permute-start(bf16[1,1024,2,352]{1,3,2,0:T(8,128)(2,1)} %bitcast.28), channel_id=1, source_target_pairs={{0,128},{128,0},{1,129},{129,1},{2,130},{130,2},{3,131},{131,3},{4... | collective-permute-start | bytes 4325384 | tf_op jit(solution)/shard_map/ppermute | solution.py:193
  134.3 10.8 %all-to-all-done = bf16[16,20,1024]{2,1,0:T(8,128)(2,1)S(1)} async-done(((bf16[16,20,1024]{2,1,0:T(8,128)(2,1)}), bf16[16,20,1024]{2,1,0:T(8,128)(2,1)S(1)}, u32[]{:S(2)}, u32[]{:S(2)}) %all-to-all-start) | async-done | bytes 655392 | tf_op jit(solution)/shard_map/all_to_all | solution.py:149
  146.3 8.3 %collective-permute-start.9 = (bf16[1,352,1024]{2,1,0:T(8,128)(2,1)}, bf16[1,352,1024]{2,1,0:T(8,128)(2,1)}, u32[]{:S(2)}, u32[]{:S(2)}) collective-permute-start(bf16[1,352,1024]{2,1,0:T(8,128)(2,1)} %bitcast.221), channel_id=1, source_target_pairs={{0,128},{128,0},{1,129},{129,1},{2,130},{130,2},{3,131},{131,3},{4... | collective-permute-start | bytes 2162696 | tf_op jit(solution)/shard_map/ppermute | solution.py:193
  156.2 1.2 reshape.452
  157.5 3.6 fusion.20
  161.1 2.2 convolution_convert_fusion.1
  163.2 1.3 fusion.130
  165.8 1.4 reshape.424
  167.2 7.4 %collective-permute-done.10 = bf16[16,20,1024]{2,0,1:T(8,128)(2,1)} collective-permute-done((bf16[16,20,1024]{2,0,1:T(8,128)(2,1)S(1)}, bf16[16,20,1024]{2,0,1:T(8,128)(2,1)}, u32[]{:S(2)}, u32[]{:S(2)}) %collective-permute-start.10) | collective-permute-done | bytes 655392 | tf_op jit(solution)/shard_map/ppermute | solution.py:158
  174.6 2.4 add_convert_fusion.1
  177.0 15.1 %all-to-all-start.1 = ((bf16[16,20,1024]{2,1,0:T(8,128)(2,1)}), bf16[16,20,1024]{2,1,0:T(8,128)(2,1)S(1)}, u32[]{:S(2)}, u32[]{:S(2)}) async-start(bf16[16,20,1024]{2,1,0:T(8,128)(2,1)} %add_convert_fusion.1), calls=%async_computation.1 | async-start | bytes 1572864 | tf_op jit(solution)/shard_map/all_to_all | solution.py:160
  192.2 3.7 collective-permute-start.6
  197.1 16.1 %all-to-all-done.1 = bf16[16,20,1024]{2,1,0:T(8,128)(2,1)S(1)} async-done(((bf16[16,20,1024]{2,1,0:T(8,128)(2,1)}), bf16[16,20,1024]{2,1,0:T(8,128)(2,1)S(1)}, u32[]{:S(2)}, u32[]{:S(2)}) %all-to-all-start.1) | async-done | bytes 655392 | tf_op jit(solution)/shard_map/all_to_all | solution.py:160
  214.8 5.7 %collective-permute-start.11 = (bf16[128,1024]{1,0:T(8,128)(2,1)S(1)}, bf16[128,1024]{1,0:T(8,128)(2,1)S(1)}, u32[]{:S(2)}, u32[]{:S(2)}) collective-permute-start(bf16[128,1024]{1,0:T(8,128)(2,1)S(1)} %multiply_reduce_fusion.1), channel_id=1, source_target_pairs={{0,1},{1,0},{2,3},{3,2},{4,5},{5,4},{6,7},{7,6},{8,9},{9,8},{10,11... | collective-permute-start | bytes 786440 | tf_op jit(solution)/shard_map/ppermute | solution.py:40
  221.5 6.4 %collective-permute-done.11 = bf16[128,1024]{1,0:T(8,128)(2,1)S(1)} collective-permute-done((bf16[128,1024]{1,0:T(8,128)(2,1)S(1)}, bf16[128,1024]{1,0:T(8,128)(2,1)S(1)}, u32[]{:S(2)}, u32[]{:S(2)}) %collective-permute-start.11) | collective-permute-done | bytes 262176 | tf_op jit(solution)/shard_map/ppermute | solution.py:40
  227.9 1.6 collective-permute-done.13
  231.4 82.5 %all-gather.5.cloned.1.call-done = bf16[4096,2,256]{0,2,1:T(8,128)(2,1)} async-done(((bf16[128,2,256]{0,2,1:T(8,128)(2,1)}), bf16[4096,2,256]{0,2,1:T(8,128)(2,1)}) %all-gather.5.cloned.1.call-update) | async-done | bytes 4194320 | tf_op jit(solution)/shard_map/all_gather | solution.py:112
  313.8 3.2 constant_dynamic-slice_fusion
  317.1 1.1 fusion.134
  319.3 3.7 fusion.37
  323.3 2.5 collective-permute-start.17
  326.6 9.7 %collective-permute-done.17 = bf16[128,1024]{1,0:T(8,128)(2,1)S(1)} collective-permute-done((bf16[128,1024]{1,0:T(8,128)(2,1)S(1)}, bf16[128,1024]{1,0:T(8,128)(2,1)S(1)}, u32[]{:S(2)}, u32[]{:S(2)}) %collective-permute-start.17) | collective-permute-done | bytes 262176 | tf_op jit(solution)/shard_map/ppermute | solution.py:40
  337.2 22.0 %all_to_all.20 = bf16[16,20,1024]{2,1,0:T(8,128)(2,1)S(1)} all-to-all(bf16[16,20,1024]{2,1,0:T(8,128)(2,1)S(1)} %reshape.417), channel_id=1, replica_groups=mesh['section'=2,'tz'=16,'tp'=2,'rep'=4] {'tz'}, dimensions={0} | all-to-all | bytes 1310720 | tf_op jit(solution)/shard_map/all_to_all | solution.py:149
  359.5 2.4 collective-permute-start.18
  361.9 8.2 %collective-permute-done.18 = bf16[16,20,1024]{2,0,1:T(8,128)(2,1)S(1)} collective-permute-done((bf16[16,20,1024]{2,0,1:T(8,128)(2,1)S(1)}, bf16[16,20,1024]{2,0,1:T(8,128)(2,1)S(1)}, u32[]{:S(2)}, u32[]{:S(2)}) %collective-permute-start.18) | collective-permute-done | bytes 655392 | tf_op jit(solution)/shard_map/ppermute | solution.py:152
  371.0 2.8 fusion.18
  375.1 1.3 copy.72
  376.4 1.9 collective-permute-start.19
  378.5 8.1 %collective-permute-done.19 = bf16[16,20,1024]{2,0,1:T(8,128)(2,1)} collective-permute-done((bf16[16,20,1024]{2,0,1:T(8,128)(2,1)}, bf16[16,20,1024]{2,0,1:T(8,128)(2,1)}, u32[]{:S(2)}, u32[]{:S(2)}) %collective-permute-start.19) | collective-permute-done | bytes 655392 | tf_op jit(solution)/shard_map/ppermute | solution.py:158
  386.6 2.5 add_convert_fusion
  389.1 6.8 %all-to-all-start.3 = ((bf16[16,20,1024]{2,1,0:T(8,128)(2,1)}), bf16[16,20,1024]{2,1,0:T(8,128)(2,1)S(1)}, u32[]{:S(2)}, u32[]{:S(2)}) async-start(bf16[16,20,1024]{2,1,0:T(8,128)(2,1)} %add_convert_fusion), calls=%async_computation.3 | async-start | bytes 1572864 | tf_op jit(solution)/shard_map/all_to_all | solution.py:160
  399.0 13.1 %all-to-all-done.3 = bf16[16,20,1024]{2,1,0:T(8,128)(2,1)S(1)} async-done(((bf16[16,20,1024]{2,1,0:T(8,128)(2,1)}), bf16[16,20,1024]{2,1,0:T(8,128)(2,1)S(1)}, u32[]{:S(2)}, u32[]{:S(2)}) %all-to-all-start.3) | async-done | bytes 655392 | tf_op jit(solution)/shard_map/all_to_all | solution.py:160
  413.5 1.5 collective-permute-start.21
  415.1 9.3 %collective-permute-start.20 = (bf16[128,1024]{1,0:T(8,128)(2,1)S(1)}, bf16[128,1024]{1,0:T(8,128)(2,1)S(1)}, u32[]{:S(2)}, u32[]{:S(2)}) collective-permute-start(bf16[128,1024]{1,0:T(8,128)(2,1)S(1)} %multiply_reduce_fusion), channel_id=1, source_target_pairs={{0,1},{1,0},{2,3},{3,2},{4,5},{5,4},{6,7},{7,6},{8,9},{9,8},{10,11... | collective-permute-start | bytes 786440 | tf_op jit(solution)/shard_map/ppermute | solution.py:40
  424.5 10.9 %collective-permute-start.14 = (bf16[196608]{0:T(1024)(128)(2,1)S(1)}, bf16[196608]{0:T(1024)(128)(2,1)S(1)}, u32[]{:S(2)}, u32[]{:S(2)}) collective-permute-start(bf16[196608]{0:T(1024)(128)(2,1)S(1)} %pad_maximum_fusion.2), channel_id=1, source_target_pairs={{128,0},{129,1},{130,2},{131,3},{132,4},{133,5},{134,6},{135,7},{1... | collective-permute-start | bytes 1179656 | tf_op jit(solution)/shard_map/ppermute | solution.py:210
  437.0 1.3 collective-permute-start.23
  440.9 2.9 collective-permute-done.23
  (177 shorter events, 33.4 us)
Async XLA Ops:
  7.2 5.1 %copy-start.14 = (f32[1,2,1024]{2,1,0:T(2,128)S(1)}, f32[1,2,1024]{2,1,0:T(2,128)}, u32[]{:S(2)}) copy-start(f32[1,2,1024]{2,1,0:T(2,128)} %param.16) | copy-start | bytes 24580
  7.2 5.2 %copy-start.8 = (bf16[2,128,1024]{2,1,0:T(8,128)(2,1)S(1)}, bf16[2,128,1024]{2,1,0:T(8,128)(2,1)}, u32[]{:S(2)}) copy-start(bf16[2,128,1024]{2,1,0:T(8,128)(2,1)} %param.12) | copy-start | bytes 1572868
  7.2 92.2 %all-gather.3.cloned.1.call-start = ((), (), s32[]{:S(2)}) async-start(), calls=%async_computation.4 | async-start | bytes 4325376 | tf_op jit(solution)/shard_map/all_gather | solution.py:112
  9.0 8.7 %copy-start.6 = (bf16[1,1024,3,256]{1,3,2,0:T(8,128)(2,1)}, bf16[1,1024,3,256]{1,3,2,0:T(8,128)(2,1)S(1)}, u32[]{:S(2)}) copy-start(bf16[1,1024,3,256]{1,3,2,0:T(8,128)(2,1)S(1)} %copy.61) | copy-start | bytes 4718596
  9.0 6.5 %collective-permute-start.1 = (bf16[1024,768]{0,1:T(8,128)(2,1)S(1)}, bf16[1024,768]{0,1:T(8,128)(2,1)}, u32[]{:S(2)}, u32[]{:S(2)}) collective-permute-start(bf16[1024,768]{0,1:T(8,128)(2,1)S(1)} %bitcast.193), channel_id=1, source_target_pairs={{0,128},{128,0},{1,129},{129,1},{2,130},{130,2},{3,131},{131,3},{4... | collective-permute-start | bytes 4718600 | tf_op jit(solution)/shard_map/ppermute | solution.py:193
  12.3 3.2 collective-permute-start
  15.5 3.2 copy-start.13
  15.5 4.6 %copy-start.17 = (s32[2,128,2]{1,2,0:T(2,128)S(1)}, s32[2,128,2]{1,2,0:T(2,128)}, u32[]{:S(2)}) copy-start(s32[2,128,2]{1,2,0:T(2,128)} %param.14) | copy-start | bytes 6148
  18.6 89.9 %collective-permute-start.2 = (bf16[256,1024]{1,0:T(8,128)(2,1)S(1)}, bf16[256,1024]{1,0:T(8,128)(2,1)S(1)}, u32[]{:S(2)}, u32[]{:S(2)}) collective-permute-start(bf16[256,1024]{1,0:T(8,128)(2,1)S(1)} %bitcast.192), channel_id=1, source_target_pairs={{0,128},{128,0},{1,129},{129,1},{2,130},{130,2},{3,131},{131,3},{4... | collective-permute-start | bytes 1572872 | tf_op jit(solution)/shard_map/ppermute | solution.py:193
  108.5 13.6 %copy-start.4 = (bf16[256,1024]{1,0:T(8,128)(2,1)}, bf16[256,1024]{1,0:T(8,128)(2,1)S(1)}, u32[]{:S(2)}) copy-start(bf16[256,1024]{1,0:T(8,128)(2,1)S(1)} %collective-permute-done.2) | copy-start | bytes 1572868
  108.8 13.0 %collective-permute-start.5 = (bf16[128,1024]{1,0:T(8,128)(2,1)S(1)}, bf16[128,1024]{1,0:T(8,128)(2,1)S(1)}, u32[]{:S(2)}, u32[]{:S(2)}) collective-permute-start(bf16[128,1024]{1,0:T(8,128)(2,1)S(1)} %convolution_convert_fusion.5), channel_id=1, source_target_pairs={{0,3},{1,2},{2,1},{3,0},{4,7},{5,6},{6,5},{7,4},{8,11},{9,10},{10,... | collective-permute-start | bytes 786440 | tf_op jit(solution)/shard_map/ppermute | solution.py:40
  111.3 10.5 %collective-permute-start.4 = (bf16[128,1024]{1,0:T(8,128)(2,1)S(1)}, bf16[128,1024]{1,0:T(8,128)(2,1)S(1)}, u32[]{:S(2)}, u32[]{:S(2)}) collective-permute-start(bf16[128,1024]{1,0:T(8,128)(2,1)S(1)} %convolution_convert_fusion.5), channel_id=1, source_target_pairs={{0,2},{1,3},{2,0},{3,1},{4,6},{5,7},{6,4},{7,5},{8,10},{9,11},{10,... | collective-permute-start | bytes 786440 | tf_op jit(solution)/shard_map/ppermute | solution.py:40
  111.9 10.0 %collective-permute-start.3 = (bf16[128,1024]{1,0:T(8,128)(2,1)S(1)}, bf16[128,1024]{1,0:T(8,128)(2,1)S(1)}, u32[]{:S(2)}, u32[]{:S(2)}) collective-permute-start(bf16[128,1024]{1,0:T(8,128)(2,1)S(1)} %convolution_convert_fusion.5), channel_id=1, source_target_pairs={{0,1},{1,0},{2,3},{3,2},{4,5},{5,4},{6,7},{7,6},{8,9},{9,8},{10,11... | collective-permute-start | bytes 786440 | tf_op jit(solution)/shard_map/ppermute | solution.py:40
  123.6 21.5 %all-to-all-start = ((bf16[16,20,1024]{2,1,0:T(8,128)(2,1)}), bf16[16,20,1024]{2,1,0:T(8,128)(2,1)S(1)}, u32[]{:S(2)}, u32[]{:S(2)}) async-start(bf16[16,20,1024]{2,1,0:T(8,128)(2,1)} %reshape.410), calls=%async_computation | async-start | bytes 1572864 | tf_op jit(solution)/shard_map/all_to_all | solution.py:149
  127.8 29.6 %collective-permute-start.8 = (bf16[1,1024,2,352]{1,3,2,0:T(8,128)(2,1)}, bf16[1,1024,2,352]{1,3,2,0:T(8,128)(2,1)}, u32[]{:S(2)}, u32[]{:S(2)}) collective-permute-start(bf16[1,1024,2,352]{1,3,2,0:T(8,128)(2,1)} %bitcast.28), channel_id=1, source_target_pairs={{0,128},{128,0},{1,129},{129,1},{2,130},{130,2},{3,131},{131,3},{4... | collective-permute-start | bytes 4325384 | tf_op jit(solution)/shard_map/ppermute | solution.py:193
  145.4 10.3 %collective-permute-start.7 = (bf16[16,20,1024]{2,0,1:T(8,128)(2,1)S(1)}, bf16[16,20,1024]{2,0,1:T(8,128)(2,1)S(1)}, u32[]{:S(2)}, u32[]{:S(2)}) collective-permute-start(bf16[16,20,1024]{2,0,1:T(8,128)(2,1)S(1)} %copy.64), channel_id=1, source_target_pairs={{0,4},{4,0},{1,5},{5,1},{2,6},{6,2},{3,7},{7,3},{8,12},{12,8},{9,1... | collective-permute-start | bytes 1966088 | tf_op jit(solution)/shard_map/ppermute | solution.py:152
  146.3 14.7 %collective-permute-start.9 = (bf16[1,352,1024]{2,1,0:T(8,128)(2,1)}, bf16[1,352,1024]{2,1,0:T(8,128)(2,1)}, u32[]{:S(2)}, u32[]{:S(2)}) collective-permute-start(bf16[1,352,1024]{2,1,0:T(8,128)(2,1)} %bitcast.221), channel_id=1, source_target_pairs={{0,128},{128,0},{1,129},{129,1},{2,130},{130,2},{3,131},{131,3},{4... | collective-permute-start | bytes 2162696 | tf_op jit(solution)/shard_map/ppermute | solution.py:193
  157.4 3.6 copy-start.19
  165.0 9.6 %collective-permute-start.10 = (bf16[16,20,1024]{2,0,1:T(8,128)(2,1)S(1)}, bf16[16,20,1024]{2,0,1:T(8,128)(2,1)}, u32[]{:S(2)}, u32[]{:S(2)}) collective-permute-start(bf16[16,20,1024]{2,0,1:T(8,128)(2,1)S(1)} %copy.66), channel_id=1, source_target_pairs={{0,4},{4,0},{1,5},{5,1},{2,6},{6,2},{3,7},{7,3},{8,12},{12,8},{9,1... | collective-permute-start | bytes 1966088 | tf_op jit(solution)/shard_map/ppermute | solution.py:158
  167.2 25.0 %copy-start.9 = (bf16[1,1024,16]{1,2,0:T(8,128)(2,1)S(1)}, bf16[1,1024,16]{1,2,0:T(8,128)(2,1)}, u32[]{:S(2)}) copy-start(bf16[1,1024,16]{1,2,0:T(8,128)(2,1)} %param.19) | copy-start | bytes 98308
  177.0 36.2 %all-to-all-start.1 = ((bf16[16,20,1024]{2,1,0:T(8,128)(2,1)}), bf16[16,20,1024]{2,1,0:T(8,128)(2,1)S(1)}, u32[]{:S(2)}, u32[]{:S(2)}) async-start(bf16[16,20,1024]{2,1,0:T(8,128)(2,1)} %add_convert_fusion.1), calls=%async_computation.1 | async-start | bytes 1572864 | tf_op jit(solution)/shard_map/all_to_all | solution.py:160
  192.2 121.7 %all-gather.5.cloned.1.call-start = ((), (), s32[]{:S(2)}) async-start(), calls=%async_computation.5 | async-start | bytes 4325376 | tf_op jit(solution)/shard_map/all_gather | solution.py:112
  192.2 4.5 collective-permute-start.6
  196.8 16.5 %copy-start.11 = (bf16[1024,16]{0,1:T(8,128)(2,1)}, bf16[1024,16]{0,1:T(8,128)(2,1)S(1)}, u32[]{:S(2)}) copy-start(bf16[1024,16]{0,1:T(8,128)(2,1)S(1)} %collective-permute-done.6) | copy-start | bytes 98308
  214.6 15.2 %copy-start.7 = (bf16[1,1024,3,256]{1,3,2,0:T(8,128)(2,1)S(1)}, bf16[1,1024,3,256]{1,3,2,0:T(8,128)(2,1)}, u32[]{:S(2)}) copy-start(bf16[1,1024,3,256]{1,3,2,0:T(8,128)(2,1)} %copy-done.6) | copy-start | bytes 4718596
  214.7 6.8 %collective-permute-start.12 = (bf16[128,1024]{1,0:T(8,128)(2,1)S(1)}, bf16[128,1024]{1,0:T(8,128)(2,1)S(1)}, u32[]{:S(2)}, u32[]{:S(2)}) collective-permute-start(bf16[128,1024]{1,0:T(8,128)(2,1)S(1)} %multiply_reduce_fusion.1), channel_id=1, source_target_pairs={{0,2},{1,3},{2,0},{3,1},{4,6},{5,7},{6,4},{7,5},{8,10},{9,11},{10,... | collective-permute-start | bytes 786440 | tf_op jit(solution)/shard_map/ppermute | solution.py:40
  214.8 13.1 %collective-permute-start.11 = (bf16[128,1024]{1,0:T(8,128)(2,1)S(1)}, bf16[128,1024]{1,0:T(8,128)(2,1)S(1)}, u32[]{:S(2)}, u32[]{:S(2)}) collective-permute-start(bf16[128,1024]{1,0:T(8,128)(2,1)S(1)} %multiply_reduce_fusion.1), channel_id=1, source_target_pairs={{0,1},{1,0},{2,3},{3,2},{4,5},{5,4},{6,7},{7,6},{8,9},{9,8},{10,11... | collective-permute-start | bytes 786440 | tf_op jit(solution)/shard_map/ppermute | solution.py:40
  220.5 8.9 %collective-permute-start.13 = (bf16[128,1024]{1,0:T(8,128)(2,1)S(1)}, bf16[128,1024]{1,0:T(8,128)(2,1)S(1)}, u32[]{:S(2)}, u32[]{:S(2)}) collective-permute-start(bf16[128,1024]{1,0:T(8,128)(2,1)S(1)} %multiply_reduce_fusion.1), channel_id=1, source_target_pairs={{0,3},{1,2},{2,1},{3,0},{4,7},{5,6},{6,5},{7,4},{8,11},{9,10},{10,... | collective-permute-start | bytes 786440 | tf_op jit(solution)/shard_map/ppermute | solution.py:40
  229.8 106.5 %copy-start = (bf16[128,1024]{1,0:T(8,128)(2,1)}, bf16[128,1024]{1,0:T(8,128)(2,1)S(1)}, u32[]{:S(2)}) copy-start(bf16[128,1024]{1,0:T(8,128)(2,1)S(1)} %get-tuple-element.14) | copy-start | bytes 786436
  319.3 3.7 copy-start.3
  319.3 3.7 copy-start.5
  323.3 13.0 %collective-permute-start.17 = (bf16[128,1024]{1,0:T(8,128)(2,1)S(1)}, bf16[128,1024]{1,0:T(8,128)(2,1)S(1)}, u32[]{:S(2)}, u32[]{:S(2)}) collective-permute-start(bf16[128,1024]{1,0:T(8,128)(2,1)S(1)} %convolution_convert_fusion.4), channel_id=1, source_target_pairs={{0,3},{1,2},{2,1},{3,0},{4,7},{5,6},{6,5},{7,4},{8,11},{9,10},{10,... | collective-permute-start | bytes 786440 | tf_op jit(solution)/shard_map/ppermute | solution.py:40
  325.8 10.5 %collective-permute-start.16 = (bf16[128,1024]{1,0:T(8,128)(2,1)S(1)}, bf16[128,1024]{1,0:T(8,128)(2,1)S(1)}, u32[]{:S(2)}, u32[]{:S(2)}) collective-permute-start(bf16[128,1024]{1,0:T(8,128)(2,1)S(1)} %convolution_convert_fusion.4), channel_id=1, source_target_pairs={{0,2},{1,3},{2,0},{3,1},{4,6},{5,7},{6,4},{7,5},{8,10},{9,11},{10,... | collective-permute-start | bytes 786440 | tf_op jit(solution)/shard_map/ppermute | solution.py:40
  326.3 10.0 %collective-permute-start.15 = (bf16[128,1024]{1,0:T(8,128)(2,1)S(1)}, bf16[128,1024]{1,0:T(8,128)(2,1)S(1)}, u32[]{:S(2)}, u32[]{:S(2)}) collective-permute-start(bf16[128,1024]{1,0:T(8,128)(2,1)S(1)} %convolution_convert_fusion.4), channel_id=1, source_target_pairs={{0,1},{1,0},{2,3},{3,2},{4,5},{5,4},{6,7},{7,6},{8,9},{9,8},{10,11... | collective-permute-start | bytes 786440 | tf_op jit(solution)/shard_map/ppermute | solution.py:40
  336.6 22.6 %copy-start.15 = (f32[128]{0:T(128)}, f32[128]{0:T(128)S(1)}, u32[]{:S(2)}) copy-start(f32[128]{0:T(128)S(1)} %add_rsqrt_fusion) | copy-start | bytes 1540
  359.5 10.6 %collective-permute-start.18 = (bf16[16,20,1024]{2,0,1:T(8,128)(2,1)S(1)}, bf16[16,20,1024]{2,0,1:T(8,128)(2,1)S(1)}, u32[]{:S(2)}, u32[]{:S(2)}) collective-permute-start(bf16[16,20,1024]{2,0,1:T(8,128)(2,1)S(1)} %copy.70), channel_id=1, source_target_pairs={{0,4},{4,0},{1,5},{5,1},{2,6},{6,2},{3,7},{7,3},{8,12},{12,8},{9,1... | collective-permute-start | bytes 1966088 | tf_op jit(solution)/shard_map/ppermute | solution.py:152
  376.4 10.2 %collective-permute-start.19 = (bf16[16,20,1024]{2,0,1:T(8,128)(2,1)}, bf16[16,20,1024]{2,0,1:T(8,128)(2,1)}, u32[]{:S(2)}, u32[]{:S(2)}) collective-permute-start(bf16[16,20,1024]{2,0,1:T(8,128)(2,1)} %copy.72), channel_id=1, source_target_pairs={{0,4},{4,0},{1,5},{5,1},{2,6},{6,2},{3,7},{7,3},{8,12},{12,8},{9,1... | collective-permute-start | bytes 1966088 | tf_op jit(solution)/shard_map/ppermute | solution.py:158
  378.5 17.5 %copy-start.18 = (s32[2,32]{1,0:T(2,128)S(1)}, s32[2,32]{1,0:T(2,128)}, u32[]{:S(2)}) copy-start(s32[2,32]{1,0:T(2,128)} %param.15) | copy-start | bytes 772
  389.1 9.5 %copy-start.1 = (bf16[128,1024]{1,0:T(8,128)(2,1)S(1)}, bf16[128,1024]{1,0:T(8,128)(2,1)}, u32[]{:S(2)}) copy-start(bf16[128,1024]{1,0:T(8,128)(2,1)} %copy-done) | copy-start | bytes 786436
  389.1 9.5 %copy-start.10 = (bf16[1,1024,16]{1,2,0:T(8,128)(2,1)S(1)}, bf16[1,1024,16]{1,2,0:T(8,128)(2,1)}, u32[]{:S(2)}) copy-start(bf16[1,1024,16]{1,2,0:T(8,128)(2,1)} %param.19) | copy-start | bytes 98308
  389.1 9.5 %copy-start.12 = (bf16[1024,16]{0,1:T(8,128)(2,1)S(1)}, bf16[1024,16]{0,1:T(8,128)(2,1)}, u32[]{:S(2)}) copy-start(bf16[1024,16]{0,1:T(8,128)(2,1)} %copy-done.11) | copy-start | bytes 98308
  389.1 9.5 %copy-start.16 = (f32[128]{0:T(128)S(1)}, f32[128]{0:T(128)}, u32[]{:S(2)}) copy-start(f32[128]{0:T(128)} %copy-done.15) | copy-start | bytes 1540
  389.1 23.0 %all-to-all-start.3 = ((bf16[16,20,1024]{2,1,0:T(8,128)(2,1)}), bf16[16,20,1024]{2,1,0:T(8,128)(2,1)S(1)}, u32[]{:S(2)}, u32[]{:S(2)}) async-start(bf16[16,20,1024]{2,1,0:T(8,128)(2,1)} %add_convert_fusion), calls=%async_computation.3 | async-start | bytes 1572864 | tf_op jit(solution)/shard_map/all_to_all | solution.py:160
  413.5 23.1 %collective-permute-start.21 = (bf16[128,1024]{1,0:T(8,128)(2,1)S(1)}, bf16[128,1024]{1,0:T(8,128)(2,1)S(1)}, u32[]{:S(2)}, u32[]{:S(2)}) collective-permute-start(bf16[128,1024]{1,0:T(8,128)(2,1)S(1)} %multiply_reduce_fusion), channel_id=1, source_target_pairs={{0,2},{1,3},{2,0},{3,1},{4,6},{5,7},{6,4},{7,5},{8,10},{9,11},{10,... | collective-permute-start | bytes 786440 | tf_op jit(solution)/shard_map/ppermute | solution.py:40
  415.1 21.6 %collective-permute-start.20 = (bf16[128,1024]{1,0:T(8,128)(2,1)S(1)}, bf16[128,1024]{1,0:T(8,128)(2,1)S(1)}, u32[]{:S(2)}, u32[]{:S(2)}) collective-permute-start(bf16[128,1024]{1,0:T(8,128)(2,1)S(1)} %multiply_reduce_fusion), channel_id=1, source_target_pairs={{0,1},{1,0},{2,3},{3,2},{4,5},{5,4},{6,7},{7,6},{8,9},{9,8},{10,11... | collective-permute-start | bytes 786440 | tf_op jit(solution)/shard_map/ppermute | solution.py:40
  424.4 12.3 %collective-permute-start.22 = (bf16[128,1024]{1,0:T(8,128)(2,1)S(1)}, bf16[128,1024]{1,0:T(8,128)(2,1)S(1)}, u32[]{:S(2)}, u32[]{:S(2)}) collective-permute-start(bf16[128,1024]{1,0:T(8,128)(2,1)S(1)} %multiply_reduce_fusion), channel_id=1, source_target_pairs={{0,3},{1,2},{2,1},{3,0},{4,7},{5,6},{6,5},{7,4},{8,11},{9,10},{10,... | collective-permute-start | bytes 786440 | tf_op jit(solution)/shard_map/ppermute | solution.py:40
  424.5 14.9 %collective-permute-start.14 = (bf16[196608]{0:T(1024)(128)(2,1)S(1)}, bf16[196608]{0:T(1024)(128)(2,1)S(1)}, u32[]{:S(2)}, u32[]{:S(2)}) collective-permute-start(bf16[196608]{0:T(1024)(128)(2,1)S(1)} %pad_maximum_fusion.2), channel_id=1, source_target_pairs={{128,0},{129,1},{130,2},{131,3},{132,4},{133,5},{134,6},{135,7},{1... | collective-permute-start | bytes 1179656 | tf_op jit(solution)/shard_map/ppermute | solution.py:210
  437.0 6.8 %collective-permute-start.23 = (bf16[196608]{0:T(1024)(128)(2,1)S(1)}, bf16[196608]{0:T(1024)(128)(2,1)S(1)}, u32[]{:S(2)}, u32[]{:S(2)}) collective-permute-start(bf16[196608]{0:T(1024)(128)(2,1)S(1)} %pad_maximum_fusion.3), channel_id=1, source_target_pairs={{0,128},{1,129},{2,130},{3,131},{4,132},{5,133},{6,134},{7,135},{8... | collective-permute-start | bytes 1179656 | tf_op jit(solution)/shard_map/ppermute | solution.py:210
  (2 other events, 5.8 us)
Sparse Core Ops, SparseCore 0:
  18.7 80.6 all-gather.2
  231.5 82.3 all-gather.4
